TPU v7x, 32 devices: a whole 2x2x4 slice. The times are simulated.
32 devices in a mesh: seq: 8 (over y, x, core), tensor: 4 (over z).
Axes of the slice: x: 2, y: 2, z: 4, core: 2. Of those that a mesh axis runs over, the one named last changes fastest.
Arguments:
- queries: bfloat16 [4096, 8192], P('seq', 'tensor')
- image_refs: int32 [4096, 1], P('seq'), may hold values from 0 to 7; in each aligned block of 512 rows (0 to 511, 512 to 1023, ...) at most 128 rows name the same one
- features: bfloat16 [8, 1601, 8192], P('seq', None, 'tensor'), may hold values from -6 to 6
- kv_weight: bfloat16 [8192, 2048], P('tensor'), may hold values from -0.0625 to 0.0625
Outputs:
- attended: bfloat16 [4096, 8192], P('seq', 'tensor')
Inputs may be any that keep to these rules, and one draw needn't show every extreme that they name: image_refs holds an image number per text token; at most 128 tokens of one device reference the same image, and some device has an image referenced by exactly 128 of its tokens.
All inputs are finite; a program needn't handle non-finite values.
Results may differ from a plain program's by a relative error of at most 0.03.
Values may be sent and summed in bfloat16 or wider, within the bound.
No kernel may reach another device: no remote copies, remote signals or barrier semaphores. Data moves between devices by JAX's collectives and lax.ppermute only.
A program may use at most 128 MiB of HBM per device.

v0:
```python
import jax
import jax.numpy as jnp
from jax import lax
from jax.sharding import PartitionSpec as P

HEADS = 64
KV_HEADS = 8
HEAD_DIM = 128


def attend(query_rows, key_values, group, head_dim):
    row_count = query_rows.shape[0]
    query_heads = query_rows.shape[1] // head_dim
    kv_heads = key_values.shape[1] // (2 * head_dim)
    image_len = key_values.shape[0]
    per_head = query_rows.reshape(row_count, query_heads, head_dim).transpose(1, 0, 2)
    split_kv = key_values.reshape(image_len, kv_heads, 2, head_dim)
    key_heads = split_kv[:, :, 0, :].transpose(1, 0, 2)
    value_heads = split_kv[:, :, 1, :].transpose(1, 0, 2)
    score_scale = head_dim ** (-0.5)

    def one_head(inputs):
        head_query, head_index = inputs
        key_mat = key_heads[head_index // group]
        value_mat = value_heads[head_index // group]
        scores = (
            lax.dot_general(
                head_query, key_mat, (((1,), (1,)), ((), ())), preferred_element_type=jnp.float32
            )
            * score_scale
        )
        row_max = jnp.max(scores, axis=1, keepdims=True)
        weights_exp = jnp.exp(scores - row_max)
        totals = jnp.sum(weights_exp, axis=1, keepdims=True)
        probs = weights_exp.astype(jnp.bfloat16)
        weighted = jnp.dot(probs, value_mat, preferred_element_type=jnp.float32) / totals
        return weighted.astype(jnp.bfloat16)

    heads_out = lax.map(one_head, (per_head, jnp.arange(query_heads, dtype=jnp.int32)))
    return heads_out.transpose(1, 0, 2).reshape(row_count, query_heads * head_dim)


def on_device(queries, image_refs, features, kv_weight):
    seq_devices = lax.axis_size("seq")
    token_count = queries.shape[0]
    width_cols = queries.shape[1]
    capacity = 2 * token_count // seq_devices
    owners = image_refs[:, 0]
    onehot = (owners[:, None] == jnp.arange(seq_devices, dtype=jnp.int32)[None, :]).astype(
        jnp.int32
    )
    running = jnp.cumsum(onehot, axis=0)
    position = jnp.sum(onehot * (running - 1), axis=1)
    slot_index = owners * capacity + position
    outgoing = (
        jnp.zeros((seq_devices * capacity, width_cols), jnp.bfloat16).at[slot_index].set(queries)
    )
    outgoing = outgoing.reshape(seq_devices, capacity, width_cols)
    group = HEADS // KV_HEADS
    image_block = features[0]
    summed = lax.psum_scatter(
        lax.dot_general(
            kv_weight, image_block, (((0,), (1,)), ((), ())), preferred_element_type=jnp.float32
        ).astype(jnp.bfloat16),
        "tensor",
        scatter_dimension=0,
        tiled=True,
    ).astype(jnp.float32)
    key_values = summed.T.astype(jnp.bfloat16)
    received = lax.all_to_all(outgoing, "seq", split_axis=0, concat_axis=0, tiled=True)
    flat_rows = received.reshape(-1, width_cols)
    answered = attend(flat_rows, key_values, group, HEAD_DIM).reshape(received.shape)
    returned = lax.all_to_all(answered, "seq", split_axis=0, concat_axis=0, tiled=True)
    return returned.reshape(seq_devices * capacity, width_cols)[slot_index]


def solution(mesh):
    placed = (P("seq", "tensor"), P("seq", None), P("seq", None, "tensor"), P("tensor", None))
    return jax.shard_map(
        on_device, mesh=mesh, in_specs=placed, out_specs=P("seq", "tensor"), check_vma=False
    )
```

profile of v0, /device:TPU:0, one launch (start us, length us, event | category | flops | bytes accessed | tf_op | source)
XLA Modules:
  0.0 371.1 jit_solution(9986236662026952010)
XLA Ops:
  6.5 19.7 %convolution_convert_fusion = bf16[2048,1601]{0,1:T(8,128)(2,1)} fusion(bf16[2048,2048]{1,0:T(8,128)(2,1)} %param.9, bf16[1,1601,2048]{2,1,0:T(8,128)(2,1)} %param.8), kind=kOutput, calls=%fused_computation.23 | convolution fusion | flops 13433440256 | bytes 21504000 | tf_op jit(solution)/shard_map/dot_general | solution.py:62
  26.9 1.1 reduce-window.6
  28.4 7.7 %scatter_custom_fusion = bf16[1024,2048]{1,0:T(8,128)(2,1)} fusion(s32[512]{0:T(512)S(1)} %bitcast.64, bf16[512,2048]{1,0:T(8,128)(2,1)} %param.6, bf16[]{:T(256)} %constant.79.clone.1), kind=kCustom, calls=%fused_computation.25 | custom fusion | bytes 4194816 | tf_op jit(solution)/shard_map/scatter | solution.py:56
  36.1 5.0 %all-to-all-start = ((bf16[8,128,2048]{2,1,0:T(8,128)(2,1)}), bf16[8,128,2048]{2,1,0:T(8,128)(2,1)}, u32[]{:S(2)}, u32[]{:S(2)}) async-start(bf16[8,128,2048]{2,1,0:T(8,128)(2,1)} %bitcast.59), calls=%async_computation | async-start | bytes 8388608 | tf_op jit(solution)/shard_map/all_to_all | solution.py:70
  41.0 49.5 %all-to-all-done = bf16[8,128,2048]{2,1,0:T(8,128)(2,1)} async-done(((bf16[8,128,2048]{2,1,0:T(8,128)(2,1)}), bf16[8,128,2048]{2,1,0:T(8,128)(2,1)}, u32[]{:S(2)}, u32[]{:S(2)}) %all-to-all-start) | async-done | bytes 4194336 | tf_op jit(solution)/shard_map/all_to_all | solution.py:70
  90.6 3.6 copy.13
  94.2 3.1 copy.9
  97.3 47.4 %reduce-scatter.2.cloned.1.call-done = bf16[512,1601]{0,1:T(8,128)(2,1)} async-done(((bf16[2048,1601]{0,1:T(8,128)(2,1)}), bf16[512,1601]{0,1:T(8,128)(2,1)}) %reduce-scatter.2.cloned.1.call-update) | async-done | bytes 1639440 | tf_op jit(solution)/shard_map/reduce_scatter | solution.py:61
  144.7 3.7 %reshape.32 = bf16[1601,2,2,128]{3,2,1,0:T(2,128)(2,1)S(1)} reshape(bf16[1601,512]{1,0:T(8,128)(2,1)} %bitcast.61) | data formatting | bytes 3278848 | tf_op jit(solution)/shard_map/reshape | solution.py:17
  148.4 2.3 fusion.33
  151.1 137.5 %while.12 = (s32[]{:T(128)}, bf16[16,1024,128]{2,1,0:T(8,128)(2,1)}, bf16[16,1024,128]{2,1,0:T(8,128)(2,1)}, s32[16]{0:T(128)S(1)}, bf16[2,1601,128]{2,1,0:T(8,1...) while((s32[]{:T(128)}, ...), condition=%wide.region_8.9_spmd, body=%wide.region_5.8_spmd.sunk | while | flops 852760576 | bytes 21071168 | solution.py:39
  154.5 2.0 multiply_reduce_fusion.2
  156.6 1.1 fusion.41
  157.7 2.0 fusion.42
  163.1 2.0 multiply_reduce_fusion.2
  165.1 1.1 fusion.41
  166.3 2.0 fusion.42
  171.7 2.0 multiply_reduce_fusion.2
  173.8 1.1 fusion.41
  174.9 2.0 fusion.42
  180.3 2.0 multiply_reduce_fusion.2
  182.3 1.1 fusion.41
  183.5 2.0 fusion.42
  188.9 2.0 multiply_reduce_fusion.2
  190.9 1.1 fusion.41
  192.0 2.0 fusion.42
  197.5 2.0 multiply_reduce_fusion.2
  199.5 1.1 fusion.41
  200.6 2.0 fusion.42
  206.0 2.0 multiply_reduce_fusion.2
  208.1 1.1 fusion.41
  209.2 2.0 fusion.42
  214.6 2.0 multiply_reduce_fusion.2
  216.6 1.1 fusion.41
  217.8 2.0 fusion.42
  223.2 2.0 multiply_reduce_fusion.2
  225.2 1.1 fusion.41
  226.4 2.0 fusion.42
  231.8 2.0 multiply_reduce_fusion.2
  233.8 1.1 fusion.41
  235.0 2.0 fusion.42
  240.4 2.0 multiply_reduce_fusion.2
  242.4 1.1 fusion.41
  243.6 2.0 fusion.42
  249.0 2.0 multiply_reduce_fusion.2
  251.1 1.1 fusion.41
  252.2 2.0 fusion.42
  257.6 2.0 multiply_reduce_fusion.2
  259.7 1.1 fusion.41
  260.8 2.0 fusion.42
  266.2 2.0 multiply_reduce_fusion.2
  268.2 1.1 fusion.41
  269.4 2.0 fusion.42
  274.8 2.0 multiply_reduce_fusion.2
  276.8 1.1 fusion.41
  278.0 2.0 fusion.42
  283.4 2.0 multiply_reduce_fusion.2
  285.4 1.1 fusion.41
  286.6 2.0 fusion.42
  288.6 6.8 %copy.10 = bf16[1024,16,128]{2,1,0:T(8,128)(2,1)} copy(bf16[1024,16,128]{2,0,1:T(8,128)(2,1)} %bitcast.19) | data formatting | bytes 8388608 | tf_op jit(solution)/shard_map/transpose | solution.py:40
  295.4 7.3 %reshape_reshape.7 = bf16[8,128,2048]{2,1,0:T(8,128)(2,1)} reshape(bf16[1024,16,128]{2,1,0:T(8,128)(2,1)} %copy.10) | data formatting | bytes 8388608 | tf_op jit(solution)/shard_map/reshape;reshape | solution.py:72
  302.7 4.8 %all-to-all-start.1 = ((bf16[8,128,2048]{2,1,0:T(8,128)(2,1)}), bf16[8,128,2048]{2,1,0:T(8,128)(2,1)}, u32[]{:S(2)}, u32[]{:S(2)}) async-start(bf16[8,128,2048]{2,1,0:T(8,128)(2,1)} %reshape_reshape.7), calls=%async_computation.2 | async-start | bytes 8388608 | tf_op jit(solution)/shard_map/all_to_all | solution.py:73
  307.5 48.9 %all-to-all-done.1 = bf16[8,128,2048]{2,1,0:T(8,128)(2,1)} async-done(((bf16[8,128,2048]{2,1,0:T(8,128)(2,1)}), bf16[8,128,2048]{2,1,0:T(8,128)(2,1)}, u32[]{:S(2)}, u32[]{:S(2)}) %all-to-all-start.1) | async-done | bytes 4194336 | tf_op jit(solution)/shard_map/all_to_all | solution.py:73
  356.3 8.0 %gather_fusion = bf16[512,2048]{1,0:T(8,128)(2,1)} fusion(bf16[1024,2048]{1,0:T(8,128)(2,1)} %bitcast.20, s32[1024]{0:T(1024)S(1)} %pad_clamp_fusion), kind=kCustom, calls=%fused_computation | custom fusion | bytes 4196352 | tf_op jit(solution)/shard_map/gather | solution.py:74
  (30 shorter events, 11.9 us)
Async XLA Ops:
  6.5 138.1 %reduce-scatter.2.cloned.1.call-start = ((), (), s32[]{:S(2)}) async-start(), calls=%async_computation.3 | async-start | bytes 8232960 | tf_op jit(solution)/shard_map/reduce_scatter | solution.py:61
  26.2 0.7 copy-start
  36.1 54.5 %all-to-all-start = ((bf16[8,128,2048]{2,1,0:T(8,128)(2,1)}), bf16[8,128,2048]{2,1,0:T(8,128)(2,1)}, u32[]{:S(2)}, u32[]{:S(2)}) async-start(bf16[8,128,2048]{2,1,0:T(8,128)(2,1)} %bitcast.59), calls=%async_computation | async-start | bytes 8388608 | tf_op jit(solution)/shard_map/all_to_all | solution.py:70
  302.7 53.6 %all-to-all-start.1 = ((bf16[8,128,2048]{2,1,0:T(8,128)(2,1)}), bf16[8,128,2048]{2,1,0:T(8,128)(2,1)}, u32[]{:S(2)}, u32[]{:S(2)}) async-start(bf16[8,128,2048]{2,1,0:T(8,128)(2,1)} %reshape_reshape.7), calls=%async_computation.2 | async-start | bytes 8388608 | tf_op jit(solution)/shard_map/all_to_all | solution.py:73
Sparse Core Ops, SparseCore 0:
  26.3 118.2 reduce-scatter.1
where the time goes:
time: 373 us; the launch traced here: 371 us
  waiting for transfers between devices  146 us (39%)
  matrix products  83.7 us (22%)
  local copies, waits for them, and re-layouts  54.3 us (15%)
  loops' own time  44.7 us (12%)
  other arithmetic  19.4 us (5%)
  between operations  13.5 us (4%)
  starting transfers between devices  9.72 us (3%)
    all_to_all x1, waiting for transfers between devices, on_device(): lax.all_to_all(outgoing, 'seq', split_axis=0, concat_axis=0, tiled=True)  49.5 us
    all_to_all x1, waiting for transfers between devices, on_device(): lax.all_to_all(answered, 'seq', split_axis=0, concat_axis=0, tiled=True)  48.9 us
    reduce_scatter x1, waiting for transfers between devices, on_device(): lax.psum_scatter(lax.dot_general(kv_weight, image_block, (((0,), (1,)), (...  47.4 us
    another operation x1, loops' own time, attend(): lax.map(one_head, (per_head, jnp.arange(query_heads, dtype=jnp.int32)))  44.7 us
    dot_general x16, matrix products, one_head(): lax.dot_general(head_query, key_mat, (((1,), (1,)), ((), ())), preferred_...  32.3 us
    dot_general x16, matrix products, one_head(): jnp.dot(probs, value_mat, preferred_element_type=jnp.float32) / totals  31.8 us
    dot_general x1, matrix products, on_device(): lax.dot_general(kv_weight, image_block, (((0,), (1,)), ((), ())), preferr...  19.7 us
    reduce_sum x16, other arithmetic, one_head(): totals = jnp.sum(weights_exp, axis=1, keepdims=True)  18.1 us
  transfers between devices with their start and end apart: 3, of which 3 were waited for; matrix products, arithmetic and copies ran while one was open for 4% of the time, Pallas kernels for 0%

commit v1 on v0

v1 whole, which is shorter than its diff:
```python
import functools

import jax
import jax.numpy as jnp
from jax import lax
from jax.experimental import pallas as pl
from jax.experimental.pallas import tpu as pltpu
from jax.sharding import PartitionSpec as P

HEADS = 64
KV_HEADS = 8
HEAD_DIM = 128
ROW_TILE = 256


def attend_kernel(scale, q_ref, k_ref, v_ref, o_ref):
    q = q_ref[...]
    scores = (
        lax.dot_general(
            q, k_ref[...], (((1,), (0,)), ((), ())), preferred_element_type=jnp.float32
        )
        * scale
    )
    row_max = jnp.max(scores, axis=1, keepdims=True)
    weights_exp = jnp.exp(scores - row_max)
    totals = jnp.sum(weights_exp, axis=1, keepdims=True)
    probs = weights_exp.astype(jnp.bfloat16)
    weighted = lax.dot_general(
        probs, v_ref[...], (((1,), (1,)), ((), ())), preferred_element_type=jnp.float32
    )
    o_ref[...] = (weighted / totals).astype(o_ref.dtype)


def attend(query_rows, kv_t, group, head_dim):
    rows, width = query_rows.shape
    query_heads = width // head_dim
    image_len = kv_t.shape[1]
    tile = min(ROW_TILE, rows)
    assert rows % tile == 0
    scale = head_dim ** (-0.5)
    flops = 4 * rows * query_heads * image_len * head_dim
    return pl.pallas_call(
        functools.partial(attend_kernel, scale),
        out_shape=jax.ShapeDtypeStruct((rows, width), jnp.bfloat16),
        grid=(query_heads, rows // tile),
        in_specs=[
            pl.BlockSpec((tile, head_dim), lambda h, i: (i, h)),
            pl.BlockSpec((head_dim, image_len), lambda h, i: (2 * (h // group), 0)),
            pl.BlockSpec((head_dim, image_len), lambda h, i: (2 * (h // group) + 1, 0)),
        ],
        out_specs=pl.BlockSpec((tile, head_dim), lambda h, i: (i, h)),
        compiler_params=pltpu.CompilerParams(
            dimension_semantics=("arbitrary", "arbitrary"),
            vmem_limit_bytes=48 * 1024 * 1024,
        ),
        cost_estimate=pl.CostEstimate(
            flops=flops,
            transcendentals=rows * query_heads * image_len,
            bytes_accessed=2 * (2 * rows * width + kv_t.size),
        ),
    )(query_rows, kv_t, kv_t)


def on_device(queries, image_refs, features, kv_weight):
    seq_devices = lax.axis_size("seq")
    token_count = queries.shape[0]
    width_cols = queries.shape[1]
    capacity = 2 * token_count // seq_devices
    owners = image_refs[:, 0]
    onehot = (owners[:, None] == jnp.arange(seq_devices, dtype=jnp.int32)[None, :]).astype(
        jnp.int32
    )
    running = jnp.cumsum(onehot, axis=0)
    position = jnp.sum(onehot * (running - 1), axis=1)
    slot_index = owners * capacity + position
    outgoing = (
        jnp.zeros((seq_devices * capacity, width_cols), jnp.bfloat16).at[slot_index].set(queries)
    )
    outgoing = outgoing.reshape(seq_devices, capacity, width_cols)
    group = HEADS // KV_HEADS
    image_block = features[0]
    kv_t = lax.psum_scatter(
        lax.dot_general(
            kv_weight, image_block, (((0,), (1,)), ((), ())), preferred_element_type=jnp.float32
        ).astype(jnp.bfloat16),
        "tensor",
        scatter_dimension=0,
        tiled=True,
    )
    received = lax.all_to_all(outgoing, "seq", split_axis=0, concat_axis=0, tiled=True)
    flat_rows = received.reshape(-1, width_cols)
    answered = attend(flat_rows, kv_t, group, HEAD_DIM).reshape(received.shape)
    returned = lax.all_to_all(answered, "seq", split_axis=0, concat_axis=0, tiled=True)
    return returned.reshape(seq_devices * capacity, width_cols)[slot_index]


def solution(mesh):
    placed = (P("seq", "tensor"), P("seq", None), P("seq", None, "tensor"), P("tensor", None))
    return jax.shard_map(
        on_device, mesh=mesh, in_specs=placed, out_specs=P("seq", "tensor"), check_vma=False
    )
```

time: 373 us -> 321 us (0.86)
  Pallas kernels: 0 us -> 90.7 us
  matrix products: 83.7 us -> 19.7 us
  blocking collectives: 0 us -> 54.2 us
  loops' own time: 44.7 us -> 0 us
  waiting for transfers between devices: 146 us -> 107 us
  local copies, waits for them, and re-layouts: 54.3 us -> 29.5 us
  other arithmetic: 19.4 us -> 1.27 us
  starting transfers between devices: 9.72 us -> 4.55 us
    pallas_call x0 -> x1, Pallas kernels: none -> 90.7 us  [attend(): pl.pallas_call(functools.partial(attend_kernel, scale), out_shape=jax.Sha...]
    dot_general x32 -> x0, matrix products: 64.1 us -> none  [the longest x16 32.3 us: one_head(): lax.dot_general(head_query, key_mat, (((1,), (1,)), ((), ())), preferred_...]
    all_to_all x0 -> x1, blocking collectives: none -> 54.2 us  [on_device(): lax.all_to_all(outgoing, 'seq', split_axis=0, concat_axis=0, tiled=True)]
    all_to_all x1 -> x0, waiting for transfers between devices: 49.5 us -> none  [on_device(): lax.all_to_all(outgoing, 'seq', split_axis=0, concat_axis=0, tiled=True)]
    another operation x1 -> x0, loops' own time: 44.7 us -> none  [attend(): lax.map(one_head, (per_head, jnp.arange(query_heads, dtype=jnp.int32)))]
    reduce_sum x16 -> x0, other arithmetic: 18.1 us -> none  [one_head(): totals = jnp.sum(weights_exp, axis=1, keepdims=True)]
    reduce_scatter x1, waiting for transfers between devices: 47.4 us -> 58 us  [on_device(): lax.psum_scatter(lax.dot_general(kv_weight, image_block, (((0,), (1,)), (...]
    dynamic_slice x16 -> x0, local copies, waits for them, and re-layouts: 10.6 us -> none  [attend(): lax.map(one_head, (per_head, jnp.arange(query_heads, dtype=jnp.int32)))]
  transfers between devices with their start and end apart: 3 -> 2, of which waited for: 3 -> 2; matrix products, arithmetic and copies ran while one was open for 4% -> 3% of each run, Pallas kernels for 0% -> 0%
where the time goes in v1:
time: 321 us
  waiting for transfers between devices  107 us (33%)
  Pallas kernels  90.7 us (28%)
  blocking collectives  54.2 us (17%)
  local copies, waits for them, and re-layouts  29.5 us (9%)
  matrix products  19.7 us (6%)
  between operations  13.4 us (4%)
  starting transfers between devices  4.55 us (1%)
    pallas_call x1, Pallas kernels, attend(): pl.pallas_call(functools.partial(attend_kernel, scale), out_shape=jax.Sha...  90.7 us
    reduce_scatter x1, waiting for transfers between devices, on_device(): lax.psum_scatter(lax.dot_general(kv_weight, image_block, (((0,), (1,)), (...  58 us
    all_to_all x1, blocking collectives, on_device(): lax.all_to_all(outgoing, 'seq', split_axis=0, concat_axis=0, tiled=True)  54.2 us
    all_to_all x1, waiting for transfers between devices, on_device(): lax.all_to_all(answered, 'seq', split_axis=0, concat_axis=0, tiled=True)  49.1 us
    dot_general x1, matrix products, on_device(): lax.dot_general(kv_weight, image_block, (((0,), (1,)), ((), ())), preferr...  19.7 us
    convert_element_type x1, local copies, waits for them, and re-layouts, on_device(): kv_t = lax.psum_scatter(lax.dot_general(kv_weight, image_block, (((0,), (...  9.58 us
    gather x1, local copies, waits for them, and re-layouts, on_device(): return returned.reshape(seq_devices * capacity, width_cols)[slot_index]  7.95 us
    scatter x1, local copies, waits for them, and re-layouts, on_device(): jnp.zeros((seq_devices * capacity, width_cols), jnp.bfloat16).at[slot_index]  7.72 us
  transfers between devices with their start and end apart: 2, of which 2 were waited for; matrix products, arithmetic and copies ran while one was open for 3% of the time, Pallas kernels for 0%

profile of v1, /device:TPU:0, one launch (start us, length us, event | category | flops | bytes accessed | tf_op | source)
XLA Modules:
  0.0 320.6 jit_solution(13816294903739969715)
XLA Ops:
  6.5 0.0 reduce-scatter.2.cloned.1.call-start
  6.5 19.7 %convolution_convert_fusion = bf16[2048,1601]{0,1:T(8,128)(2,1)} fusion(bf16[2048,2048]{1,0:T(8,128)(2,1)} %param.7, bf16[1,1601,2048]{2,1,0:T(8,128)(2,1)} %param.6), kind=kOutput, calls=%fused_computation.2 | convolution fusion | flops 13433440256 | bytes 21504000 | tf_op jit(solution)/shard_map/dot_general | solution.py:83
  26.3 9.6 %copy.7 = bf16[2048,1601]{1,0:T(8,128)(2,1)} copy(bf16[2048,1601]{0,1:T(8,128)(2,1)} %convolution_convert_fusion) | data formatting | bytes 13115392 | tf_op jit(solution)/shard_map/convert_element_type | solution.py:85
  35.8 0.0 copy-start.2
  35.8 0.0 reduce-scatter.2.cloned.1.call-update
  35.9 0.7 copy-done.2
  36.5 1.1 reduce-window.6
  37.7 0.2 slice_reduce_fusion
  37.9 0.1 fusion.3
  38.0 7.7 %scatter_custom_fusion = bf16[1024,2048]{1,0:T(8,128)(2,1)} fusion(s32[512]{0:T(512)S(1)} %bitcast.23, bf16[512,2048]{1,0:T(8,128)(2,1)} %param.4, bf16[]{:T(256)} %constant.5.clone.1), kind=kCustom, calls=%fused_computation.4 | custom fusion | bytes 4194816 | tf_op jit(solution)/shard_map/scatter | solution.py:77
  45.7 54.2 %all_to_all.10 = bf16[8,128,2048]{2,1,0:T(8,128)(2,1)} all-to-all(bf16[8,128,2048]{2,1,0:T(8,128)(2,1)} %bitcast.19), channel_id=1, replica_groups=mesh['seq'=8,'tensor'=4] {'seq'}, dimensions={0} | all-to-all | bytes 8388608 | tf_op jit(solution)/shard_map/all_to_all | solution.py:90
  100.0 58.0 %reduce-scatter.2.cloned.1.call-done.k_ref.v_ref = bf16[512,1601]{1,0:T(8,128)(2,1)} async-done(((bf16[2048,1601]{1,0:T(8,128)(2,1)}), bf16[512,1601]{1,0:T(8,128)(2,1)}) %reduce-scatter.2.cloned.1.call-update) | async-done | bytes 1639440 | tf_op jit(solution)/shard_map/reduce_scatter | solution.py:82
  158.0 0.0 copy-start.1
  158.0 1.5 copy-done.1
  159.5 90.7 %shard_map.46 = bf16[1024,2048]{1,0:T(8,128)(2,1)S(1)} custom-call(bf16[1024,2048]{1,0:T(8,128)(2,1)} %bitcast.20, bf16[512,1601]{1,0:T(8,128)(2,1)S(1)} %copy-done.1, bf16[512,1601]{1,0:T(8,128)(2,1)S(1)} %copy-done.1), custom_call_target="tpu_custom_call" | custom-call | flops 13430161408 | bytes 10028032 | tf_op jit(solution)/shard_map/pallas_call | solution.py:42
  250.1 0.0 copy-start
  250.2 2.0 copy-done
  252.1 4.5 %all-to-all-start.1 = ((bf16[8,128,2048]{2,1,0:T(8,128)(2,1)}), bf16[8,128,2048]{2,1,0:T(8,128)(2,1)}, u32[]{:S(2)}, u32[]{:S(2)}) async-start(bf16[8,128,2048]{2,1,0:T(8,128)(2,1)} %bitcast.18), calls=%async_computation.2 | async-start | bytes 8388608 | tf_op jit(solution)/shard_map/all_to_all | solution.py:93
  256.7 49.1 %all-to-all-done.1 = bf16[8,128,2048]{2,1,0:T(8,128)(2,1)} async-done(((bf16[8,128,2048]{2,1,0:T(8,128)(2,1)}), bf16[8,128,2048]{2,1,0:T(8,128)(2,1)}, u32[]{:S(2)}, u32[]{:S(2)}) %all-to-all-start.1) | async-done | bytes 4194336 | tf_op jit(solution)/shard_map/all_to_all | solution.py:93
  305.8 8.0 %gather_fusion = bf16[512,2048]{1,0:T(8,128)(2,1)} fusion(bf16[1024,2048]{1,0:T(8,128)(2,1)} %bitcast.10, s32[1024]{0:T(1024)S(1)} %pad_clamp_fusion), kind=kCustom, calls=%fused_computation | custom fusion | bytes 4196352 | tf_op jit(solution)/shard_map/gather | solution.py:94
  (5 shorter events, 0.1 us)
Async XLA Ops:
  6.5 151.5 %reduce-scatter.2.cloned.1.call-start = ((), (), s32[]{:S(2)}) async-start(), calls=%async_computation.3 | async-start | bytes 8519680 | tf_op jit(solution)/shard_map/reduce_scatter | solution.py:82
  35.8 0.7 copy-start.2
  158.0 1.5 copy-start.1
  250.1 2.0 copy-start
  252.1 53.6 %all-to-all-start.1 = ((bf16[8,128,2048]{2,1,0:T(8,128)(2,1)}), bf16[8,128,2048]{2,1,0:T(8,128)(2,1)}, u32[]{:S(2)}, u32[]{:S(2)}) async-start(bf16[8,128,2048]{2,1,0:T(8,128)(2,1)} %bitcast.18), calls=%async_computation.2 | async-start | bytes 8388608 | tf_op jit(solution)/shard_map/all_to_all | solution.py:93
Sparse Core Ops, SparseCore 0:
  36.0 121.9 reduce-scatter.1

commit v2 on v1

v2 whole, which is shorter than its diff:
```python
import functools

import jax
import jax.numpy as jnp
from jax import lax
from jax.experimental import pallas as pl
from jax.experimental.pallas import tpu as pltpu
from jax.sharding import PartitionSpec as P

HEADS = 64
KV_HEADS = 8
HEAD_DIM = 128
ROW_TILE = 256


def attend_kernel(scale, q_ref, k_ref, v_ref, o_ref):
    q = q_ref[...]
    scores = (
        lax.dot_general(
            q, k_ref[...], (((1,), (1,)), ((), ())), preferred_element_type=jnp.float32
        )
        * scale
    )
    row_max = jnp.max(scores, axis=1, keepdims=True)
    weights_exp = jnp.exp(scores - row_max)
    totals = jnp.sum(weights_exp, axis=1, keepdims=True)
    probs = weights_exp.astype(jnp.bfloat16)
    weighted = jnp.dot(probs, v_ref[...], preferred_element_type=jnp.float32)
    o_ref[...] = (weighted / totals).astype(o_ref.dtype)


def attend(query_rows, key_values, group, head_dim, first_head):
    rows = query_rows.shape[0]
    query_heads = group
    width = group * head_dim
    image_len = key_values.shape[0]
    tile = min(ROW_TILE, rows)
    assert rows % tile == 0
    scale = head_dim ** (-0.5)
    flops = 4 * rows * query_heads * image_len * head_dim
    return pl.pallas_call(
        functools.partial(attend_kernel, scale),
        out_shape=jax.ShapeDtypeStruct((rows, width), jnp.bfloat16),
        grid=(query_heads, rows // tile),
        in_specs=[
            pl.BlockSpec((tile, head_dim), lambda h, i: (i, first_head + h)),
            pl.BlockSpec((image_len, head_dim), lambda h, i: (0, 0)),
            pl.BlockSpec((image_len, head_dim), lambda h, i: (0, 1)),
        ],
        out_specs=pl.BlockSpec((tile, head_dim), lambda h, i: (i, h)),
        compiler_params=pltpu.CompilerParams(
            dimension_semantics=("arbitrary", "arbitrary"),
            vmem_limit_bytes=48 * 1024 * 1024,
        ),
        cost_estimate=pl.CostEstimate(
            flops=flops,
            transcendentals=rows * query_heads * image_len,
            bytes_accessed=2 * (2 * rows * width + key_values.size),
        ),
    )(query_rows, key_values, key_values)


def on_device(queries, image_refs, features, kv_weight):
    seq_devices = lax.axis_size("seq")
    token_count = queries.shape[0]
    width_cols = queries.shape[1]
    capacity = 2 * token_count // seq_devices
    owners = image_refs[:, 0]
    onehot = (owners[:, None] == jnp.arange(seq_devices, dtype=jnp.int32)[None, :]).astype(
        jnp.int32
    )
    running = jnp.cumsum(onehot, axis=0)
    position = jnp.sum(onehot * (running - 1), axis=1)
    slot_index = owners * capacity + position
    outgoing = (
        jnp.zeros((seq_devices * capacity, width_cols), jnp.bfloat16).at[slot_index].set(queries)
    )
    outgoing = outgoing.reshape(seq_devices, capacity, width_cols)
    group = HEADS // KV_HEADS
    image_block = features[0]
    tensor_devices = lax.axis_size("tensor")
    local_kv = KV_HEADS // tensor_devices
    split_weight = kv_weight.reshape(kv_weight.shape[0], tensor_devices, local_kv, 2 * HEAD_DIM)
    received = lax.all_to_all(outgoing, "seq", split_axis=0, concat_axis=0, tiled=True)
    flat_rows = received.reshape(-1, width_cols)
    pieces = []
    for head in range(local_kv):
        weight_part = split_weight[:, :, head, :].reshape(kv_weight.shape[0], -1)
        key_values = lax.psum_scatter(
            jnp.dot(image_block, weight_part, preferred_element_type=jnp.float32).astype(
                jnp.bfloat16
            ),
            "tensor",
            scatter_dimension=1,
            tiled=True,
        )
        answered = attend(flat_rows, key_values, group, HEAD_DIM, head * group)
        answered = answered.reshape(seq_devices, capacity, -1)
        returned = lax.all_to_all(answered, "seq", split_axis=0, concat_axis=0, tiled=True)
        pieces.append(returned.reshape(seq_devices * capacity, -1)[slot_index])
    return jnp.concatenate(pieces, axis=1)


def solution(mesh):
    placed = (P("seq", "tensor"), P("seq", None), P("seq", None, "tensor"), P("tensor", None))
    return jax.shard_map(
        on_device, mesh=mesh, in_specs=placed, out_specs=P("seq", "tensor"), check_vma=False
    )
```

time: 321 us -> 248 us (0.77)
  waiting for transfers between devices: 107 us -> 37.8 us
  Pallas kernels: 90.7 us -> 75.5 us
  local copies, waits for them, and re-layouts: 29.5 us -> 35 us
  starting transfers between devices: 4.55 us -> 7.99 us
    reduce_scatter x1 -> x2, waiting for transfers between devices: 58 us -> 13.2 us  [on_device(): lax.psum_scatter(jnp.dot(image_block, weight_part, preferred_element_type...]
    all_to_all x1 -> x2, waiting for transfers between devices: 49.1 us -> 24.5 us  [on_device(): lax.all_to_all(answered, 'seq', split_axis=0, concat_axis=0, tiled=True)]
    pallas_call x1 -> x2, Pallas kernels: 90.7 us -> 75.5 us  [attend(): pl.pallas_call(functools.partial(attend_kernel, scale), out_shape=jax.Sha...]
    unnamed x6 -> x11, local copies, waits for them, and re-layouts: 4.07 us -> 15.6 us
    convert_element_type x1 -> x0, local copies, waits for them, and re-layouts: 9.58 us -> none  [on_device(): kv_t = lax.psum_scatter(lax.dot_general(kv_weight, image_block, (((0,), (...]
    slice x1 -> x2, local copies, waits for them, and re-layouts: 0.21 us -> 5.56 us  [the longest x1 5.35 us: on_device(): weight_part = split_weight[:, :, head, :].reshape(kv_weight.shape[0], -1)]
    all_to_all x1 -> x2, starting transfers between devices: 4.54 us -> 7.94 us  [on_device(): lax.all_to_all(answered, 'seq', split_axis=0, concat_axis=0, tiled=True)]
    gather x1 -> x2, local copies, waits for them, and re-layouts: 7.95 us -> 6.65 us  [on_device(): pieces.append(returned.reshape(seq_devices * capacity, -1)[slot_index])]
  transfers between devices with their start and end apart: 2 -> 4, of which waited for: 2 -> 2; matrix products, arithmetic and copies ran while one was open for 3% -> 9% of each run, Pallas kernels for 0% -> 30%
where the time goes in v2:
time: 248 us
  Pallas kernels  75.5 us (30%)
  blocking collectives  54.4 us (22%)
  waiting for transfers between devices  37.8 us (15%)
  local copies, waits for them, and re-layouts  35 us (14%)
  matrix products  20.7 us (8%)
  between operations  13.5 us (5%)
  starting transfers between devices  7.99 us (3%)
  other arithmetic  2.8 us (1%)
    pallas_call x2, Pallas kernels, attend(): pl.pallas_call(functools.partial(attend_kernel, scale), out_shape=jax.Sha...  75.5 us
    all_to_all x1, blocking collectives, on_device(): lax.all_to_all(outgoing, 'seq', split_axis=0, concat_axis=0, tiled=True)  54.4 us
    all_to_all x2, waiting for transfers between devices, on_device(): lax.all_to_all(answered, 'seq', split_axis=0, concat_axis=0, tiled=True)  24.5 us
    dot_general x2, matrix products, on_device(): jnp.dot(image_block, weight_part, preferred_element_type=jnp.float32)  20.7 us
    unnamed x11, local copies, waits for them, and re-layouts  15.6 us
    reduce_scatter x2, waiting for transfers between devices, on_device(): lax.psum_scatter(jnp.dot(image_block, weight_part, preferred_element_type...  13.2 us
    all_to_all x2, starting transfers between devices, on_device(): lax.all_to_all(answered, 'seq', split_axis=0, concat_axis=0, tiled=True)  7.94 us
    scatter x1, local copies, waits for them, and re-layouts, on_device(): jnp.zeros((seq_devices * capacity, width_cols), jnp.bfloat16).at[slot_index]  7.25 us
  transfers between devices with their start and end apart: 4, of which 2 were waited for; matrix products, arithmetic and copies ran while one was open for 9% of the time, Pallas kernels for 30%

profile of v2, /device:TPU:0, one launch (start us, length us, event | category | flops | bytes accessed | tf_op | source)
XLA Modules:
  0.0 247.7 jit_solution(6533407798258016971)
XLA Ops:
  6.5 0.0 reduce-scatter.3.cloned.1.call-start
  6.5 0.0 slice-start
  6.5 12.5 %copy.5 = bf16[2048,2048]{0,1:T(8,128)(2,1)} copy(bf16[2048,2048]{1,0:T(8,128)(2,1)} %param.7) | data formatting | bytes 16777216 | tf_op args[3]
  19.0 0.0 slice-start.1
  19.0 5.3 %fusion.14 = (bf16[2048,4,1,256]{0,3,2,1:T(8,128)(2,1)S(1)}, bf16[2048,4,1,256]{0,3,2,1:T(8,128)(2,1)}) fusion(bf16[2048,4,2,256]{0,3,2,1:T(8,128)(2,1)} %bitcast.31), kind=kLoop, calls=%fused_computation.20 | loop fusion | bytes 16777216 | tf_op jit(solution)/shard_map/slice | solution.py:88
  24.4 0.0 slice-done
  24.4 0.8 slice-done.1
  25.2 8.6 %fusion.4 = bf16[1601,1024]{1,0:T(8,128)(2,1)} fusion(bf16[2048,1024]{0,1:T(8,128)(2,1)S(1)} %bitcast.36, bf16[1,1601,2048]{2,1,0:T(8,128)(2,1)S(1)} %bitcast.43), kind=kOutput, calls=%fused_computation.7 | convolution fusion | flops 6716720128 | bytes 14030848 | tf_op jit(solution)/shard_map/dot_general | solution.py:90
  33.8 0.0 reduce-scatter.3.cloned.1.call-update
  33.8 0.0 reduce-scatter.5.cloned.1.call-start
  33.9 0.0 copy-start.2
  33.9 12.0 %fusion.7 = bf16[1601,1024]{1,0:T(8,128)(2,1)} fusion(bf16[2048,1024]{0,1:T(8,128)(2,1)} %bitcast.35, bf16[1,1601,2048]{2,1,0:T(8,128)(2,1)} %param.6), kind=kOutput, calls=%fused_computation.8 | convolution fusion | flops 6716720128 | bytes 14030848 | tf_op jit(solution)/shard_map/dot_general | solution.py:90
  45.9 0.0 reduce-scatter.5.cloned.1.call-update
  46.0 0.0 copy-done.2
  46.0 1.1 reduce-window.6
  47.1 0.2 slice_reduce_fusion
  47.4 0.1 fusion.12
  47.5 7.3 %scatter_custom_fusion = bf16[1024,2048]{1,0:T(8,128)(2,1)} fusion(s32[512]{0:T(512)S(1)} %bitcast.39, bf16[512,2048]{1,0:T(8,128)(2,1)} %param.4, bf16[]{:T(256)} %constant.5.clone.1), kind=kCustom, calls=%fused_computation.10 | custom fusion | bytes 4194816 | tf_op jit(solution)/shard_map/scatter | solution.py:76
  54.7 54.4 %all_to_all.15 = bf16[8,128,2048]{2,1,0:T(8,128)(2,1)} all-to-all(bf16[8,128,2048]{2,1,0:T(8,128)(2,1)} %bitcast.32), channel_id=1, replica_groups=mesh['seq'=8,'tensor'=4] {'seq'}, dimensions={0} | all-to-all | bytes 8388608 | tf_op jit(solution)/shard_map/all_to_all | solution.py:84
  109.1 0.0 reduce-scatter.3.cloned.1.call-done.k_ref.v_ref
  109.1 0.0 copy-start
  109.1 1.1 copy-done
  110.2 37.7 %shard_map.46 = bf16[1024,1024]{1,0:T(8,128)(2,1)} custom-call(bf16[1024,2048]{1,0:T(8,128)(2,1)} %bitcast.33, bf16[1601,256]{1,0:T(8,128)(2,1)S(1)} %copy-done, bf16[1601,256]{1,0:T(8,128)(2,1)S(1)} %copy-done), custom_call_target="tpu_custom_call" | custom-call | flops 6715080704 | bytes 5014016 | tf_op jit(solution)/shard_map/pallas_call | solution.py:41
  147.9 3.6 %all-to-all-start.1 = ((bf16[8,128,1024]{2,1,0:T(8,128)(2,1)}), bf16[8,128,1024]{2,1,0:T(8,128)(2,1)S(1)}, u32[]{:S(2)}, u32[]{:S(2)}) async-start(bf16[8,128,1024]{2,1,0:T(8,128)(2,1)} %bitcast.11), calls=%async_computation.2 | async-start | bytes 4194304 | tf_op jit(solution)/shard_map/all_to_all | solution.py:99
  151.5 13.2 %reduce-scatter.5.cloned.1.call-done.k_ref.v_ref = bf16[1601,256]{1,0:T(8,128)(2,1)} async-done(((bf16[1601,1024]{1,0:T(8,128)(2,1)}), bf16[1601,256]{1,0:T(8,128)(2,1)}) %reduce-scatter.5.cloned.1.call-update) | async-done | bytes 819728 | tf_op jit(solution)/shard_map/reduce_scatter | solution.py:89
  164.8 0.0 copy-start.1
  164.8 1.1 copy-done.1
  165.9 37.8 %shard_map.47 = bf16[1024,1024]{1,0:T(8,128)(2,1)} custom-call(bf16[1024,2048]{1,0:T(8,128)(2,1)} %bitcast.34, bf16[1601,256]{1,0:T(8,128)(2,1)S(1)} %copy-done.1, bf16[1601,256]{1,0:T(8,128)(2,1)S(1)} %copy-done.1), custom_call_target="tpu_custom_call" | custom-call | flops 6715080704 | bytes 5014016 | tf_op jit(solution)/shard_map/pallas_call | solution.py:41
  203.7 0.0 all-to-all-done.1
  203.7 4.3 %all-to-all-start.2 = ((bf16[8,128,1024]{2,1,0:T(8,128)(2,1)}), bf16[8,128,1024]{2,1,0:T(8,128)(2,1)}, u32[]{:S(2)}, u32[]{:S(2)}) async-start(bf16[8,128,1024]{2,1,0:T(8,128)(2,1)} %bitcast.14), calls=%async_computation.4 | async-start | bytes 4194304 | tf_op jit(solution)/shard_map/all_to_all | solution.py:99
  208.1 2.1 gather_fusion
  210.2 24.5 %all-to-all-done.2 = bf16[8,128,1024]{2,1,0:T(8,128)(2,1)} async-done(((bf16[8,128,1024]{2,1,0:T(8,128)(2,1)}), bf16[8,128,1024]{2,1,0:T(8,128)(2,1)}, u32[]{:S(2)}, u32[]{:S(2)}) %all-to-all-start.2) | async-done | bytes 2097184 | tf_op jit(solution)/shard_map/all_to_all | solution.py:99
  234.7 4.6 %gather_fusion.1 = bf16[512,1024]{1,0:T(8,128)(2,1)S(1)} fusion(bf16[1024,1024]{1,0:T(8,128)(2,1)} %bitcast.15, s32[1024]{0:T(1024)S(1)} %pad_clamp_fusion), kind=kCustom, calls=%fused_computation.1 | custom fusion | bytes 2099200 | tf_op jit(solution)/shard_map/gather | solution.py:100
  239.3 1.5 pad_maximum_fusion
  (6 shorter events, 0.1 us)
Async XLA Ops:
  6.5 102.6 %reduce-scatter.3.cloned.1.call-start = ((), (), s32[]{:S(2)}) async-start(), calls=%async_computation.5 | async-start | bytes 4116480 | tf_op jit(solution)/shard_map/reduce_scatter | solution.py:89
  6.5 17.8 %slice-start = ((s8[6586368]{0:T(1024)(128)(4,1)}), s8[2392064]{0:T(1024)(128)(4,1)S(1)}, s32[]{:S(2)}) async-start(s8[6586368]{0:T(1024)(128)(4,1)} %bitcast.42), calls=%async_computation.7 | async-start | bytes 4784128
  19.0 6.2 %slice-start.1 = ((s8[6586368]{0:T(1024)(128)(4,1)}), s8[4194304]{0:T(1024)(128)(4,1)S(1)}, s32[]{:S(2)}) async-start(s8[6586368]{0:T(1024)(128)(4,1)} %bitcast.42), calls=%async_computation.8 | async-start | bytes 8388608
  33.8 130.9 %reduce-scatter.5.cloned.1.call-start = ((), (), s32[]{:S(2)}) async-start(), calls=%async_computation.6 | async-start | bytes 4116480 | tf_op jit(solution)/shard_map/reduce_scatter | solution.py:89
  33.9 12.1 %copy-start.2 = (s32[512,1]{0,1:T(1,128)S(1)}, s32[512,1]{0,1:T(1,128)}, u32[]{:S(2)}) copy-start(s32[512,1]{0,1:T(1,128)} %param.5) | copy-start | bytes 6148
  109.1 1.1 copy-start
  147.9 55.8 %all-to-all-start.1 = ((bf16[8,128,1024]{2,1,0:T(8,128)(2,1)}), bf16[8,128,1024]{2,1,0:T(8,128)(2,1)S(1)}, u32[]{:S(2)}, u32[]{:S(2)}) async-start(bf16[8,128,1024]{2,1,0:T(8,128)(2,1)} %bitcast.11), calls=%async_computation.2 | async-start | bytes 4194304 | tf_op jit(solution)/shard_map/all_to_all | solution.py:99
  164.8 1.1 copy-start.1
  203.7 31.0 %all-to-all-start.2 = ((bf16[8,128,1024]{2,1,0:T(8,128)(2,1)}), bf16[8,128,1024]{2,1,0:T(8,128)(2,1)}, u32[]{:S(2)}, u32[]{:S(2)}) async-start(bf16[8,128,1024]{2,1,0:T(8,128)(2,1)} %bitcast.14), calls=%async_computation.4 | async-start | bytes 4194304 | tf_op jit(solution)/shard_map/all_to_all | solution.py:99
Sparse Core Ops, SparseCore 0:
  34.0 65.5 reduce-scatter.2
  101.9 62.8 reduce-scatter.4

commit v3 on v2

--- a/solution.py
+++ b/solution.py
@@ -14,6 +14,7 @@
 
 
 def attend_kernel(scale, q_ref, k_ref, v_ref, o_ref):
+    head_dim = o_ref.shape[1]
     q = q_ref[...]
     scores = (
         lax.dot_general(
@@ -23,10 +24,10 @@
     )
     row_max = jnp.max(scores, axis=1, keepdims=True)
     weights_exp = jnp.exp(scores - row_max)
-    totals = jnp.sum(weights_exp, axis=1, keepdims=True)
     probs = weights_exp.astype(jnp.bfloat16)
     weighted = jnp.dot(probs, v_ref[...], preferred_element_type=jnp.float32)
-    o_ref[...] = (weighted / totals).astype(o_ref.dtype)
+    totals = weighted[:, head_dim : head_dim + 1]
+    o_ref[...] = (weighted[:, :head_dim] / totals).astype(o_ref.dtype)
 
 
 def attend(query_rows, key_values, group, head_dim, first_head):
@@ -34,10 +35,13 @@
     query_heads = group
     width = group * head_dim
     image_len = key_values.shape[0]
+    values_ones = jnp.concatenate(
+        [key_values[:, head_dim:], jnp.ones((image_len, head_dim), key_values.dtype)], axis=1
+    )
     tile = min(ROW_TILE, rows)
     assert rows % tile == 0
     scale = head_dim ** (-0.5)
-    flops = 4 * rows * query_heads * image_len * head_dim
+    flops = 6 * rows * query_heads * image_len * head_dim
     return pl.pallas_call(
         functools.partial(attend_kernel, scale),
         out_shape=jax.ShapeDtypeStruct((rows, width), jnp.bfloat16),
@@ -45,7 +49,7 @@
         in_specs=[
             pl.BlockSpec((tile, head_dim), lambda h, i: (i, first_head + h)),
             pl.BlockSpec((image_len, head_dim), lambda h, i: (0, 0)),
-            pl.BlockSpec((image_len, head_dim), lambda h, i: (0, 1)),
+            pl.BlockSpec((image_len, 2 * head_dim), lambda h, i: (0, 0)),
         ],
         out_specs=pl.BlockSpec((tile, head_dim), lambda h, i: (i, h)),
         compiler_params=pltpu.CompilerParams(
@@ -57,7 +61,7 @@
             transcendentals=rows * query_heads * image_len,
             bytes_accessed=2 * (2 * rows * width + key_values.size),
         ),
-    )(query_rows, key_values, key_values)
+    )(query_rows, key_values, values_ones)
 
 
 def on_device(queries, image_refs, features, kv_weight):
@@ -80,15 +84,21 @@
     image_block = features[0]
     tensor_devices = lax.axis_size("tensor")
     local_kv = KV_HEADS // tensor_devices
-    split_weight = kv_weight.reshape(kv_weight.shape[0], tensor_devices, local_kv, 2 * HEAD_DIM)
+    projected = jnp.dot(image_block, kv_weight, preferred_element_type=jnp.float32).astype(
+        jnp.bfloat16
+    )
+    kv_width = 2 * HEAD_DIM
     received = lax.all_to_all(outgoing, "seq", split_axis=0, concat_axis=0, tiled=True)
     flat_rows = received.reshape(-1, width_cols)
     pieces = []
     for head in range(local_kv):
-        weight_part = split_weight[:, :, head, :].reshape(kv_weight.shape[0], -1)
         key_values = lax.psum_scatter(
-            jnp.dot(image_block, weight_part, preferred_element_type=jnp.float32).astype(
-                jnp.bfloat16
+            jnp.concatenate(
+                [
+                    projected[:, (dest * local_kv + head) * kv_width :][:, :kv_width]
+                    for dest in range(tensor_devices)
+                ],
+                axis=1,
             ),
             "tensor",
             scatter_dimension=1,

time: 248 us -> 250 us (level)
  blocking collectives: 54.4 us -> 0 us
  waiting for transfers between devices: 37.8 us -> 87.7 us
  local copies, waits for them, and re-layouts: 35 us -> 19 us
  Pallas kernels: 75.5 us -> 90.2 us
  starting transfers between devices: 7.99 us -> 13.4 us
  other arithmetic: 2.8 us -> 7.73 us
  matrix products: 20.7 us -> 18 us
    all_to_all x1 -> x0, blocking collectives: 54.4 us -> none  [on_device(): lax.all_to_all(outgoing, 'seq', split_axis=0, concat_axis=0, tiled=True)]
    reduce_scatter x2, waiting for transfers between devices: 13.2 us -> 63.1 us  [on_device(): lax.psum_scatter(jnp.concatenate([projected[:, (dest * local_kv + head) *...]
    pallas_call x2, Pallas kernels: 75.5 us -> 90.2 us  [attend(): pl.pallas_call(functools.partial(attend_kernel, scale), out_shape=jax.Sha...]
    unnamed x11 -> x6, local copies, waits for them, and re-layouts: 15.6 us -> 2.28 us
    all_to_all x0 -> x1, starting transfers between devices: none -> 5.19 us  [on_device(): lax.all_to_all(outgoing, 'seq', split_axis=0, concat_axis=0, tiled=True)]
    concatenate x0 -> x2, other arithmetic: none -> 4.95 us  [on_device(): jnp.concatenate([projected[:, (dest * local_kv + head) * kv_width:][:, :k...]
    slice x2 -> x4, local copies, waits for them, and re-layouts: 5.56 us -> 2.7 us  [the longest x2 2.06 us: attend(): key_values[:, head_dim:]]
    dot_general x2 -> x1, matrix products: 20.7 us -> 18 us  [on_device(): jnp.dot(image_block, kv_weight, preferred_element_type=jnp.float32)]
  transfers between devices with their start and end apart: 4 -> 5, of which waited for: 2 -> 3; matrix products, arithmetic and copies ran while one was open for 9% -> 6% of each run, Pallas kernels for 30% -> 36%
where the time goes in v3:
time: 250 us
  Pallas kernels  90.2 us (36%)
  waiting for transfers between devices  87.7 us (35%)
  local copies, waits for them, and re-layouts  19 us (8%)
  matrix products  18 us (7%)
  between operations  13.5 us (5%)
  starting transfers between devices  13.4 us (5%)
  other arithmetic  7.73 us (3%)
    pallas_call x2, Pallas kernels, attend(): pl.pallas_call(functools.partial(attend_kernel, scale), out_shape=jax.Sha...  90.2 us
    reduce_scatter x2, waiting for transfers between devices, on_device(): lax.psum_scatter(jnp.concatenate([projected[:, (dest * local_kv + head) *...  63.1 us
    all_to_all x2, waiting for transfers between devices, on_device(): lax.all_to_all(answered, 'seq', split_axis=0, concat_axis=0, tiled=True)  24.5 us
    dot_general x1, matrix products, on_device(): jnp.dot(image_block, kv_weight, preferred_element_type=jnp.float32)  18 us
    all_to_all x2, starting transfers between devices, on_device(): lax.all_to_all(answered, 'seq', split_axis=0, concat_axis=0, tiled=True)  8.12 us
    scatter x1, local copies, waits for them, and re-layouts, on_device(): jnp.zeros((seq_devices * capacity, width_cols), jnp.bfloat16).at[slot_index]  7.25 us
    gather x2, local copies, waits for them, and re-layouts, on_device(): pieces.append(returned.reshape(seq_devices * capacity, -1)[slot_index])  6.65 us
    all_to_all x1, starting transfers between devices, on_device(): lax.all_to_all(outgoing, 'seq', split_axis=0, concat_axis=0, tiled=True)  5.19 us
  transfers between devices with their start and end apart: 5, of which 3 were waited for; matrix products, arithmetic and copies ran while one was open for 6% of the time, Pallas kernels for 36%

profile of v3, /device:TPU:0, one launch (start us, length us, event | category | flops | bytes accessed | tf_op | source)
XLA Modules:
  0.0 249.5 jit_solution(12062299215119680771)
XLA Ops:
  6.5 0.0 reduce-scatter.3.cloned.1.call-start
  6.5 18.0 %convolution_convert_fusion = bf16[1601,2048]{1,0:T(8,128)(2,1)S(1)} fusion(bf16[2048,2048]{1,0:T(8,128)(2,1)} %param.7, bf16[1,1601,2048]{2,1,0:T(8,128)(2,1)} %param.6), kind=kOutput, calls=%fused_computation.3 | convolution fusion | flops 13433440256 | bytes 21504000 | tf_op jit(solution)/shard_map/dot_general | solution.py:87
  24.5 0.4 fusion.5
  24.9 2.5 pad_maximum_fusion
  27.4 0.0 reduce-scatter.3.cloned.1.call-update
  27.4 0.0 reduce-scatter.5.cloned.1.call-start
  27.5 0.0 copy-start.2
  27.5 2.5 pad_maximum_fusion.1
  30.0 0.0 reduce-scatter.5.cloned.1.call-update
  30.0 0.0 copy-done.2
  30.0 1.1 reduce-window.6
  31.2 0.2 slice_reduce_fusion
  31.4 0.1 fusion.3
  31.5 7.3 %scatter_custom_fusion = bf16[1024,2048]{1,0:T(8,128)(2,1)} fusion(s32[512]{0:T(512)S(1)} %bitcast.24, bf16[512,2048]{1,0:T(8,128)(2,1)} %param.4, bf16[]{:T(256)} %constant.6.clone.1), kind=kCustom, calls=%fused_computation.8 | custom fusion | bytes 4194816 | tf_op jit(solution)/shard_map/scatter | solution.py:80
  38.8 5.2 %all-to-all-start = ((bf16[8,128,2048]{2,1,0:T(8,128)(2,1)}), bf16[8,128,2048]{2,1,0:T(8,128)(2,1)}, u32[]{:S(2)}, u32[]{:S(2)}) async-start(bf16[8,128,2048]{2,1,0:T(8,128)(2,1)} %bitcast.21), calls=%async_computation | async-start | bytes 8388608 | tf_op jit(solution)/shard_map/all_to_all | solution.py:91
  44.0 49.2 %reduce-scatter.3.cloned.1.call-done.k_ref = bf16[1601,256]{1,0:T(8,128)(2,1)} async-done(((bf16[1601,1024]{1,0:T(8,128)(2,1)}), bf16[1601,256]{1,0:T(8,128)(2,1)}) %reduce-scatter.3.cloned.1.call-update) | async-done | bytes 819728 | tf_op jit(solution)/shard_map/reduce_scatter | solution.py:95
  93.2 1.0 slice.69
  94.2 0.1 concatenate.16.v_ref
  94.3 0.0 all-to-all-done
  94.3 0.0 copy-start
  94.3 1.1 copy-done
  95.5 45.2 %shard_map.46 = bf16[1024,1024]{1,0:T(8,128)(2,1)} custom-call(bf16[1024,2048]{1,0:T(8,128)(2,1)} %bitcast.7.q_ref, bf16[1601,256]{1,0:T(8,128)(2,1)S(1)} %copy-done, bf16[1601,256]{1,0:T(8,128)(2,1)S(1)} %concatenate.16.v_ref), custom_call_target="tpu_custom_call" | custom-call | flops 10072621056 | bytes 5014016 | tf_op jit(solution)/shard_map/pallas_call | solution.py:45
  140.7 3.8 %all-to-all-start.1 = ((bf16[8,128,1024]{2,1,0:T(8,128)(2,1)}), bf16[8,128,1024]{2,1,0:T(8,128)(2,1)S(1)}, u32[]{:S(2)}, u32[]{:S(2)}) async-start(bf16[8,128,1024]{2,1,0:T(8,128)(2,1)} %bitcast.9), calls=%async_computation.2 | async-start | bytes 4194304 | tf_op jit(solution)/shard_map/all_to_all | solution.py:109
  144.5 13.9 %reduce-scatter.5.cloned.1.call-done.k_ref = bf16[1601,256]{1,0:T(8,128)(2,1)} async-done(((bf16[1601,1024]{1,0:T(8,128)(2,1)}), bf16[1601,256]{1,0:T(8,128)(2,1)}) %reduce-scatter.5.cloned.1.call-update) | async-done | bytes 819728 | tf_op jit(solution)/shard_map/reduce_scatter | solution.py:95
  158.4 1.0 slice.74
  159.4 0.1 concatenate.18.v_ref
  159.5 0.0 copy-start.1
  159.5 1.1 copy-done.1
  160.7 44.9 %shard_map.47 = bf16[1024,1024]{1,0:T(8,128)(2,1)} custom-call(bf16[1024,2048]{1,0:T(8,128)(2,1)} %bitcast.7.q_ref, bf16[1601,256]{1,0:T(8,128)(2,1)S(1)} %copy-done.1, bf16[1601,256]{1,0:T(8,128)(2,1)S(1)} %concatenate.18.v_ref), custom_call_target="tpu_custom_call" | custom-call | flops 10072621056 | bytes 5014016 | tf_op jit(solution)/shard_map/pallas_call | solution.py:45
  205.6 0.0 all-to-all-done.1
  205.6 4.3 %all-to-all-start.2 = ((bf16[8,128,1024]{2,1,0:T(8,128)(2,1)}), bf16[8,128,1024]{2,1,0:T(8,128)(2,1)}, u32[]{:S(2)}, u32[]{:S(2)}) async-start(bf16[8,128,1024]{2,1,0:T(8,128)(2,1)} %bitcast.11), calls=%async_computation.4 | async-start | bytes 4194304 | tf_op jit(solution)/shard_map/all_to_all | solution.py:109
  210.0 2.1 gather_fusion
  212.0 24.5 %all-to-all-done.2 = bf16[8,128,1024]{2,1,0:T(8,128)(2,1)} async-done(((bf16[8,128,1024]{2,1,0:T(8,128)(2,1)}), bf16[8,128,1024]{2,1,0:T(8,128)(2,1)}, u32[]{:S(2)}, u32[]{:S(2)}) %all-to-all-start.2) | async-done | bytes 2097184 | tf_op jit(solution)/shard_map/all_to_all | solution.py:109
  236.6 4.6 %gather_fusion.1 = bf16[512,1024]{1,0:T(8,128)(2,1)S(1)} fusion(bf16[1024,1024]{1,0:T(8,128)(2,1)} %bitcast.12, s32[1024]{0:T(1024)S(1)} %pad_clamp_fusion), kind=kCustom, calls=%fused_computation.1 | custom fusion | bytes 2099200 | tf_op jit(solution)/shard_map/gather | solution.py:110
  241.2 1.5 pad_maximum_fusion.2
  (5 shorter events, 0.1 us)
Async XLA Ops:
  6.5 86.7 %reduce-scatter.3.cloned.1.call-start = ((), (), s32[]{:S(2)}) async-start(), calls=%async_computation.5 | async-start | bytes 4116480 | tf_op jit(solution)/shard_map/reduce_scatter | solution.py:95
  27.4 131.0 %reduce-scatter.5.cloned.1.call-start = ((), (), s32[]{:S(2)}) async-start(), calls=%async_computation.6 | async-start | bytes 4116480 | tf_op jit(solution)/shard_map/reduce_scatter | solution.py:95
  27.5 2.5 %copy-start.2 = (s32[512,1]{0,1:T(1,128)S(1)}, s32[512,1]{0,1:T(1,128)}, u32[]{:S(2)}) copy-start(s32[512,1]{0,1:T(1,128)} %param.5) | copy-start | bytes 6148
  38.8 55.5 %all-to-all-start = ((bf16[8,128,2048]{2,1,0:T(8,128)(2,1)}), bf16[8,128,2048]{2,1,0:T(8,128)(2,1)}, u32[]{:S(2)}, u32[]{:S(2)}) async-start(bf16[8,128,2048]{2,1,0:T(8,128)(2,1)} %bitcast.21), calls=%async_computation | async-start | bytes 8388608 | tf_op jit(solution)/shard_map/all_to_all | solution.py:91
  94.3 1.1 copy-start
  140.7 64.9 %all-to-all-start.1 = ((bf16[8,128,1024]{2,1,0:T(8,128)(2,1)}), bf16[8,128,1024]{2,1,0:T(8,128)(2,1)S(1)}, u32[]{:S(2)}, u32[]{:S(2)}) async-start(bf16[8,128,1024]{2,1,0:T(8,128)(2,1)} %bitcast.9), calls=%async_computation.2 | async-start | bytes 4194304 | tf_op jit(solution)/shard_map/all_to_all | solution.py:109
  159.5 1.1 copy-start.1
  205.6 31.0 %all-to-all-start.2 = ((bf16[8,128,1024]{2,1,0:T(8,128)(2,1)}), bf16[8,128,1024]{2,1,0:T(8,128)(2,1)}, u32[]{:S(2)}, u32[]{:S(2)}) async-start(bf16[8,128,1024]{2,1,0:T(8,128)(2,1)} %bitcast.11), calls=%async_computation.4 | async-start | bytes 4194304 | tf_op jit(solution)/shard_map/all_to_all | solution.py:109
Sparse Core Ops, SparseCore 0:
  27.6 65.5 reduce-scatter.2
  95.5 62.8 reduce-scatter.4

commit v4 on v3

v4 whole, which is shorter than its diff:
```python
import functools

import jax
import jax.numpy as jnp
from jax import lax
from jax.experimental import pallas as pl
from jax.experimental.pallas import tpu as pltpu
from jax.sharding import PartitionSpec as P

HEADS = 64
KV_HEADS = 8
HEAD_DIM = 128
ROW_TILE = 256


def attend_kernel(scale, tiles_ref, q_ref, k_ref, v_ref, o_ref):
    @pl.when(pl.program_id(1) < tiles_ref[0])
    def _():
        q = q_ref[...]
        scores = (
            lax.dot_general(
                q, k_ref[...], (((1,), (1,)), ((), ())), preferred_element_type=jnp.float32
            )
            * scale
        )
        row_max = jnp.max(scores, axis=1, keepdims=True)
        weights_exp = jnp.exp(scores - row_max)
        totals = jnp.sum(weights_exp, axis=1, keepdims=True)
        probs = weights_exp.astype(jnp.bfloat16)
        weighted = jnp.dot(probs, v_ref[...], preferred_element_type=jnp.float32)
        o_ref[...] = (weighted / totals).astype(o_ref.dtype)


def attend(query_rows, key_values, group, head_dim, first_head, live_tiles, tile):
    rows = query_rows.shape[0]
    query_heads = group
    width = group * head_dim
    image_len = key_values.shape[0]
    assert rows % tile == 0
    scale = head_dim ** (-0.5)
    flops = 4 * rows * query_heads * image_len * head_dim

    def row_block(i, tiles):
        return jnp.minimum(i, tiles[0] - 1)

    return pl.pallas_call(
        functools.partial(attend_kernel, scale),
        out_shape=jax.ShapeDtypeStruct((rows, width), jnp.bfloat16),
        grid_spec=pltpu.PrefetchScalarGridSpec(
            num_scalar_prefetch=1,
            grid=(query_heads, rows // tile),
            in_specs=[
                pl.BlockSpec((tile, head_dim), lambda h, i, t: (row_block(i, t), first_head + h)),
                pl.BlockSpec((image_len, head_dim), lambda h, i, t: (0, 0)),
                pl.BlockSpec((image_len, head_dim), lambda h, i, t: (0, 1)),
            ],
            out_specs=pl.BlockSpec((tile, head_dim), lambda h, i, t: (row_block(i, t), h)),
        ),
        compiler_params=pltpu.CompilerParams(
            dimension_semantics=("arbitrary", "arbitrary"),
            vmem_limit_bytes=48 * 1024 * 1024,
        ),
        cost_estimate=pl.CostEstimate(
            flops=flops // 2,
            transcendentals=rows * query_heads * image_len // 2,
            bytes_accessed=2 * (rows * width + key_values.size),
        ),
    )(live_tiles, query_rows, key_values, key_values)


def on_device(queries, image_refs, features, kv_weight):
    seq_devices = lax.axis_size("seq")
    token_count = queries.shape[0]
    width_cols = queries.shape[1]
    capacity = 2 * token_count // seq_devices
    rows = seq_devices * capacity
    tile = min(ROW_TILE, rows)
    owners = image_refs[:, 0]
    onehot = (owners[:, None] == jnp.arange(seq_devices, dtype=jnp.int32)[None, :]).astype(
        jnp.int32
    )
    running = jnp.cumsum(onehot, axis=0)
    position = jnp.sum(onehot * (running - 1), axis=1)
    slot_index = owners * capacity + position
    outgoing = (
        jnp.zeros((rows, width_cols), jnp.bfloat16).at[slot_index].set(queries)
    )
    outgoing = outgoing.reshape(seq_devices, capacity, width_cols)
    sent_counts = jnp.sum(onehot, axis=0).reshape(seq_devices, 1)
    counts = lax.all_to_all(sent_counts, "seq", split_axis=0, concat_axis=0, tiled=True)[:, 0]
    ends = jnp.cumsum(counts)
    starts = ends - counts
    total = ends[-1]
    live_tiles = jnp.maximum((total + tile - 1) // tile, 1).astype(jnp.int32).reshape(1)
    packed = jnp.arange(rows, dtype=jnp.int32)
    source = jnp.minimum(
        jnp.sum((ends[None, :] <= packed[:, None]).astype(jnp.int32), axis=1), seq_devices - 1
    )
    packed_slot = jnp.where(packed < total, source * capacity + packed - starts[source], 0)
    slot_source = packed // capacity
    slot_offset = packed % capacity
    slot_packed = jnp.where(
        slot_offset < counts[slot_source], starts[slot_source] + slot_offset, 0
    )

    group = HEADS // KV_HEADS
    image_block = features[0]
    tensor_devices = lax.axis_size("tensor")
    local_kv = KV_HEADS // tensor_devices
    projected = jnp.dot(image_block, kv_weight, preferred_element_type=jnp.float32).astype(
        jnp.bfloat16
    )
    kv_width = 2 * HEAD_DIM
    received = lax.all_to_all(outgoing, "seq", split_axis=0, concat_axis=0, tiled=True)
    packed_rows = received.reshape(-1, width_cols)[packed_slot]
    pieces = []
    for head in range(local_kv):
        key_values = lax.psum_scatter(
            jnp.concatenate(
                [
                    projected[:, (dest * local_kv + head) * kv_width :][:, :kv_width]
                    for dest in range(tensor_devices)
                ],
                axis=1,
            ),
            "tensor",
            scatter_dimension=1,
            tiled=True,
        )
        answered = attend(packed_rows, key_values, group, HEAD_DIM, head * group, live_tiles, tile)
        answered = answered[slot_packed].reshape(seq_devices, capacity, -1)
        returned = lax.all_to_all(answered, "seq", split_axis=0, concat_axis=0, tiled=True)
        pieces.append(returned.reshape(rows, -1)[slot_index])
    return jnp.concatenate(pieces, axis=1)


def solution(mesh):
    placed = (P("seq", "tensor"), P("seq", None), P("seq", None, "tensor"), P("tensor", None))
    return jax.shard_map(
        on_device, mesh=mesh, in_specs=placed, out_specs=P("seq", "tensor"), check_vma=False
    )
```

time: 250 us -> 246 us (0.984)
  Pallas kernels: 90.2 us -> 51 us
  waiting for transfers between devices: 87.7 us -> 58.6 us
  starting transfers between devices: 13.4 us -> 39.1 us
  local copies, waits for them, and re-layouts: 19 us -> 42.4 us
  other arithmetic: 7.73 us -> 21.1 us
    reduce_scatter x2, waiting for transfers between devices: 63.1 us -> 2.17 us  [on_device(): lax.psum_scatter(jnp.concatenate([projected[:, (dest * local_kv + head) *...]
    pallas_call x2, Pallas kernels: 90.2 us -> 51 us  [attend(): pl.pallas_call(functools.partial(attend_kernel, scale), out_shape=jax.Sha...]
    all_to_all x1, waiting for transfers between devices: 0.01 us -> 34.4 us  [on_device(): lax.all_to_all(outgoing, 'seq', split_axis=0, concat_axis=0, tiled=True)]
    gather x2 -> x7, local copies, waits for them, and re-layouts: 6.65 us -> 31 us  [the longest x1 11.6 us: on_device(): packed_rows = received.reshape(-1, width_cols)[packed_slot]]
    all_to_all x2, starting transfers between devices: 8.12 us -> 29.2 us  [on_device(): lax.all_to_all(answered, 'seq', split_axis=0, concat_axis=0, tiled=True)]
    gather x1 -> x9, other arithmetic: 0.01 us -> 10.9 us  [the longest x3 5.13 us: on_device(): starts[source]]
    all_to_all x0 -> x1, starting transfers between devices: none -> 5.19 us  [on_device(): lax.all_to_all(sent_counts, 'seq', split_axis=0, concat_axis=0, tiled=True)]
    all_to_all x2, waiting for transfers between devices: 24.5 us -> 22 us  [on_device(): lax.all_to_all(answered, 'seq', split_axis=0, concat_axis=0, tiled=True)]
  transfers between devices with their start and end apart: 5 -> 6, of which waited for: 3 -> 3; matrix products, arithmetic and copies ran while one was open for 6% -> 22% of each run, Pallas kernels for 36% -> 21%
where the time goes in v4:
time: 246 us; the launch traced here: 245 us
  waiting for transfers between devices  58.6 us (24%)
  Pallas kernels  51 us (21%)
  local copies, waits for them, and re-layouts  42.4 us (17%)
  starting transfers between devices  39.1 us (16%)
  other arithmetic  21.1 us (9%)
  matrix products  18 us (7%)
  between operations  14.2 us (6%)
    pallas_call x2, Pallas kernels, attend(): pl.pallas_call(functools.partial(attend_kernel, scale), out_shape=jax.Sha...  51 us
    all_to_all x1, waiting for transfers between devices, on_device(): lax.all_to_all(outgoing, 'seq', split_axis=0, concat_axis=0, tiled=True)  34.4 us
    all_to_all x2, starting transfers between devices, on_device(): lax.all_to_all(answered, 'seq', split_axis=0, concat_axis=0, tiled=True)  29.2 us
    all_to_all x2, waiting for transfers between devices, on_device(): lax.all_to_all(answered, 'seq', split_axis=0, concat_axis=0, tiled=True)  22 us
    dot_general x1, matrix products, on_device(): jnp.dot(image_block, kv_weight, preferred_element_type=jnp.float32)  18 us
    gather x1, local copies, waits for them, and re-layouts, on_device(): packed_rows = received.reshape(-1, width_cols)[packed_slot]  11.6 us
    gather x2, local copies, waits for them, and re-layouts, on_device(): answered = answered[slot_packed].reshape(seq_devices, capacity, -1)  10.7 us
    gather x2, local copies, waits for them, and re-layouts, on_device(): pieces.append(returned.reshape(rows, -1)[slot_index])  7.37 us
  transfers between devices with their start and end apart: 6, of which 3 were waited for; matrix products, arithmetic and copies ran while one was open for 22% of the time, Pallas kernels for 21%

profile of v4, /device:TPU:0, one launch (start us, length us, event | category | flops | bytes accessed | tf_op | source)
XLA Modules:
  0.0 244.5 jit_solution(7919967033321242629)
XLA Ops:
  6.5 0.0 reduce-scatter.3.cloned.1.call-start
  6.5 18.0 %convolution_convert_fusion = bf16[1601,2048]{1,0:T(8,128)(2,1)S(1)} fusion(bf16[2048,2048]{1,0:T(8,128)(2,1)} %param.7, bf16[1,1601,2048]{2,1,0:T(8,128)(2,1)} %param.6), kind=kOutput, calls=%fused_computation.6 | convolution fusion | flops 13433440256 | bytes 21504000 | tf_op jit(solution)/shard_map/dot_general | solution.py:110
  24.5 0.4 fusion.5
  24.9 2.5 %pad_maximum_fusion = bf16[1601,1024]{1,0:T(8,128)(2,1)} fusion(bf16[1601,256]{1,0:T(8,128)(2,1)S(1)} %get-tuple-element.12, bf16[1601,256]{1,0:T(8,128)(2,1)S(1)} %get-tuple-element.13, bf16[1601,256]{1,0:T(8,128)(2,1)S(1)} %get-tuple-element.14, bf16[1601,256]{1,0:T(8,128)(2,1)S(1)} %get-tuple-element.7), kind=kLoop, calls=%fused_computation.8 | loop fusion | flops 13115392 | bytes 6557696 | tf_op jit(solution)/shard_map/concatenate | solution.py:119
  27.4 0.0 reduce-scatter.3.cloned.1.call-update
  27.4 0.0 reduce-scatter.5.cloned.1.call-start
  27.5 0.0 copy-start.2
  27.5 2.5 %pad_maximum_fusion.1 = bf16[1601,1024]{1,0:T(8,128)(2,1)} fusion(bf16[1601,256]{1,0:T(8,128)(2,1)S(1)} %get-tuple-element.8, bf16[1601,256]{1,0:T(8,128)(2,1)S(1)} %get-tuple-element.9, bf16[1601,256]{1,0:T(8,128)(2,1)S(1)} %get-tuple-element.10, bf16[1601,256]{1,0:T(8,128)(2,1)S(1)} %get-tuple-element.11), kind=kLoop, calls=%fused_computation.9 | loop fusion | flops 13115392 | bytes 6557696 | tf_op jit(solution)/shard_map/concatenate | solution.py:119
  30.0 0.0 reduce-scatter.5.cloned.1.call-update
  30.0 0.0 copy-done.2
  30.0 1.1 reduce-window.11
  31.2 0.2 slice_reduce_fusion
  31.4 0.1 fusion.3
  31.6 0.7 copy.7
  32.3 5.2 %all-to-all-start = ((s32[8,1,1]{2,1,0:T(1,128)}), s32[8,1,1]{2,1,0:T(1,128)S(1)}, u32[]{:S(2)}, u32[]{:S(2)}) async-start(s32[8,1,1]{2,1,0:T(1,128)} %copy.7), calls=%async_computation | async-start | bytes 8192 | tf_op jit(solution)/shard_map/all_to_all | solution.py:90
  37.5 7.3 %scatter_custom_fusion = bf16[1024,2048]{1,0:T(8,128)(2,1)} fusion(s32[512]{0:T(512)S(1)} %bitcast.69, bf16[512,2048]{1,0:T(8,128)(2,1)} %param.4, bf16[]{:T(256)} %constant.63.clone.1), kind=kCustom, calls=%fused_computation.11 | custom fusion | bytes 4194816 | tf_op jit(solution)/shard_map/scatter | solution.py:86
  44.7 0.0 all-to-all-done
  44.7 4.7 %all-to-all-start.1 = ((bf16[8,128,2048]{2,1,0:T(8,128)(2,1)}), bf16[8,128,2048]{2,1,0:T(8,128)(2,1)}, u32[]{:S(2)}, u32[]{:S(2)}) async-start(bf16[8,128,2048]{2,1,0:T(8,128)(2,1)} %bitcast.53), calls=%async_computation.1 | async-start | bytes 8388608 | tf_op jit(solution)/shard_map/all_to_all | solution.py:114
  49.5 0.2 reduce
  49.7 0.2 reduce-window.10
  49.9 0.6 slice.46
  51.2 0.6 fusion.6
  51.8 4.4 %compare_select_fusion.13 = s32[1024,1]{0,1:T(1,128)S(1)} fusion(s32[]{:T(128)} %bitcast.26, s32[]{:T(128)} %bitcast.27, s32[]{:T(128)} %bitcast.28, s32[]{:T(128)} %bitcast.29, s32[]{:T(128)} %bitcast.30, s32[]{:T(128)} %bitcast.32, s32[]{:T(128)} %bitcast.31), kind=kLoop, calls=%fused_computation.39 | loop fusion | flops 23552 | bytes 4124 | tf_op jit(solution)/shard_map/gather | solution.py:103
  56.2 0.7 fusion.7
  56.9 0.1 convert_reduce_fusion
  57.0 4.4 %compare_select_fusion.4 = (s32[1024,1]{0,1:T(1,128)S(1)}, s32[1024,1]{0,1:T(1,128)S(1)}) fusion(s32[]{:T(128)} %bitcast.14, s32[]{:T(128)} %bitcast.15, s32[]{:T(128)} %bitcast.16, s32[]{:T(128)} %bitcast.17, s32[]{:T(128)} %bitcast.18, s32[]{:T(128)} %bitcast.20, s32[]{:T(128)} %bitcast.19, s32[1024,1]{0,1:T(1,128)S(1)} %bitcast.57), kind=kLoop, calls=%fused_computation.28 | loop fusion | flops 38912 | bytes 12316 | tf_op jit(solution)/shard_map/gather | solution.py:99
  61.4 0.7 broadcast_select_fusion.2
  62.1 0.7 compare_select_fusion.2
  62.8 1.3 broadcast_select_fusion.1
  64.2 34.4 %all-to-all-done.1 = bf16[8,128,2048]{2,1,0:T(8,128)(2,1)} async-done(((bf16[8,128,2048]{2,1,0:T(8,128)(2,1)}), bf16[8,128,2048]{2,1,0:T(8,128)(2,1)}, u32[]{:S(2)}, u32[]{:S(2)}) %all-to-all-start.1) | async-done | bytes 4194336 | tf_op jit(solution)/shard_map/all_to_all | solution.py:114
  98.6 11.6 %gather_fusion = bf16[1024,2048]{1,0:T(8,128)(2,1)} fusion(bf16[1024,2048]{1,0:T(8,128)(2,1)} %bitcast.10, s32[1024]{0:T(1024)S(1)} %broadcast_clamp_fusion.1), kind=kCustom, calls=%fused_computation | custom fusion | bytes 8392704 | tf_op jit(solution)/shard_map/gather | solution.py:115
  110.1 0.0 reduce-scatter.3.cloned.1.call-done.k_ref.v_ref
  110.1 0.0 copy-start
  110.1 1.1 copy-done
  111.3 25.5 %shard_map.46 = bf16[1024,1024]{1,0:T(8,128)(2,1)S(1)} custom-call(s32[1]{0:T(128)} %bitcast.3.tiles_ref, bf16[1024,2048]{1,0:T(8,128)(2,1)} %gather_fusion, bf16[1601,256]{1,0:T(8,128)(2,1)S(1)} %copy-done, bf16[1601,256]{1,0:T(8,128)(2,1)S(1)} %copy-done), custom_call_target="tpu_custom_call" | custom-call | flops 3357540352 | bytes 2916864 | tf_op jit(solution)/shard_map/pallas_call | solution.py:46
  136.8 5.4 %gather_fusion.1 = bf16[1024,1024]{1,0:T(8,128)(2,1)} fusion(bf16[1024,1024]{1,0:T(8,128)(2,1)S(1)} %shard_map.46, s32[1024]{0:T(1024)S(1)} %broadcast_clamp_fusion), kind=kCustom, calls=%fused_computation.1 | custom fusion | bytes 4198400 | tf_op jit(solution)/shard_map/gather | solution.py:131
  142.2 14.1 %all-to-all-start.2 = ((bf16[8,128,1024]{2,1,0:T(8,128)(2,1)}), bf16[8,128,1024]{2,1,0:T(8,128)(2,1)}, u32[]{:S(2)}, u32[]{:S(2)}) async-start(bf16[8,128,1024]{2,1,0:T(8,128)(2,1)} %bitcast.54), calls=%async_computation.3 | async-start | bytes 4194304 | tf_op jit(solution)/shard_map/all_to_all | solution.py:132
  156.2 2.2 reduce-scatter.5.cloned.1.call-done.k_ref.v_ref
  158.4 0.0 copy-start.1
  158.4 1.1 copy-done.1
  159.6 25.6 %shard_map.47 = bf16[1024,1024]{1,0:T(8,128)(2,1)S(1)} custom-call(s32[1]{0:T(128)} %bitcast.3.tiles_ref, bf16[1024,2048]{1,0:T(8,128)(2,1)} %gather_fusion, bf16[1601,256]{1,0:T(8,128)(2,1)S(1)} %copy-done.1, bf16[1601,256]{1,0:T(8,128)(2,1)S(1)} %copy-done.1), custom_call_target="tpu_custom_call" | custom-call | flops 3357540352 | bytes 2916864 | tf_op jit(solution)/shard_map/pallas_call | solution.py:46
  185.1 5.3 %gather_fusion.3 = bf16[1024,1024]{1,0:T(8,128)(2,1)} fusion(bf16[1024,1024]{1,0:T(8,128)(2,1)S(1)} %shard_map.47, s32[1024]{0:T(1024)S(1)} %broadcast_clamp_fusion), kind=kCustom, calls=%fused_computation.3 | custom fusion | bytes 4198400 | tf_op jit(solution)/shard_map/gather | solution.py:131
  190.5 0.0 all-to-all-done.2
  190.5 15.1 %all-to-all-start.3 = ((bf16[8,128,1024]{2,1,0:T(8,128)(2,1)}), bf16[8,128,1024]{2,1,0:T(8,128)(2,1)S(1)}, u32[]{:S(2)}, u32[]{:S(2)}) async-start(bf16[8,128,1024]{2,1,0:T(8,128)(2,1)} %bitcast.55), calls=%async_computation.5 | async-start | bytes 4194304 | tf_op jit(solution)/shard_map/all_to_all | solution.py:132
  205.5 4.6 %gather_fusion.2 = bf16[512,1024]{1,0:T(8,128)(2,1)S(1)} fusion(bf16[1024,1024]{1,0:T(8,128)(2,1)} %bitcast.39, s32[1024]{0:T(1024)S(1)} %pad_clamp_fusion), kind=kCustom, calls=%fused_computation.2 | custom fusion | bytes 2099200 | tf_op jit(solution)/shard_map/gather | solution.py:133
  210.1 22.0 %all-to-all-done.3 = bf16[8,128,1024]{2,1,0:T(8,128)(2,1)S(1)} async-done(((bf16[8,128,1024]{2,1,0:T(8,128)(2,1)}), bf16[8,128,1024]{2,1,0:T(8,128)(2,1)S(1)}, u32[]{:S(2)}, u32[]{:S(2)}) %all-to-all-start.3) | async-done | bytes 2097184 | tf_op jit(solution)/shard_map/all_to_all | solution.py:132
  232.1 2.8 %gather_fusion.4 = bf16[512,1024]{1,0:T(8,128)(2,1)} fusion(bf16[1024,1024]{1,0:T(8,128)(2,1)S(1)} %bitcast.52, s32[1024]{0:T(1024)S(1)} %pad_clamp_fusion), kind=kCustom, calls=%fused_computation.4 | custom fusion | bytes 2099200 | tf_op jit(solution)/shard_map/gather | solution.py:133
  234.9 2.8 %pad_maximum_fusion.2 = bf16[512,2048]{1,0:T(8,128)(2,1)} fusion(bf16[512,1024]{1,0:T(8,128)(2,1)} %gather_fusion.4, bf16[512,1024]{1,0:T(8,128)(2,1)S(1)} %gather_fusion.2), kind=kLoop, calls=%fused_computation.10 | loop fusion | flops 4194304 | bytes 4194304 | tf_op jit(solution)/shard_map/concatenate | solution.py:134
  (12 shorter events, 0.1 us)
Async XLA Ops:
  6.5 103.6 %reduce-scatter.3.cloned.1.call-start = ((), (), s32[]{:S(2)}) async-start(), calls=%async_computation.6 | async-start | bytes 4116480 | tf_op jit(solution)/shard_map/reduce_scatter | solution.py:118
  27.4 131.0 %reduce-scatter.5.cloned.1.call-start = ((), (), s32[]{:S(2)}) async-start(), calls=%async_computation.7 | async-start | bytes 4116480 | tf_op jit(solution)/shard_map/reduce_scatter | solution.py:118
  27.5 2.5 %copy-start.2 = (s32[512,1]{0,1:T(1,128)S(1)}, s32[512,1]{0,1:T(1,128)}, u32[]{:S(2)}) copy-start(s32[512,1]{0,1:T(1,128)} %param.5) | copy-start | bytes 6148
  32.3 12.5 %all-to-all-start = ((s32[8,1,1]{2,1,0:T(1,128)}), s32[8,1,1]{2,1,0:T(1,128)S(1)}, u32[]{:S(2)}, u32[]{:S(2)}) async-start(s32[8,1,1]{2,1,0:T(1,128)} %copy.7), calls=%async_computation | async-start | bytes 8192 | tf_op jit(solution)/shard_map/all_to_all | solution.py:90
  44.7 53.9 %all-to-all-start.1 = ((bf16[8,128,2048]{2,1,0:T(8,128)(2,1)}), bf16[8,128,2048]{2,1,0:T(8,128)(2,1)}, u32[]{:S(2)}, u32[]{:S(2)}) async-start(bf16[8,128,2048]{2,1,0:T(8,128)(2,1)} %bitcast.53), calls=%async_computation.1 | async-start | bytes 8388608 | tf_op jit(solution)/shard_map/all_to_all | solution.py:114
  110.1 1.1 copy-start
  142.2 48.3 %all-to-all-start.2 = ((bf16[8,128,1024]{2,1,0:T(8,128)(2,1)}), bf16[8,128,1024]{2,1,0:T(8,128)(2,1)}, u32[]{:S(2)}, u32[]{:S(2)}) async-start(bf16[8,128,1024]{2,1,0:T(8,128)(2,1)} %bitcast.54), calls=%async_computation.3 | async-start | bytes 4194304 | tf_op jit(solution)/shard_map/all_to_all | solution.py:132
  158.4 1.1 copy-start.1
  190.5 41.7 %all-to-all-start.3 = ((bf16[8,128,1024]{2,1,0:T(8,128)(2,1)}), bf16[8,128,1024]{2,1,0:T(8,128)(2,1)S(1)}, u32[]{:S(2)}, u32[]{:S(2)}) async-start(bf16[8,128,1024]{2,1,0:T(8,128)(2,1)} %bitcast.55), calls=%async_computation.5 | async-start | bytes 4194304 | tf_op jit(solution)/shard_map/all_to_all | solution.py:132
Sparse Core Ops, SparseCore 0:
  27.6 65.5 reduce-scatter.2
  95.5 62.8 reduce-scatter.4

commit v5 on v4

--- a/solution.py
+++ b/solution.py
@@ -13,56 +13,61 @@
 ROW_TILE = 256
 
 
-def attend_kernel(scale, tiles_ref, q_ref, k_ref, v_ref, o_ref):
-    @pl.when(pl.program_id(1) < tiles_ref[0])
+def attend_kernel(scale, group, head_dim, tiles_ref, q_ref, k_ref, v_ref, o_ref):
+    @pl.when(pl.program_id(0) < tiles_ref[0])
     def _():
-        q = q_ref[...]
-        scores = (
-            lax.dot_general(
-                q, k_ref[...], (((1,), (1,)), ((), ())), preferred_element_type=jnp.float32
+        keys = k_ref[...]
+        values = v_ref[...]
+        for head in range(group):
+            columns = slice(head * head_dim, (head + 1) * head_dim)
+            scores = (
+                lax.dot_general(
+                    q_ref[:, columns],
+                    keys,
+                    (((1,), (1,)), ((), ())),
+                    preferred_element_type=jnp.float32,
+                )
+                * scale
             )
-            * scale
-        )
-        row_max = jnp.max(scores, axis=1, keepdims=True)
-        weights_exp = jnp.exp(scores - row_max)
-        totals = jnp.sum(weights_exp, axis=1, keepdims=True)
-        probs = weights_exp.astype(jnp.bfloat16)
-        weighted = jnp.dot(probs, v_ref[...], preferred_element_type=jnp.float32)
-        o_ref[...] = (weighted / totals).astype(o_ref.dtype)
+            row_max = jnp.max(scores, axis=1, keepdims=True)
+            weights_exp = jnp.exp(scores - row_max)
+            totals = jnp.sum(weights_exp, axis=1, keepdims=True)
+            probs = weights_exp.astype(jnp.bfloat16)
+            weighted = jnp.dot(probs, values, preferred_element_type=jnp.float32)
+            o_ref[:, columns] = (weighted / totals).astype(o_ref.dtype)
 
 
 def attend(query_rows, key_values, group, head_dim, first_head, live_tiles, tile):
     rows = query_rows.shape[0]
-    query_heads = group
     width = group * head_dim
     image_len = key_values.shape[0]
-    assert rows % tile == 0
+    assert rows % tile == 0 and first_head % group == 0
     scale = head_dim ** (-0.5)
-    flops = 4 * rows * query_heads * image_len * head_dim
+    flops = 4 * rows * group * image_len * head_dim
 
     def row_block(i, tiles):
         return jnp.minimum(i, tiles[0] - 1)
 
     return pl.pallas_call(
-        functools.partial(attend_kernel, scale),
+        functools.partial(attend_kernel, scale, group, head_dim),
         out_shape=jax.ShapeDtypeStruct((rows, width), jnp.bfloat16),
         grid_spec=pltpu.PrefetchScalarGridSpec(
             num_scalar_prefetch=1,
-            grid=(query_heads, rows // tile),
+            grid=(rows // tile,),
             in_specs=[
-                pl.BlockSpec((tile, head_dim), lambda h, i, t: (row_block(i, t), first_head + h)),
-                pl.BlockSpec((image_len, head_dim), lambda h, i, t: (0, 0)),
-                pl.BlockSpec((image_len, head_dim), lambda h, i, t: (0, 1)),
+                pl.BlockSpec((tile, width), lambda i, t: (row_block(i, t), first_head // group)),
+                pl.BlockSpec((image_len, head_dim), lambda i, t: (0, 0)),
+                pl.BlockSpec((image_len, head_dim), lambda i, t: (0, 1)),
             ],
-            out_specs=pl.BlockSpec((tile, head_dim), lambda h, i, t: (row_block(i, t), h)),
+            out_specs=pl.BlockSpec((tile, width), lambda i, t: (row_block(i, t), 0)),
         ),
         compiler_params=pltpu.CompilerParams(
-            dimension_semantics=("arbitrary", "arbitrary"),
+            dimension_semantics=("arbitrary",),
             vmem_limit_bytes=48 * 1024 * 1024,
         ),
         cost_estimate=pl.CostEstimate(
             flops=flops // 2,
-            transcendentals=rows * query_heads * image_len // 2,
+            transcendentals=rows * group * image_len // 2,
             bytes_accessed=2 * (rows * width + key_values.size),
         ),
     )(live_tiles, query_rows, key_values, key_values)

time: 246 us -> 234 us (0.951)
  Pallas kernels: 51 us -> 27.7 us
  waiting for transfers between devices: 58.6 us -> 70.3 us
    pallas_call x2, Pallas kernels: 51 us -> 27.7 us  [attend(): pl.pallas_call(functools.partial(attend_kernel, scale, group, head_dim),...]
    reduce_scatter x2, waiting for transfers between devices: 2.17 us -> 13.8 us  [on_device(): lax.psum_scatter(jnp.concatenate([projected[:, (dest * local_kv + head) *...]
  transfers between devices with their start and end apart: 6 -> 6, of which waited for: 3 -> 3; matrix products, arithmetic and copies ran while one was open for 22% -> 23% of each run, Pallas kernels for 21% -> 12%
where the time goes in v5:
time: 234 us; the launch traced here: 232 us
  waiting for transfers between devices  70.3 us (30%)
  local copies, waits for them, and re-layouts  42.4 us (18%)
  starting transfers between devices  38.5 us (16%)
  Pallas kernels  27.7 us (12%)
  other arithmetic  21.1 us (9%)
  matrix products  18 us (8%)
  between operations  14.2 us (6%)
    all_to_all x1, waiting for transfers between devices, on_device(): lax.all_to_all(outgoing, 'seq', split_axis=0, concat_axis=0, tiled=True)  34.4 us
    all_to_all x2, starting transfers between devices, on_device(): lax.all_to_all(answered, 'seq', split_axis=0, concat_axis=0, tiled=True)  28.5 us
    pallas_call x2, Pallas kernels, attend(): pl.pallas_call(functools.partial(attend_kernel, scale, group, head_dim),...  27.7 us
    all_to_all x2, waiting for transfers between devices, on_device(): lax.all_to_all(answered, 'seq', split_axis=0, concat_axis=0, tiled=True)  22 us
    dot_general x1, matrix products, on_device(): jnp.dot(image_block, kv_weight, preferred_element_type=jnp.float32)  18 us
    reduce_scatter x2, waiting for transfers between devices, on_device(): lax.psum_scatter(jnp.concatenate([projected[:, (dest * local_kv + head) *...  13.8 us
    gather x1, local copies, waits for them, and re-layouts, on_device(): packed_rows = received.reshape(-1, width_cols)[packed_slot]  11.6 us
    gather x2, local copies, waits for them, and re-layouts, on_device(): answered = answered[slot_packed].reshape(seq_devices, capacity, -1)  10.7 us
  transfers between devices with their start and end apart: 6, of which 3 were waited for; matrix products, arithmetic and copies ran while one was open for 23% of the time, Pallas kernels for 12%

profile of v5, /device:TPU:0, one launch (start us, length us, event | category | flops | bytes accessed | tf_op | source)
XLA Modules:
  0.0 232.2 jit_solution(7533425008718541490)
XLA Ops:
  6.5 0.0 reduce-scatter.3.cloned.1.call-start
  6.5 18.0 %convolution_convert_fusion = bf16[1601,2048]{1,0:T(8,128)(2,1)S(1)} fusion(bf16[2048,2048]{1,0:T(8,128)(2,1)} %param.7, bf16[1,1601,2048]{2,1,0:T(8,128)(2,1)} %param.6), kind=kOutput, calls=%fused_computation.6 | convolution fusion | flops 13433440256 | bytes 21504000 | tf_op jit(solution)/shard_map/dot_general | solution.py:115
  24.5 0.4 fusion.5
  24.9 2.5 %pad_maximum_fusion = bf16[1601,1024]{1,0:T(8,128)(2,1)} fusion(bf16[1601,256]{1,0:T(8,128)(2,1)S(1)} %get-tuple-element.12, bf16[1601,256]{1,0:T(8,128)(2,1)S(1)} %get-tuple-element.13, bf16[1601,256]{1,0:T(8,128)(2,1)S(1)} %get-tuple-element.14, bf16[1601,256]{1,0:T(8,128)(2,1)S(1)} %get-tuple-element.7), kind=kLoop, calls=%fused_computation.8 | loop fusion | flops 13115392 | bytes 6557696 | tf_op jit(solution)/shard_map/concatenate | solution.py:124
  27.4 0.0 reduce-scatter.3.cloned.1.call-update
  27.4 0.0 reduce-scatter.5.cloned.1.call-start
  27.5 0.0 copy-start.2
  27.5 2.5 %pad_maximum_fusion.1 = bf16[1601,1024]{1,0:T(8,128)(2,1)} fusion(bf16[1601,256]{1,0:T(8,128)(2,1)S(1)} %get-tuple-element.8, bf16[1601,256]{1,0:T(8,128)(2,1)S(1)} %get-tuple-element.9, bf16[1601,256]{1,0:T(8,128)(2,1)S(1)} %get-tuple-element.10, bf16[1601,256]{1,0:T(8,128)(2,1)S(1)} %get-tuple-element.11), kind=kLoop, calls=%fused_computation.9 | loop fusion | flops 13115392 | bytes 6557696 | tf_op jit(solution)/shard_map/concatenate | solution.py:124
  30.0 0.0 reduce-scatter.5.cloned.1.call-update
  30.0 0.0 copy-done.2
  30.0 1.1 reduce-window.11
  31.2 0.2 slice_reduce_fusion
  31.4 0.1 fusion.3
  31.6 0.7 copy.7
  32.3 5.2 %all-to-all-start = ((s32[8,1,1]{2,1,0:T(1,128)}), s32[8,1,1]{2,1,0:T(1,128)S(1)}, u32[]{:S(2)}, u32[]{:S(2)}) async-start(s32[8,1,1]{2,1,0:T(1,128)} %copy.7), calls=%async_computation | async-start | bytes 8192 | tf_op jit(solution)/shard_map/all_to_all | solution.py:95
  37.5 7.3 %scatter_custom_fusion = bf16[1024,2048]{1,0:T(8,128)(2,1)} fusion(s32[512]{0:T(512)S(1)} %bitcast.69, bf16[512,2048]{1,0:T(8,128)(2,1)} %param.4, bf16[]{:T(256)} %constant.63.clone.1), kind=kCustom, calls=%fused_computation.11 | custom fusion | bytes 4194816 | tf_op jit(solution)/shard_map/scatter | solution.py:91
  44.7 0.0 all-to-all-done
  44.7 4.7 %all-to-all-start.1 = ((bf16[8,128,2048]{2,1,0:T(8,128)(2,1)}), bf16[8,128,2048]{2,1,0:T(8,128)(2,1)}, u32[]{:S(2)}, u32[]{:S(2)}) async-start(bf16[8,128,2048]{2,1,0:T(8,128)(2,1)} %bitcast.53), calls=%async_computation.1 | async-start | bytes 8388608 | tf_op jit(solution)/shard_map/all_to_all | solution.py:119
  49.5 0.2 reduce
  49.7 0.2 reduce-window.10
  49.9 0.6 slice.46
  51.2 0.6 fusion.6
  51.8 4.4 %compare_select_fusion.13 = s32[1024,1]{0,1:T(1,128)S(1)} fusion(s32[]{:T(128)} %bitcast.26, s32[]{:T(128)} %bitcast.27, s32[]{:T(128)} %bitcast.28, s32[]{:T(128)} %bitcast.29, s32[]{:T(128)} %bitcast.30, s32[]{:T(128)} %bitcast.32, s32[]{:T(128)} %bitcast.31), kind=kLoop, calls=%fused_computation.39 | loop fusion | flops 23552 | bytes 4124 | tf_op jit(solution)/shard_map/gather | solution.py:108
  56.2 0.7 fusion.7
  56.9 0.1 convert_reduce_fusion
  57.0 4.4 %compare_select_fusion.4 = (s32[1024,1]{0,1:T(1,128)S(1)}, s32[1024,1]{0,1:T(1,128)S(1)}) fusion(s32[]{:T(128)} %bitcast.14, s32[]{:T(128)} %bitcast.15, s32[]{:T(128)} %bitcast.16, s32[]{:T(128)} %bitcast.17, s32[]{:T(128)} %bitcast.18, s32[]{:T(128)} %bitcast.20, s32[]{:T(128)} %bitcast.19, s32[1024,1]{0,1:T(1,128)S(1)} %bitcast.57), kind=kLoop, calls=%fused_computation.28 | loop fusion | flops 38912 | bytes 12316 | tf_op jit(solution)/shard_map/gather | solution.py:104
  61.4 0.7 broadcast_select_fusion.2
  62.1 0.7 compare_select_fusion.2
  62.8 1.3 broadcast_select_fusion.1
  64.2 34.4 %all-to-all-done.1 = bf16[8,128,2048]{2,1,0:T(8,128)(2,1)} async-done(((bf16[8,128,2048]{2,1,0:T(8,128)(2,1)}), bf16[8,128,2048]{2,1,0:T(8,128)(2,1)}, u32[]{:S(2)}, u32[]{:S(2)}) %all-to-all-start.1) | async-done | bytes 4194336 | tf_op jit(solution)/shard_map/all_to_all | solution.py:119
  98.6 11.6 %gather_fusion = bf16[1024,2048]{1,0:T(8,128)(2,1)} fusion(bf16[1024,2048]{1,0:T(8,128)(2,1)} %bitcast.10, s32[1024]{0:T(1024)S(1)} %broadcast_clamp_fusion.1), kind=kCustom, calls=%fused_computation | custom fusion | bytes 8392704 | tf_op jit(solution)/shard_map/gather | solution.py:120
  110.1 0.0 reduce-scatter.3.cloned.1.call-done.k_ref.v_ref
  110.1 0.0 copy-start
  110.1 1.1 copy-done
  111.3 13.8 %shard_map.46 = bf16[1024,1024]{1,0:T(8,128)(2,1)S(1)} custom-call(s32[1]{0:T(128)} %bitcast.3.tiles_ref, bf16[1024,2048]{1,0:T(8,128)(2,1)} %gather_fusion, bf16[1601,256]{1,0:T(8,128)(2,1)S(1)} %copy-done, bf16[1601,256]{1,0:T(8,128)(2,1)S(1)} %copy-done), custom_call_target="tpu_custom_call" | custom-call | flops 3357540352 | bytes 2916864 | tf_op jit(solution)/shard_map/pallas_call | solution.py:51
  125.1 5.4 %gather_fusion.1 = bf16[1024,1024]{1,0:T(8,128)(2,1)} fusion(bf16[1024,1024]{1,0:T(8,128)(2,1)S(1)} %shard_map.46, s32[1024]{0:T(1024)S(1)} %broadcast_clamp_fusion), kind=kCustom, calls=%fused_computation.1 | custom fusion | bytes 4198400 | tf_op jit(solution)/shard_map/gather | solution.py:136
  130.5 14.0 %all-to-all-start.2 = ((bf16[8,128,1024]{2,1,0:T(8,128)(2,1)}), bf16[8,128,1024]{2,1,0:T(8,128)(2,1)}, u32[]{:S(2)}, u32[]{:S(2)}) async-start(bf16[8,128,1024]{2,1,0:T(8,128)(2,1)} %bitcast.54), calls=%async_computation.3 | async-start | bytes 4194304 | tf_op jit(solution)/shard_map/all_to_all | solution.py:137
  144.6 13.8 %reduce-scatter.5.cloned.1.call-done.k_ref.v_ref = bf16[1601,256]{1,0:T(8,128)(2,1)} async-done(((bf16[1601,1024]{1,0:T(8,128)(2,1)}), bf16[1601,256]{1,0:T(8,128)(2,1)}) %reduce-scatter.5.cloned.1.call-update) | async-done | bytes 819728 | tf_op jit(solution)/shard_map/reduce_scatter | solution.py:123
  158.4 0.0 copy-start.1
  158.4 1.1 copy-done.1
  159.6 13.8 %shard_map.47 = bf16[1024,1024]{1,0:T(8,128)(2,1)S(1)} custom-call(s32[1]{0:T(128)} %bitcast.3.tiles_ref, bf16[1024,2048]{1,0:T(8,128)(2,1)} %gather_fusion, bf16[1601,256]{1,0:T(8,128)(2,1)S(1)} %copy-done.1, bf16[1601,256]{1,0:T(8,128)(2,1)S(1)} %copy-done.1), custom_call_target="tpu_custom_call" | custom-call | flops 3357540352 | bytes 2916864 | tf_op jit(solution)/shard_map/pallas_call | solution.py:51
  173.4 5.3 %gather_fusion.3 = bf16[1024,1024]{1,0:T(8,128)(2,1)} fusion(bf16[1024,1024]{1,0:T(8,128)(2,1)S(1)} %shard_map.47, s32[1024]{0:T(1024)S(1)} %broadcast_clamp_fusion), kind=kCustom, calls=%fused_computation.3 | custom fusion | bytes 4198400 | tf_op jit(solution)/shard_map/gather | solution.py:136
  178.7 0.0 all-to-all-done.2
  178.7 14.5 %all-to-all-start.3 = ((bf16[8,128,1024]{2,1,0:T(8,128)(2,1)}), bf16[8,128,1024]{2,1,0:T(8,128)(2,1)S(1)}, u32[]{:S(2)}, u32[]{:S(2)}) async-start(bf16[8,128,1024]{2,1,0:T(8,128)(2,1)} %bitcast.55), calls=%async_computation.5 | async-start | bytes 4194304 | tf_op jit(solution)/shard_map/all_to_all | solution.py:137
  193.2 4.6 %gather_fusion.2 = bf16[512,1024]{1,0:T(8,128)(2,1)S(1)} fusion(bf16[1024,1024]{1,0:T(8,128)(2,1)} %bitcast.39, s32[1024]{0:T(1024)S(1)} %pad_clamp_fusion), kind=kCustom, calls=%fused_computation.2 | custom fusion | bytes 2099200 | tf_op jit(solution)/shard_map/gather | solution.py:138
  197.8 22.0 %all-to-all-done.3 = bf16[8,128,1024]{2,1,0:T(8,128)(2,1)S(1)} async-done(((bf16[8,128,1024]{2,1,0:T(8,128)(2,1)}), bf16[8,128,1024]{2,1,0:T(8,128)(2,1)S(1)}, u32[]{:S(2)}, u32[]{:S(2)}) %all-to-all-start.3) | async-done | bytes 2097184 | tf_op jit(solution)/shard_map/all_to_all | solution.py:137
  219.8 2.8 %gather_fusion.4 = bf16[512,1024]{1,0:T(8,128)(2,1)} fusion(bf16[1024,1024]{1,0:T(8,128)(2,1)S(1)} %bitcast.52, s32[1024]{0:T(1024)S(1)} %pad_clamp_fusion), kind=kCustom, calls=%fused_computation.4 | custom fusion | bytes 2099200 | tf_op jit(solution)/shard_map/gather | solution.py:138
  222.6 2.8 %pad_maximum_fusion.2 = bf16[512,2048]{1,0:T(8,128)(2,1)} fusion(bf16[512,1024]{1,0:T(8,128)(2,1)} %gather_fusion.4, bf16[512,1024]{1,0:T(8,128)(2,1)S(1)} %gather_fusion.2), kind=kLoop, calls=%fused_computation.10 | loop fusion | flops 4194304 | bytes 4194304 | tf_op jit(solution)/shard_map/concatenate | solution.py:139
  (12 shorter events, 0.1 us)
Async XLA Ops:
  6.5 103.6 %reduce-scatter.3.cloned.1.call-start = ((), (), s32[]{:S(2)}) async-start(), calls=%async_computation.6 | async-start | bytes 4116480 | tf_op jit(solution)/shard_map/reduce_scatter | solution.py:123
  27.4 131.0 %reduce-scatter.5.cloned.1.call-start = ((), (), s32[]{:S(2)}) async-start(), calls=%async_computation.7 | async-start | bytes 4116480 | tf_op jit(solution)/shard_map/reduce_scatter | solution.py:123
  27.5 2.5 %copy-start.2 = (s32[512,1]{0,1:T(1,128)S(1)}, s32[512,1]{0,1:T(1,128)}, u32[]{:S(2)}) copy-start(s32[512,1]{0,1:T(1,128)} %param.5) | copy-start | bytes 6148
  32.3 12.5 %all-to-all-start = ((s32[8,1,1]{2,1,0:T(1,128)}), s32[8,1,1]{2,1,0:T(1,128)S(1)}, u32[]{:S(2)}, u32[]{:S(2)}) async-start(s32[8,1,1]{2,1,0:T(1,128)} %copy.7), calls=%async_computation | async-start | bytes 8192 | tf_op jit(solution)/shard_map/all_to_all | solution.py:95
  44.7 53.9 %all-to-all-start.1 = ((bf16[8,128,2048]{2,1,0:T(8,128)(2,1)}), bf16[8,128,2048]{2,1,0:T(8,128)(2,1)}, u32[]{:S(2)}, u32[]{:S(2)}) async-start(bf16[8,128,2048]{2,1,0:T(8,128)(2,1)} %bitcast.53), calls=%async_computation.1 | async-start | bytes 8388608 | tf_op jit(solution)/shard_map/all_to_all | solution.py:119
  110.1 1.1 copy-start
  130.5 48.2 %all-to-all-start.2 = ((bf16[8,128,1024]{2,1,0:T(8,128)(2,1)}), bf16[8,128,1024]{2,1,0:T(8,128)(2,1)}, u32[]{:S(2)}, u32[]{:S(2)}) async-start(bf16[8,128,1024]{2,1,0:T(8,128)(2,1)} %bitcast.54), calls=%async_computation.3 | async-start | bytes 4194304 | tf_op jit(solution)/shard_map/all_to_all | solution.py:137
  158.4 1.1 copy-start.1
  178.7 41.1 %all-to-all-start.3 = ((bf16[8,128,1024]{2,1,0:T(8,128)(2,1)}), bf16[8,128,1024]{2,1,0:T(8,128)(2,1)S(1)}, u32[]{:S(2)}, u32[]{:S(2)}) async-start(bf16[8,128,1024]{2,1,0:T(8,128)(2,1)} %bitcast.55), calls=%async_computation.5 | async-start | bytes 4194304 | tf_op jit(solution)/shard_map/all_to_all | solution.py:137
Sparse Core Ops, SparseCore 0:
  27.6 65.5 reduce-scatter.2
  95.5 62.8 reduce-scatter.4

commit v6 on v5

--- a/solution.py
+++ b/solution.py
@@ -18,8 +18,9 @@
     def _():
         keys = k_ref[...]
         values = v_ref[...]
-        for head in range(group):
-            columns = slice(head * head_dim, (head + 1) * head_dim)
+
+        def one_head(head, carry):
+            columns = pl.ds(pl.multiple_of(head * head_dim, head_dim), head_dim)
             scores = (
                 lax.dot_general(
                     q_ref[:, columns],
@@ -35,10 +36,13 @@
             probs = weights_exp.astype(jnp.bfloat16)
             weighted = jnp.dot(probs, values, preferred_element_type=jnp.float32)
             o_ref[:, columns] = (weighted / totals).astype(o_ref.dtype)
+            return carry
+
+        lax.fori_loop(0, group, one_head, 0)
 
 
-def attend(query_rows, key_values, group, head_dim, first_head, live_tiles, tile):
-    rows = query_rows.shape[0]
+def attend(query_rows, key_values, group, head_dim, first_head, live_tiles, tile, pad_rows):
+    rows = query_rows.shape[0] - pad_rows
     width = group * head_dim
     image_len = key_values.shape[0]
     assert rows % tile == 0 and first_head % group == 0
@@ -50,7 +54,7 @@
 
     return pl.pallas_call(
         functools.partial(attend_kernel, scale, group, head_dim),
-        out_shape=jax.ShapeDtypeStruct((rows, width), jnp.bfloat16),
+        out_shape=jax.ShapeDtypeStruct((rows + pad_rows, width), jnp.bfloat16),
         grid_spec=pltpu.PrefetchScalarGridSpec(
             num_scalar_prefetch=1,
             grid=(rows // tile,),
@@ -97,17 +101,6 @@
     starts = ends - counts
     total = ends[-1]
     live_tiles = jnp.maximum((total + tile - 1) // tile, 1).astype(jnp.int32).reshape(1)
-    packed = jnp.arange(rows, dtype=jnp.int32)
-    source = jnp.minimum(
-        jnp.sum((ends[None, :] <= packed[:, None]).astype(jnp.int32), axis=1), seq_devices - 1
-    )
-    packed_slot = jnp.where(packed < total, source * capacity + packed - starts[source], 0)
-    slot_source = packed // capacity
-    slot_offset = packed % capacity
-    slot_packed = jnp.where(
-        slot_offset < counts[slot_source], starts[slot_source] + slot_offset, 0
-    )
-
     group = HEADS // KV_HEADS
     image_block = features[0]
     tensor_devices = lax.axis_size("tensor")
@@ -117,7 +110,9 @@
     )
     kv_width = 2 * HEAD_DIM
     received = lax.all_to_all(outgoing, "seq", split_axis=0, concat_axis=0, tiled=True)
-    packed_rows = received.reshape(-1, width_cols)[packed_slot]
+    packed_rows = jnp.zeros((rows + capacity, width_cols), jnp.bfloat16)
+    for src in range(seq_devices):
+        packed_rows = lax.dynamic_update_slice(packed_rows, received[src], (starts[src], 0))
     pieces = []
     for head in range(local_kv):
         key_values = lax.psum_scatter(
@@ -132,8 +127,15 @@
             scatter_dimension=1,
             tiled=True,
         )
-        answered = attend(packed_rows, key_values, group, HEAD_DIM, head * group, live_tiles, tile)
-        answered = answered[slot_packed].reshape(seq_devices, capacity, -1)
+        answered = attend(
+            packed_rows, key_values, group, HEAD_DIM, head * group, live_tiles, tile, capacity
+        )
+        answered = jnp.stack(
+            [
+                lax.dynamic_slice_in_dim(answered, starts[src], capacity, axis=0)
+                for src in range(seq_devices)
+            ]
+        )
         returned = lax.all_to_all(answered, "seq", split_axis=0, concat_axis=0, tiled=True)
         pieces.append(returned.reshape(rows, -1)[slot_index])
     return jnp.concatenate(pieces, axis=1)

time: 234 us -> 297 us (1.27)
  Pallas kernels: 27.7 us -> 74.8 us
  local copies, waits for them, and re-layouts: 42.4 us -> 68.8 us
  starting transfers between devices: 38.5 us -> 17.9 us
  between operations: 14.2 us -> 29.3 us
  other arithmetic: 21.1 us -> 8.21 us
  waiting for transfers between devices: 70.3 us -> 79.3 us
    pallas_call x2, Pallas kernels: 27.7 us -> 74.8 us  [attend(): pl.pallas_call(functools.partial(attend_kernel, scale, group, head_dim),...]
    dynamic_update_slice x0 -> x8, local copies, waits for them, and re-layouts: none -> 30.7 us  [on_device(): lax.dynamic_update_slice(packed_rows, received[src], (starts[src], 0))]
    all_to_all x2, waiting for transfers between devices: 22 us -> 47.6 us  [on_device(): lax.all_to_all(answered, 'seq', split_axis=0, concat_axis=0, tiled=True)]
    gather x5 -> x0, local copies, waits for them, and re-layouts: 23.6 us -> none  [the longest x1 11.6 us: on_device(): packed_rows = received.reshape(-1, width_cols)[packed_slot]]
    all_to_all x2, starting transfers between devices: 28.5 us -> 7.94 us  [on_device(): lax.all_to_all(answered, 'seq', split_axis=0, concat_axis=0, tiled=True)]
    reduce_scatter x2, waiting for transfers between devices: 13.8 us -> 0.01 us  [on_device(): lax.psum_scatter(jnp.concatenate([projected[:, (dest * local_kv + head) *...]
    gather x8 -> x0, other arithmetic: 10.9 us -> none  [the longest x3 5.13 us: on_device(): starts[source]]
    unnamed x6 -> x23, local copies, waits for them, and re-layouts: 2.3 us -> 12.8 us
  transfers between devices with their start and end apart: 6 -> 6, of which waited for: 3 -> 3; matrix products, arithmetic and copies ran while one was open for 23% -> 20% of each run, Pallas kernels for 12% -> 13%
where the time goes in v6:
time: 297 us; the launch traced here: 296 us
  waiting for transfers between devices  79.3 us (27%)
  Pallas kernels  74.8 us (25%)
  local copies, waits for them, and re-layouts  68.8 us (23%)
  between operations  29.3 us (10%)
  matrix products  18 us (6%)
  starting transfers between devices  17.9 us (6%)
  other arithmetic  8.21 us (3%)
    pallas_call x2, Pallas kernels, attend(): pl.pallas_call(functools.partial(attend_kernel, scale, group, head_dim),...  74.8 us
    all_to_all x2, waiting for transfers between devices, on_device(): lax.all_to_all(answered, 'seq', split_axis=0, concat_axis=0, tiled=True)  47.6 us
    all_to_all x1, waiting for transfers between devices, on_device(): lax.all_to_all(outgoing, 'seq', split_axis=0, concat_axis=0, tiled=True)  31.6 us
    dynamic_update_slice x8, local copies, waits for them, and re-layouts, on_device(): lax.dynamic_update_slice(packed_rows, received[src], (starts[src], 0))  30.7 us
    dot_general x1, matrix products, on_device(): jnp.dot(image_block, kv_weight, preferred_element_type=jnp.float32)  18 us
    unnamed x23, local copies, waits for them, and re-layouts  12.8 us
    all_to_all x2, starting transfers between devices, on_device(): lax.all_to_all(answered, 'seq', split_axis=0, concat_axis=0, tiled=True)  7.94 us
    scatter x1, local copies, waits for them, and re-layouts, on_device(): jnp.zeros((rows, width_cols), jnp.bfloat16).at[slot_index].set(queries)  7.25 us
  transfers between devices with their start and end apart: 6, of which 3 were waited for; matrix products, arithmetic and copies ran while one was open for 20% of the time, Pallas kernels for 13%

profile of v6, /device:TPU:0, one launch (start us, length us, event | category | flops | bytes accessed | tf_op | source)
XLA Modules:
  0.0 296.3 jit_solution(5103499033632977899)
XLA Ops:
  6.5 0.0 reduce-scatter.3.cloned.1.call-start
  6.5 18.0 %convolution_convert_fusion = bf16[1601,2048]{1,0:T(8,128)(2,1)S(1)} fusion(bf16[2048,2048]{1,0:T(8,128)(2,1)} %param.7, bf16[1,1601,2048]{2,1,0:T(8,128)(2,1)} %param.6), kind=kOutput, calls=%fused_computation.3 | convolution fusion | flops 13433440256 | bytes 21504000 | tf_op jit(solution)/shard_map/dot_general | solution.py:108
  24.5 0.4 fusion.5
  24.9 2.5 pad_maximum_fusion
  27.4 0.0 reduce-scatter.3.cloned.1.call-update
  27.4 0.0 reduce-scatter.5.cloned.1.call-start
  27.5 2.5 pad_maximum_fusion.1
  30.0 0.0 copy-start.4
  30.0 0.0 reduce-scatter.5.cloned.1.call-update
  30.0 0.7 copy-done.4
  30.7 1.1 reduce-window.11
  31.8 0.2 slice_reduce_fusion
  32.0 0.1 fusion.3
  32.2 0.7 copy.6
  32.9 5.2 %all-to-all-start = ((s32[8,1,1]{2,1,0:T(1,128)}), s32[8,1,1]{2,1,0:T(1,128)S(1)}, u32[]{:S(2)}, u32[]{:S(2)}) async-start(s32[8,1,1]{2,1,0:T(1,128)} %copy.6), calls=%async_computation | async-start | bytes 8192 | tf_op jit(solution)/shard_map/all_to_all | solution.py:99
  38.1 7.3 %scatter_custom_fusion = bf16[1024,2048]{1,0:T(8,128)(2,1)} fusion(s32[512]{0:T(512)S(1)} %bitcast.83, bf16[512,2048]{1,0:T(8,128)(2,1)} %param.4, bf16[]{:T(256)} %constant.37.clone.1), kind=kCustom, calls=%fused_computation.8 | custom fusion | bytes 4194816 | tf_op jit(solution)/shard_map/scatter | solution.py:95
  45.3 0.0 all-to-all-done
  45.3 4.7 %all-to-all-start.1 = ((bf16[8,128,2048]{2,1,0:T(8,128)(2,1)}), bf16[8,128,2048]{2,1,0:T(8,128)(2,1)}, u32[]{:S(2)}, u32[]{:S(2)}) async-start(bf16[8,128,2048]{2,1,0:T(8,128)(2,1)} %bitcast.80), calls=%async_computation.1 | async-start | bytes 8388608 | tf_op jit(solution)/shard_map/all_to_all | solution.py:112
  50.1 0.2 reduce
  50.3 0.2 reduce-window.10
  50.5 0.7 fusion.6
  61.3 0.6 slice.110
  67.5 31.6 %all-to-all-done.1 = bf16[8,128,2048]{2,1,0:T(8,128)(2,1)} async-done(((bf16[8,128,2048]{2,1,0:T(8,128)(2,1)}), bf16[8,128,2048]{2,1,0:T(8,128)(2,1)}, u32[]{:S(2)}, u32[]{:S(2)}) %all-to-all-start.1) | async-done | bytes 4194336 | tf_op jit(solution)/shard_map/all_to_all | solution.py:112
  99.2 3.5 %slice_bitcast_fusion = (bf16[128,2048]{1,0:T(8,128)(2,1)S(1)}, bf16[128,2048]{1,0:T(8,128)(2,1)S(1)}, bf16[128,2048]{1,0:T(8,128)(2,1)S(1)}, bf16[128,2048]{1,0...) fusion(bf16[8,128,2048]{2,1,0:T(8,128)(2,1)} %all-to-all-done.1), kind=kLoop, calls=%fused_computation.10 | loop fusion | bytes 8388608 | tf_op jit(solution)/shard_map/squeeze | solution.py:115
  102.7 2.7 broadcast_in_dim.4
  105.4 4.0 %dynamic_update_slice.24 = bf16[1152,2048]{1,0:T(8,128)(2,1)} dynamic-update-slice(bf16[1152,2048]{1,0:T(8,128)(2,1)} %broadcast_in_dim.4, bf16[128,2048]{1,0:T(8,128)(2,1)} %get-tuple-element.22, s32[]{:T(128)S(6)} %select_n.26, s32[]{:T(128)} %constant.31.clone.1) | dynamic-update-slice | bytes 1048580 | tf_op jit(solution)/shard_map/dynamic_update_slice | solution.py:115
  109.4 4.0 %dynamic_update_slice.25 = bf16[1152,2048]{1,0:T(8,128)(2,1)} dynamic-update-slice(bf16[1152,2048]{1,0:T(8,128)(2,1)} %dynamic_update_slice.24, bf16[128,2048]{1,0:T(8,128)(2,1)} %get-tuple-element.21, s32[]{:T(128)S(6)} %select_n.27, s32[]{:T(128)} %constant.31.clone.1) | dynamic-update-slice | bytes 1048580 | tf_op jit(solution)/shard_map/dynamic_update_slice | solution.py:115
  113.4 3.8 %dynamic_update_slice.26 = bf16[1152,2048]{1,0:T(8,128)(2,1)} dynamic-update-slice(bf16[1152,2048]{1,0:T(8,128)(2,1)} %dynamic_update_slice.25, bf16[128,2048]{1,0:T(8,128)(2,1)S(1)} %get-tuple-element.20, s32[]{:T(128)S(6)} %select_n.28, s32[]{:T(128)} %constant.31.clone.1) | dynamic-update-slice | bytes 1048580 | tf_op jit(solution)/shard_map/dynamic_update_slice | solution.py:115
  117.2 3.8 %dynamic_update_slice.27 = bf16[1152,2048]{1,0:T(8,128)(2,1)} dynamic-update-slice(bf16[1152,2048]{1,0:T(8,128)(2,1)} %dynamic_update_slice.26, bf16[128,2048]{1,0:T(8,128)(2,1)S(1)} %get-tuple-element.19, s32[]{:T(128)S(6)} %select_n.56, s32[]{:T(128)} %constant.31.clone.1) | dynamic-update-slice | bytes 1048580 | tf_op jit(solution)/shard_map/dynamic_update_slice | solution.py:115
  121.0 3.8 %dynamic_update_slice.28 = bf16[1152,2048]{1,0:T(8,128)(2,1)} dynamic-update-slice(bf16[1152,2048]{1,0:T(8,128)(2,1)} %dynamic_update_slice.27, bf16[128,2048]{1,0:T(8,128)(2,1)S(1)} %get-tuple-element.18, s32[]{:T(128)S(6)} %select_n.57, s32[]{:T(128)} %constant.31.clone.1) | dynamic-update-slice | bytes 1048580 | tf_op jit(solution)/shard_map/dynamic_update_slice | solution.py:115
  124.8 3.8 %dynamic_update_slice.29 = bf16[1152,2048]{1,0:T(8,128)(2,1)} dynamic-update-slice(bf16[1152,2048]{1,0:T(8,128)(2,1)} %dynamic_update_slice.28, bf16[128,2048]{1,0:T(8,128)(2,1)S(1)} %get-tuple-element.17, s32[]{:T(128)S(6)} %select_n.58, s32[]{:T(128)} %constant.31.clone.1) | dynamic-update-slice | bytes 1048580 | tf_op jit(solution)/shard_map/dynamic_update_slice | solution.py:115
  128.6 3.8 %dynamic_update_slice.30 = bf16[1152,2048]{1,0:T(8,128)(2,1)} dynamic-update-slice(bf16[1152,2048]{1,0:T(8,128)(2,1)} %dynamic_update_slice.29, bf16[128,2048]{1,0:T(8,128)(2,1)S(1)} %get-tuple-element.16, s32[]{:T(128)S(6)} %select_n.59, s32[]{:T(128)} %constant.31.clone.1) | dynamic-update-slice | bytes 1048580 | tf_op jit(solution)/shard_map/dynamic_update_slice | solution.py:115
  132.4 3.8 %dynamic_update_slice.31.q_ref = bf16[1152,2048]{1,0:T(8,128)(2,1)} dynamic-update-slice(bf16[1152,2048]{1,0:T(8,128)(2,1)} %dynamic_update_slice.30, bf16[128,2048]{1,0:T(8,128)(2,1)S(1)} %get-tuple-element.15, s32[]{:T(128)S(6)} %select_n.60, s32[]{:T(128)} %constant.31.clone.1) | dynamic-update-slice | bytes 1048580 | tf_op jit(solution)/shard_map/dynamic_update_slice | solution.py:115
  136.2 0.0 reduce-scatter.3.cloned.1.call-done.k_ref.v_ref
  136.2 0.0 copy-start.1
  136.2 1.1 copy-done.1
  137.3 37.4 %shard_map.46 = bf16[1152,1024]{1,0:T(8,128)(2,1)S(1)} custom-call(s32[1]{0:T(128)} %bitcast.3.tiles_ref, bf16[1152,2048]{1,0:T(8,128)(2,1)} %dynamic_update_slice.31.q_ref, bf16[1601,256]{1,0:T(8,128)(2,1)S(1)} %copy-done.1, bf16[1601,256]{1,0:T(8,128)(2,1)S(1)} %copy-done.1), custom_call_target="tpu_custom_call" | custom-call | flops 3357540352 | bytes 2916864 | tf_op jit(solution)/shard_map/pallas_call | solution.py:55
  174.7 0.8 bitcast_dynamic-update-slice_fusion.15
  175.5 0.8 bitcast_dynamic-update-slice_fusion.14
  176.3 0.8 bitcast_dynamic-update-slice_fusion.13
  177.0 0.8 bitcast_dynamic-update-slice_fusion.12
  177.8 0.8 bitcast_dynamic-update-slice_fusion.11
  178.6 1.1 copy-done.2
  179.7 37.4 %shard_map.47 = bf16[1152,1024]{1,0:T(8,128)(2,1)S(1)} custom-call(s32[1]{0:T(128)} %bitcast.3.tiles_ref, bf16[1152,2048]{1,0:T(8,128)(2,1)} %dynamic_update_slice.31.q_ref, bf16[1601,256]{1,0:T(8,128)(2,1)S(1)} %copy-done.2, bf16[1601,256]{1,0:T(8,128)(2,1)S(1)} %copy-done.2), custom_call_target="tpu_custom_call" | custom-call | flops 3357540352 | bytes 2916864 | tf_op jit(solution)/shard_map/pallas_call | solution.py:55
  217.1 0.0 copy-start
  217.1 0.1 bitcast_dynamic-update-slice_fusion.7
  217.2 0.1 bitcast_dynamic-update-slice_fusion.6
  217.3 0.1 bitcast_dynamic-update-slice_fusion.5
  217.3 0.1 bitcast_dynamic-update-slice_fusion.4
  217.4 0.1 bitcast_dynamic-update-slice_fusion.3
  217.5 1.0 copy-done
  218.5 0.8 bitcast_dynamic-update-slice_fusion.2
  219.3 1.3 copy-done.3
  220.7 0.8 bitcast_dynamic-update-slice_fusion.9
  221.4 0.8 bitcast_dynamic-update-slice_fusion.8
  222.2 3.6 %all-to-all-start.2 = ((bf16[8,128,1024]{2,1,0:T(8,128)(2,1)}), bf16[8,128,1024]{2,1,0:T(8,128)(2,1)S(1)}, u32[]{:S(2)}, u32[]{:S(2)}) async-start(bf16[8,128,1024]{2,1,0:T(8,128)(2,1)} %bitcast_dynamic-update-slice_fusion.8), calls=%async_computation.3 | async-start | bytes 4194304 | tf_op jit(solution)/shard_map/all_to_all | solution.py:139
  225.8 1.7 bitcast_dynamic-update-slice_fusion.1
  227.6 1.7 bitcast_dynamic-update-slice_fusion
  229.3 23.1 %all-to-all-done.2 = bf16[8,128,1024]{2,1,0:T(8,128)(2,1)S(1)} async-done(((bf16[8,128,1024]{2,1,0:T(8,128)(2,1)}), bf16[8,128,1024]{2,1,0:T(8,128)(2,1)S(1)}, u32[]{:S(2)}, u32[]{:S(2)}) %all-to-all-start.2) | async-done | bytes 2097184 | tf_op jit(solution)/shard_map/all_to_all | solution.py:139
  252.4 4.3 %all-to-all-start.3 = ((bf16[8,128,1024]{2,1,0:T(8,128)(2,1)}), bf16[8,128,1024]{2,1,0:T(8,128)(2,1)}, u32[]{:S(2)}, u32[]{:S(2)}) async-start(bf16[8,128,1024]{2,1,0:T(8,128)(2,1)} %bitcast_dynamic-update-slice_fusion), calls=%async_computation.5 | async-start | bytes 4194304 | tf_op jit(solution)/shard_map/all_to_all | solution.py:139
  256.7 2.1 gather_fusion
  258.8 24.5 %all-to-all-done.3 = bf16[8,128,1024]{2,1,0:T(8,128)(2,1)} async-done(((bf16[8,128,1024]{2,1,0:T(8,128)(2,1)}), bf16[8,128,1024]{2,1,0:T(8,128)(2,1)}, u32[]{:S(2)}, u32[]{:S(2)}) %all-to-all-start.3) | async-done | bytes 2097184 | tf_op jit(solution)/shard_map/all_to_all | solution.py:139
  283.3 4.6 %gather_fusion.1 = bf16[512,1024]{1,0:T(8,128)(2,1)S(1)} fusion(bf16[1024,1024]{1,0:T(8,128)(2,1)} %bitcast.45, s32[1024]{0:T(1024)S(1)} %pad_clamp_fusion), kind=kCustom, calls=%fused_computation.1 | custom fusion | bytes 2099200 | tf_op jit(solution)/shard_map/gather | solution.py:140
  287.9 1.5 pad_maximum_fusion.2
  (9 shorter events, 0.1 us)
Async XLA Ops:
  6.5 129.6 %reduce-scatter.3.cloned.1.call-start = ((), (), s32[]{:S(2)}) async-start(), calls=%async_computation.6 | async-start | bytes 4116480 | tf_op jit(solution)/shard_map/reduce_scatter | solution.py:118
  27.4 151.1 %reduce-scatter.5.cloned.1.call-start = ((), (), s32[]{:S(2)}) async-start(), calls=%async_computation.7 | async-start | bytes 4116480 | tf_op jit(solution)/shard_map/reduce_scatter | solution.py:118
  30.0 0.7 copy-start.4
  32.9 12.5 %all-to-all-start = ((s32[8,1,1]{2,1,0:T(1,128)}), s32[8,1,1]{2,1,0:T(1,128)S(1)}, u32[]{:S(2)}, u32[]{:S(2)}) async-start(s32[8,1,1]{2,1,0:T(1,128)} %copy.6), calls=%async_computation | async-start | bytes 8192 | tf_op jit(solution)/shard_map/all_to_all | solution.py:99
  45.3 53.8 %all-to-all-start.1 = ((bf16[8,128,2048]{2,1,0:T(8,128)(2,1)}), bf16[8,128,2048]{2,1,0:T(8,128)(2,1)}, u32[]{:S(2)}, u32[]{:S(2)}) async-start(bf16[8,128,2048]{2,1,0:T(8,128)(2,1)} %bitcast.80), calls=%async_computation.1 | async-start | bytes 8388608 | tf_op jit(solution)/shard_map/all_to_all | solution.py:112
  136.2 1.1 copy-start.1
  178.6 1.1 copy-start.2
  217.1 1.4 copy-start
  219.3 1.3 copy-start.3
  222.2 30.2 %all-to-all-start.2 = ((bf16[8,128,1024]{2,1,0:T(8,128)(2,1)}), bf16[8,128,1024]{2,1,0:T(8,128)(2,1)S(1)}, u32[]{:S(2)}, u32[]{:S(2)}) async-start(bf16[8,128,1024]{2,1,0:T(8,128)(2,1)} %bitcast_dynamic-update-slice_fusion.8), calls=%async_computation.3 | async-start | bytes 4194304 | tf_op jit(solution)/shard_map/all_to_all | solution.py:139
  252.4 31.0 %all-to-all-start.3 = ((bf16[8,128,1024]{2,1,0:T(8,128)(2,1)}), bf16[8,128,1024]{2,1,0:T(8,128)(2,1)}, u32[]{:S(2)}, u32[]{:S(2)}) async-start(bf16[8,128,1024]{2,1,0:T(8,128)(2,1)} %bitcast_dynamic-update-slice_fusion), calls=%async_computation.5 | async-start | bytes 4194304 | tf_op jit(solution)/shard_map/all_to_all | solution.py:139
Sparse Core Ops, SparseCore 0:
  27.6 65.5 reduce-scatter.2
  95.5 62.8 reduce-scatter.4

commit v7 on v5

--- a/solution.py
+++ b/solution.py
@@ -18,8 +18,9 @@
     def _():
         keys = k_ref[...]
         values = v_ref[...]
-        for head in range(group):
-            columns = slice(head * head_dim, (head + 1) * head_dim)
+
+        def one_head(head, carry):
+            columns = pl.ds(pl.multiple_of(head * head_dim, head_dim), head_dim)
             scores = (
                 lax.dot_general(
                     q_ref[:, columns],
@@ -35,6 +36,9 @@
             probs = weights_exp.astype(jnp.bfloat16)
             weighted = jnp.dot(probs, values, preferred_element_type=jnp.float32)
             o_ref[:, columns] = (weighted / totals).astype(o_ref.dtype)
+            return carry
+
+        lax.fori_loop(0, group, one_head, 0)
 
 
 def attend(query_rows, key_values, group, head_dim, first_head, live_tiles, tile):
@@ -112,30 +116,34 @@
     image_block = features[0]
     tensor_devices = lax.axis_size("tensor")
     local_kv = KV_HEADS // tensor_devices
-    projected = jnp.dot(image_block, kv_weight, preferred_element_type=jnp.float32).astype(
-        jnp.bfloat16
-    )
     kv_width = 2 * HEAD_DIM
+    head_split = 2
+    call_heads = group // head_split
     received = lax.all_to_all(outgoing, "seq", split_axis=0, concat_axis=0, tiled=True)
     packed_rows = received.reshape(-1, width_cols)[packed_slot]
     pieces = []
     for head in range(local_kv):
+        weight_part = jnp.concatenate(
+            [
+                kv_weight[:, (dest * local_kv + head) * kv_width :][:, :kv_width]
+                for dest in range(tensor_devices)
+            ],
+            axis=1,
+        )
         key_values = lax.psum_scatter(
-            jnp.concatenate(
-                [
-                    projected[:, (dest * local_kv + head) * kv_width :][:, :kv_width]
-                    for dest in range(tensor_devices)
-                ],
-                axis=1,
+            jnp.dot(image_block, weight_part, preferred_element_type=jnp.float32).astype(
+                jnp.bfloat16
             ),
             "tensor",
             scatter_dimension=1,
             tiled=True,
         )
-        answered = attend(packed_rows, key_values, group, HEAD_DIM, head * group, live_tiles, tile)
-        answered = answered[slot_packed].reshape(seq_devices, capacity, -1)
-        returned = lax.all_to_all(answered, "seq", split_axis=0, concat_axis=0, tiled=True)
-        pieces.append(returned.reshape(rows, -1)[slot_index])
+        for part in range(head_split):
+            first = head * group + part * call_heads
+            answered = attend(packed_rows, key_values, call_heads, HEAD_DIM, first, live_tiles, tile)
+            answered = answered[slot_packed].reshape(seq_devices, capacity, -1)
+            returned = lax.all_to_all(answered, "seq", split_axis=0, concat_axis=0, tiled=True)
+            pieces.append(returned.reshape(rows, -1)[slot_index])
     return jnp.concatenate(pieces, axis=1)
 
 

time: 234 us -> 260 us (1.11)
  starting transfers between devices: 38.5 us -> 69.6 us
  local copies, waits for them, and re-layouts: 42.4 us -> 69.5 us
  waiting for transfers between devices: 70.3 us -> 49.8 us
  Pallas kernels: 27.7 us -> 19.4 us
  other arithmetic: 21.1 us -> 15 us
  matrix products: 18 us -> 20.7 us
    all_to_all x2 -> x4, starting transfers between devices: 28.5 us -> 59.8 us  [on_device(): lax.all_to_all(answered, 'seq', split_axis=0, concat_axis=0, tiled=True)]
    reduce_scatter x2, waiting for transfers between devices: 13.8 us -> 0.01 us  [on_device(): lax.psum_scatter(jnp.dot(image_block, weight_part, preferred_element_type...]
    unnamed x6 -> x20, local copies, waits for them, and re-layouts: 2.3 us -> 12 us
    gather x2 -> x4, local copies, waits for them, and re-layouts: 10.7 us -> 20.3 us  [on_device(): answered = answered[slot_packed].reshape(seq_devices, capacity, -1)]
    pallas_call x2 -> x4, Pallas kernels: 27.7 us -> 19.4 us  [attend(): pl.pallas_call(functools.partial(attend_kernel, scale, group, head_dim),...]
    all_to_all x2 -> x4, waiting for transfers between devices: 22 us -> 15.4 us  [on_device(): lax.all_to_all(answered, 'seq', split_axis=0, concat_axis=0, tiled=True)]
    concatenate x2 -> x0, other arithmetic: 4.95 us -> none  [on_device(): jnp.concatenate([projected[:, (dest * local_kv + head) * kv_width:][:, :k...]
    slice x2, local copies, waits for them, and re-layouts: 0.64 us -> 5.15 us  [the longest x1 4.94 us: on_device(): kv_weight[:, (dest * local_kv + head) * kv_width:][:, :kv_width]]
  transfers between devices with their start and end apart: 6 -> 8, of which waited for: 3 -> 5; matrix products, arithmetic and copies ran while one was open for 23% -> 29% of each run, Pallas kernels for 12% -> 8%
where the time goes in v7:
time: 260 us; the launch traced here: 258 us
  starting transfers between devices  69.6 us (27%)
  local copies, waits for them, and re-layouts  69.5 us (27%)
  waiting for transfers between devices  49.8 us (19%)
  matrix products  20.7 us (8%)
  Pallas kernels  19.4 us (7%)
  other arithmetic  15 us (6%)
  between operations  14.3 us (6%)
    all_to_all x4, starting transfers between devices, on_device(): lax.all_to_all(answered, 'seq', split_axis=0, concat_axis=0, tiled=True)  59.8 us
    all_to_all x1, waiting for transfers between devices, on_device(): lax.all_to_all(outgoing, 'seq', split_axis=0, concat_axis=0, tiled=True)  34.4 us
    dot_general x2, matrix products, on_device(): jnp.dot(image_block, weight_part, preferred_element_type=jnp.float32)  20.7 us
    gather x4, local copies, waits for them, and re-layouts, on_device(): answered = answered[slot_packed].reshape(seq_devices, capacity, -1)  20.3 us
    pallas_call x4, Pallas kernels, attend(): pl.pallas_call(functools.partial(attend_kernel, scale, group, head_dim),...  19.4 us
    all_to_all x4, waiting for transfers between devices, on_device(): lax.all_to_all(answered, 'seq', split_axis=0, concat_axis=0, tiled=True)  15.4 us
    unnamed x20, local copies, waits for them, and re-layouts  12 us
    gather x1, local copies, waits for them, and re-layouts, on_device(): packed_rows = received.reshape(-1, width_cols)[packed_slot]  11.6 us
  transfers between devices with their start and end apart: 8, of which 5 were waited for; matrix products, arithmetic and copies ran while one was open for 29% of the time, Pallas kernels for 8%

profile of v7, /device:TPU:0, one launch (start us, length us, event | category | flops | bytes accessed | tf_op | source)
XLA Modules:
  0.0 258.5 jit_solution(2180755507678349965)
XLA Ops:
  6.5 0.0 reduce-scatter.3.cloned.1.call-start
  6.5 4.9 %fusion.44 = (bf16[2048,256]{1,0:T(8,128)(2,1)S(1)}, bf16[2048,256]{1,0:T(8,128)(2,1)S(1)}, bf16[2048,256]{1,0:T(8,128)(2,1)S(1)}, bf16[2048,256]{1,0:T(8,128)(2...) fusion(bf16[2048,2048]{1,0:T(8,128)(2,1)} %param.7), kind=kLoop, calls=%fused_computation.86 | loop fusion | bytes 16777216 | tf_op jit(solution)/shard_map/slice | solution.py:128
  11.5 0.9 copy-done.9
  12.4 9.0 %fusion.33 = bf16[1601,1024]{1,0:T(8,128)(2,1)} fusion(bf16[1,1601,2048]{2,1,0:T(8,128)(2,1)S(1)} %copy-done.9, bf16[2048,256]{1,0:T(8,128)(2,1)S(1)} %get-tuple-element.10, bf16[2048,256]{1,0:T(8,128)(2,1)S(1)} %get-tuple-element.11, bf16[2048,256]{1,0:T(8,128)(2,1)S(1)} %get-tuple-element.12, bf16[2048,256]{1,0:T(8,128)(2,1)S(1)} %get-tuple-element.7), kind=kOutput, calls=%fused_computation.31 | convolution fusion | flops 6733497344 | bytes 14030848 | tf_op jit(solution)/shard_map/dot_general | solution.py:134
  21.4 0.0 reduce-scatter.3.cloned.1.call-update
  21.4 0.0 reduce-scatter.5.cloned.1.call-start
  21.5 0.0 copy-start.8
  21.5 11.7 %fusion.28 = bf16[1601,1024]{1,0:T(8,128)(2,1)} fusion(bf16[1,1601,2048]{2,1,0:T(8,128)(2,1)} %param.6, bf16[2048,256]{1,0:T(8,128)(2,1)S(1)} %get-tuple-element.13, bf16[2048,256]{1,0:T(8,128)(2,1)} %get-tuple-element.14, bf16[2048,256]{1,0:T(8,128)(2,1)S(1)} %get-tuple-element.8, bf16[2048,256]{1,0:T(8,128)(2,1)S(1)} %get-tuple-element.9), kind=kOutput, calls=%fused_computation.30 | convolution fusion | flops 6733497344 | bytes 14030848 | tf_op jit(solution)/shard_map/dot_general | solution.py:134
  33.2 0.0 reduce-scatter.5.cloned.1.call-update
  33.2 0.0 copy-done.8
  33.3 1.1 reduce-window.11
  34.4 0.2 slice_reduce_fusion
  34.7 0.1 fusion.40
  34.8 0.7 copy.7
  35.5 5.2 %all-to-all-start = ((s32[8,1,1]{2,1,0:T(1,128)}), s32[8,1,1]{2,1,0:T(1,128)S(1)}, u32[]{:S(2)}, u32[]{:S(2)}) async-start(s32[8,1,1]{2,1,0:T(1,128)} %copy.7), calls=%async_computation | async-start | bytes 8192 | tf_op jit(solution)/shard_map/all_to_all | solution.py:99
  40.7 7.3 %scatter_custom_fusion = bf16[1024,2048]{1,0:T(8,128)(2,1)} fusion(s32[512]{0:T(512)S(1)} %bitcast.88, bf16[512,2048]{1,0:T(8,128)(2,1)} %param.4, bf16[]{:T(256)} %constant.63.clone.1), kind=kCustom, calls=%fused_computation.33 | custom fusion | bytes 4194816 | tf_op jit(solution)/shard_map/scatter | solution.py:95
  48.0 0.0 all-to-all-done
  48.0 4.5 %all-to-all-start.1 = ((bf16[8,128,2048]{2,1,0:T(8,128)(2,1)}), bf16[8,128,2048]{2,1,0:T(8,128)(2,1)}, u32[]{:S(2)}, u32[]{:S(2)}) async-start(bf16[8,128,2048]{2,1,0:T(8,128)(2,1)} %bitcast.71), calls=%async_computation.1 | async-start | bytes 8388608 | tf_op jit(solution)/shard_map/all_to_all | solution.py:122
  52.6 0.2 reduce
  52.8 0.2 reduce-window.10
  53.0 0.6 slice.46
  54.2 0.6 fusion.45
  54.9 4.4 %compare_select_fusion.13 = s32[1024,1]{0,1:T(1,128)S(1)} fusion(s32[]{:T(128)} %bitcast.27, s32[]{:T(128)} %bitcast.28, s32[]{:T(128)} %bitcast.29, s32[]{:T(128)} %bitcast.30, s32[]{:T(128)} %bitcast.31, s32[]{:T(128)} %bitcast.33, s32[]{:T(128)} %bitcast.32), kind=kLoop, calls=%fused_computation.61 | loop fusion | flops 23552 | bytes 4124 | tf_op jit(solution)/shard_map/gather | solution.py:112
  59.3 0.7 fusion.46
  60.0 0.1 convert_reduce_fusion
  60.1 4.4 %compare_select_fusion.4 = (s32[1024,1]{0,1:T(1,128)S(1)}, s32[1024,1]{0,1:T(1,128)S(1)}) fusion(s32[]{:T(128)} %bitcast.14, s32[]{:T(128)} %bitcast.15, s32[]{:T(128)} %bitcast.16, s32[]{:T(128)} %bitcast.17, s32[]{:T(128)} %bitcast.18, s32[]{:T(128)} %bitcast.20, s32[]{:T(128)} %bitcast.19, s32[1024,1]{0,1:T(1,128)S(1)} %bitcast.76), kind=kLoop, calls=%fused_computation.50 | loop fusion | flops 38912 | bytes 12316 | tf_op jit(solution)/shard_map/gather | solution.py:108
  64.5 0.7 broadcast_select_fusion.2
  65.2 0.7 compare_select_fusion.2
  65.9 1.3 broadcast_select_fusion.1
  67.2 34.4 %all-to-all-done.1 = bf16[8,128,2048]{2,1,0:T(8,128)(2,1)} async-done(((bf16[8,128,2048]{2,1,0:T(8,128)(2,1)}), bf16[8,128,2048]{2,1,0:T(8,128)(2,1)}, u32[]{:S(2)}, u32[]{:S(2)}) %all-to-all-start.1) | async-done | bytes 4194336 | tf_op jit(solution)/shard_map/all_to_all | solution.py:122
  101.6 11.6 %gather_fusion = bf16[1024,2048]{1,0:T(8,128)(2,1)} fusion(bf16[1024,2048]{1,0:T(8,128)(2,1)} %bitcast.10, s32[1024]{0:T(1024)S(1)} %broadcast_clamp_fusion.1), kind=kCustom, calls=%fused_computation | custom fusion | bytes 8392704 | tf_op jit(solution)/shard_map/gather | solution.py:123
  113.2 2.2 copy-done
  115.4 1.1 copy-done.6
  116.5 4.9 %shard_map.47 = bf16[1024,512]{1,0:T(8,128)(2,1)S(1)} custom-call(s32[1]{0:T(128)} %bitcast.3.tiles_ref, bf16[1024,2048]{1,0:T(8,128)(2,1)S(1)} %copy-done, bf16[1601,256]{1,0:T(8,128)(2,1)S(1)} %copy-done.6, bf16[1601,256]{1,0:T(8,128)(2,1)S(1)} %copy-done.6), custom_call_target="tpu_custom_call" | custom-call | flops 1678770176 | bytes 1868288 | tf_op jit(solution)/shard_map/pallas_call | solution.py:55
  121.4 0.0 copy-start.7
  121.4 5.1 %gather_fusion.3 = bf16[1024,512]{1,0:T(8,128)(2,1)} fusion(bf16[1024,512]{1,0:T(8,128)(2,1)S(1)} %shard_map.47, s32[1024]{0:T(1024)S(1)} %broadcast_clamp_fusion), kind=kCustom, calls=%fused_computation.3 | custom fusion | bytes 2101248 | tf_op jit(solution)/shard_map/gather | solution.py:144
  126.5 15.5 %all-to-all-start.3 = ((bf16[8,128,512]{2,1,0:T(8,128)(2,1)}), bf16[8,128,512]{2,1,0:T(8,128)(2,1)S(1)}, u32[]{:S(2)}, u32[]{:S(2)}) async-start(bf16[8,128,512]{2,1,0:T(8,128)(2,1)} %bitcast.41), calls=%async_computation.4 | async-start | bytes 2097152 | tf_op jit(solution)/shard_map/all_to_all | solution.py:145
  142.0 0.0 copy-done.7
  142.0 0.0 copy-start.1
  142.0 2.2 copy-done.1
  144.2 4.9 %shard_map.46 = bf16[1024,512]{1,0:T(8,128)(2,1)S(1)} custom-call(s32[1]{0:T(128)} %bitcast.3.tiles_ref, bf16[1024,2048]{1,0:T(8,128)(2,1)S(1)} %copy-done.1, bf16[1601,256]{1,0:T(8,128)(2,1)S(1)} %copy-done.7, bf16[1601,256]{1,0:T(8,128)(2,1)S(1)} %copy-done.7), custom_call_target="tpu_custom_call" | custom-call | flops 1678770176 | bytes 1868288 | tf_op jit(solution)/shard_map/pallas_call | solution.py:55
  149.1 5.1 %gather_fusion.1 = bf16[1024,512]{1,0:T(8,128)(2,1)} fusion(bf16[1024,512]{1,0:T(8,128)(2,1)S(1)} %shard_map.46, s32[1024]{0:T(1024)S(1)} %broadcast_clamp_fusion), kind=kCustom, calls=%fused_computation.1 | custom fusion | bytes 2101248 | tf_op jit(solution)/shard_map/gather | solution.py:144
  154.2 3.2 %all-to-all-done.3 = bf16[8,128,512]{2,1,0:T(8,128)(2,1)S(1)} async-done(((bf16[8,128,512]{2,1,0:T(8,128)(2,1)}), bf16[8,128,512]{2,1,0:T(8,128)(2,1)S(1)}, u32[]{:S(2)}, u32[]{:S(2)}) %all-to-all-start.3) | async-done | bytes 1048608 | tf_op jit(solution)/shard_map/all_to_all | solution.py:145
  157.4 14.0 %all-to-all-start.2 = ((bf16[8,128,512]{2,1,0:T(8,128)(2,1)}), bf16[8,128,512]{2,1,0:T(8,128)(2,1)}, u32[]{:S(2)}, u32[]{:S(2)}) async-start(bf16[8,128,512]{2,1,0:T(8,128)(2,1)} %bitcast.73), calls=%async_computation.3 | async-start | bytes 2097152 | tf_op jit(solution)/shard_map/all_to_all | solution.py:145
  171.3 0.0 reduce-scatter.5.cloned.1.call-done.k_ref.v_ref
  171.3 0.0 copy-start.2
  171.3 2.2 copy-done.2
  173.5 1.1 copy-done.4
  174.7 4.9 %shard_map.48 = bf16[1024,512]{1,0:T(8,128)(2,1)S(1)} custom-call(s32[1]{0:T(128)} %bitcast.3.tiles_ref, bf16[1024,2048]{1,0:T(8,128)(2,1)S(1)} %copy-done.2, bf16[1601,256]{1,0:T(8,128)(2,1)S(1)} %copy-done.4, bf16[1601,256]{1,0:T(8,128)(2,1)S(1)} %copy-done.4), custom_call_target="tpu_custom_call" | custom-call | flops 1678770176 | bytes 1868288 | tf_op jit(solution)/shard_map/pallas_call | solution.py:55
  179.5 0.0 copy-start.5
  179.5 5.1 %gather_fusion.5 = bf16[1024,512]{1,0:T(8,128)(2,1)} fusion(bf16[1024,512]{1,0:T(8,128)(2,1)S(1)} %shard_map.48, s32[1024]{0:T(1024)S(1)} %broadcast_clamp_fusion), kind=kCustom, calls=%fused_computation.5 | custom fusion | bytes 2101248 | tf_op jit(solution)/shard_map/gather | solution.py:144
  184.6 2.2 all-to-all-done.2
  186.8 15.9 %all-to-all-start.4 = ((bf16[8,128,512]{2,1,0:T(8,128)(2,1)}), bf16[8,128,512]{2,1,0:T(8,128)(2,1)}, u32[]{:S(2)}, u32[]{:S(2)}) async-start(bf16[8,128,512]{2,1,0:T(8,128)(2,1)} %bitcast.74), calls=%async_computation.6 | async-start | bytes 2097152 | tf_op jit(solution)/shard_map/all_to_all | solution.py:145
  202.7 2.2 copy-done.3
  204.9 4.9 %shard_map.49 = bf16[1024,512]{1,0:T(8,128)(2,1)S(1)} custom-call(s32[1]{0:T(128)} %bitcast.3.tiles_ref, bf16[1024,2048]{1,0:T(8,128)(2,1)S(1)} %copy-done.3, bf16[1601,256]{1,0:T(8,128)(2,1)S(1)} %copy-done.5, bf16[1601,256]{1,0:T(8,128)(2,1)S(1)} %copy-done.5), custom_call_target="tpu_custom_call" | custom-call | flops 1678770176 | bytes 1868288 | tf_op jit(solution)/shard_map/pallas_call | solution.py:55
  209.7 5.1 %gather_fusion.7 = bf16[1024,512]{1,0:T(8,128)(2,1)} fusion(bf16[1024,512]{1,0:T(8,128)(2,1)S(1)} %shard_map.49, s32[1024]{0:T(1024)S(1)} %broadcast_clamp_fusion), kind=kCustom, calls=%fused_computation.7 | custom fusion | bytes 2101248 | tf_op jit(solution)/shard_map/gather | solution.py:144
  214.8 3.3 %all-to-all-done.4 = bf16[8,128,512]{2,1,0:T(8,128)(2,1)} async-done(((bf16[8,128,512]{2,1,0:T(8,128)(2,1)}), bf16[8,128,512]{2,1,0:T(8,128)(2,1)}, u32[]{:S(2)}, u32[]{:S(2)}) %all-to-all-start.4) | async-done | bytes 1048608 | tf_op jit(solution)/shard_map/all_to_all | solution.py:145
  218.2 14.5 %all-to-all-start.5 = ((bf16[8,128,512]{2,1,0:T(8,128)(2,1)}), bf16[8,128,512]{2,1,0:T(8,128)(2,1)S(1)}, u32[]{:S(2)}, u32[]{:S(2)}) async-start(bf16[8,128,512]{2,1,0:T(8,128)(2,1)} %bitcast.72), calls=%async_computation.7 | async-start | bytes 2097152 | tf_op jit(solution)/shard_map/all_to_all | solution.py:145
  232.7 2.0 gather_fusion.4
  234.7 3.3 %gather_fusion.2 = bf16[512,512]{1,0:T(8,128)(2,1)S(1)} fusion(bf16[1024,512]{1,0:T(8,128)(2,1)} %bitcast.40, s32[1024]{0:T(1024)S(1)} %pad_clamp_fusion), kind=kCustom, calls=%fused_computation.2 | custom fusion | bytes 1050624 | tf_op jit(solution)/shard_map/gather | solution.py:146
  238.0 3.3 %gather_fusion.6 = bf16[512,512]{1,0:T(8,128)(2,1)S(1)} fusion(bf16[1024,512]{1,0:T(8,128)(2,1)} %bitcast.45, s32[1024]{0:T(1024)S(1)} %pad_clamp_fusion), kind=kCustom, calls=%fused_computation.6 | custom fusion | bytes 1050624 | tf_op jit(solution)/shard_map/gather | solution.py:146
  241.4 6.7 %all-to-all-done.5 = bf16[8,128,512]{2,1,0:T(8,128)(2,1)S(1)} async-done(((bf16[8,128,512]{2,1,0:T(8,128)(2,1)}), bf16[8,128,512]{2,1,0:T(8,128)(2,1)S(1)}, u32[]{:S(2)}, u32[]{:S(2)}) %all-to-all-start.5) | async-done | bytes 1048608 | tf_op jit(solution)/shard_map/all_to_all | solution.py:145
  248.0 2.0 gather_fusion.8
  250.0 1.6 pad_maximum_fusion
  (19 shorter events, 0.2 us)
Async XLA Ops:
  6.5 106.7 %reduce-scatter.3.cloned.1.call-start = ((), (), s32[]{:S(2)}) async-start(), calls=%async_computation.8 | async-start | bytes 4116480 | tf_op jit(solution)/shard_map/reduce_scatter | solution.py:133
  6.5 5.9 %copy-start.9 = (bf16[1,1601,2048]{2,1,0:T(8,128)(2,1)S(1)}, bf16[1,1601,2048]{2,1,0:T(8,128)(2,1)}, u32[]{:S(2)}) copy-start(bf16[1,1601,2048]{2,1,0:T(8,128)(2,1)} %param.6) | copy-start | bytes 19673092
  21.4 149.9 %reduce-scatter.5.cloned.1.call-start = ((), (), s32[]{:S(2)}) async-start(), calls=%async_computation.9 | async-start | bytes 4116480 | tf_op jit(solution)/shard_map/reduce_scatter | solution.py:133
  21.5 11.8 %copy-start.8 = (s32[512,1]{0,1:T(1,128)S(1)}, s32[512,1]{0,1:T(1,128)}, u32[]{:S(2)}) copy-start(s32[512,1]{0,1:T(1,128)} %param.5) | copy-start | bytes 6148
  35.5 12.5 %all-to-all-start = ((s32[8,1,1]{2,1,0:T(1,128)}), s32[8,1,1]{2,1,0:T(1,128)S(1)}, u32[]{:S(2)}, u32[]{:S(2)}) async-start(s32[8,1,1]{2,1,0:T(1,128)} %copy.7), calls=%async_computation | async-start | bytes 8192 | tf_op jit(solution)/shard_map/all_to_all | solution.py:99
  48.0 53.7 %all-to-all-start.1 = ((bf16[8,128,2048]{2,1,0:T(8,128)(2,1)}), bf16[8,128,2048]{2,1,0:T(8,128)(2,1)}, u32[]{:S(2)}, u32[]{:S(2)}) async-start(bf16[8,128,2048]{2,1,0:T(8,128)(2,1)} %bitcast.71), calls=%async_computation.1 | async-start | bytes 8388608 | tf_op jit(solution)/shard_map/all_to_all | solution.py:122
  113.2 2.2 copy-start
  115.4 1.1 copy-start.6
  121.4 20.6 %copy-start.7 = (bf16[1601,256]{1,0:T(8,128)(2,1)S(1)}, bf16[1601,256]{1,0:T(8,128)(2,1)}, u32[]{:S(2)}) copy-start(bf16[1601,256]{1,0:T(8,128)(2,1)} %reduce-scatter.3.cloned.1.call-done.k_ref.v_ref) | copy-start | bytes 2459140
  126.5 30.9 %all-to-all-start.3 = ((bf16[8,128,512]{2,1,0:T(8,128)(2,1)}), bf16[8,128,512]{2,1,0:T(8,128)(2,1)S(1)}, u32[]{:S(2)}, u32[]{:S(2)}) async-start(bf16[8,128,512]{2,1,0:T(8,128)(2,1)} %bitcast.41), calls=%async_computation.4 | async-start | bytes 2097152 | tf_op jit(solution)/shard_map/all_to_all | solution.py:145
  142.0 2.3 copy-start.1
  157.4 29.4 %all-to-all-start.2 = ((bf16[8,128,512]{2,1,0:T(8,128)(2,1)}), bf16[8,128,512]{2,1,0:T(8,128)(2,1)}, u32[]{:S(2)}, u32[]{:S(2)}) async-start(bf16[8,128,512]{2,1,0:T(8,128)(2,1)} %bitcast.73), calls=%async_computation.3 | async-start | bytes 2097152 | tf_op jit(solution)/shard_map/all_to_all | solution.py:145
  171.3 2.2 copy-start.2
  173.5 1.1 copy-start.4
  179.5 23.1 %copy-start.5 = (bf16[1601,256]{1,0:T(8,128)(2,1)S(1)}, bf16[1601,256]{1,0:T(8,128)(2,1)}, u32[]{:S(2)}) copy-start(bf16[1601,256]{1,0:T(8,128)(2,1)} %reduce-scatter.5.cloned.1.call-done.k_ref.v_ref) | copy-start | bytes 2459140
  186.8 31.4 %all-to-all-start.4 = ((bf16[8,128,512]{2,1,0:T(8,128)(2,1)}), bf16[8,128,512]{2,1,0:T(8,128)(2,1)}, u32[]{:S(2)}, u32[]{:S(2)}) async-start(bf16[8,128,512]{2,1,0:T(8,128)(2,1)} %bitcast.74), calls=%async_computation.6 | async-start | bytes 2097152 | tf_op jit(solution)/shard_map/all_to_all | solution.py:145
  202.7 2.2 copy-start.3
  218.2 29.9 %all-to-all-start.5 = ((bf16[8,128,512]{2,1,0:T(8,128)(2,1)}), bf16[8,128,512]{2,1,0:T(8,128)(2,1)S(1)}, u32[]{:S(2)}, u32[]{:S(2)}) async-start(bf16[8,128,512]{2,1,0:T(8,128)(2,1)} %bitcast.72), calls=%async_computation.7 | async-start | bytes 2097152 | tf_op jit(solution)/shard_map/all_to_all | solution.py:145
Sparse Core Ops, SparseCore 0:
  21.6 65.5 reduce-scatter.2
  89.5 62.8 reduce-scatter.4

commit v8 on v7

--- a/solution.py
+++ b/solution.py
@@ -117,8 +117,6 @@
     tensor_devices = lax.axis_size("tensor")
     local_kv = KV_HEADS // tensor_devices
     kv_width = 2 * HEAD_DIM
-    head_split = 2
-    call_heads = group // head_split
     received = lax.all_to_all(outgoing, "seq", split_axis=0, concat_axis=0, tiled=True)
     packed_rows = received.reshape(-1, width_cols)[packed_slot]
     pieces = []
@@ -138,12 +136,10 @@
             scatter_dimension=1,
             tiled=True,
         )
-        for part in range(head_split):
-            first = head * group + part * call_heads
-            answered = attend(packed_rows, key_values, call_heads, HEAD_DIM, first, live_tiles, tile)
-            answered = answered[slot_packed].reshape(seq_devices, capacity, -1)
-            returned = lax.all_to_all(answered, "seq", split_axis=0, concat_axis=0, tiled=True)
-            pieces.append(returned.reshape(rows, -1)[slot_index])
+        answered = attend(packed_rows, key_values, group, HEAD_DIM, head * group, live_tiles, tile)
+        answered = answered[slot_packed].reshape(seq_devices, capacity, -1)
+        returned = lax.all_to_all(answered, "seq", split_axis=0, concat_axis=0, tiled=True)
+        pieces.append(returned.reshape(rows, -1)[slot_index])
     return jnp.concatenate(pieces, axis=1)
 
 

time: 260 us -> 246 us (0.946)
  local copies, waits for them, and re-layouts: 69.5 us -> 47.9 us
  starting transfers between devices: 69.6 us -> 50.4 us
  Pallas kernels: 19.4 us -> 38.4 us
  waiting for transfers between devices: 49.8 us -> 57.5 us
    all_to_all x4 -> x2, starting transfers between devices: 59.8 us -> 40.6 us  [on_device(): lax.all_to_all(answered, 'seq', split_axis=0, concat_axis=0, tiled=True)]
    pallas_call x4 -> x2, Pallas kernels: 19.4 us -> 38.4 us  [attend(): pl.pallas_call(functools.partial(attend_kernel, scale, group, head_dim),...]
    gather x4 -> x2, local copies, waits for them, and re-layouts: 20.3 us -> 10.7 us  [on_device(): answered = answered[slot_packed].reshape(seq_devices, capacity, -1)]
    unnamed x20 -> x8, local copies, waits for them, and re-layouts: 12 us -> 3.2 us
    all_to_all x4 -> x2, waiting for transfers between devices: 15.4 us -> 23.1 us  [on_device(): lax.all_to_all(answered, 'seq', split_axis=0, concat_axis=0, tiled=True)]
    gather x4 -> x2, local copies, waits for them, and re-layouts: 10.6 us -> 7.37 us  [on_device(): pieces.append(returned.reshape(rows, -1)[slot_index])]
  transfers between devices with their start and end apart: 8 -> 6, of which waited for: 5 -> 3; matrix products, arithmetic and copies ran while one was open for 29% -> 25% of each run, Pallas kernels for 8% -> 16%
where the time goes in v8:
time: 246 us
  waiting for transfers between devices  57.5 us (23%)
  starting transfers between devices  50.4 us (20%)
  local copies, waits for them, and re-layouts  47.9 us (19%)
  Pallas kernels  38.4 us (16%)
  matrix products  21 us (9%)
  other arithmetic  16.1 us (7%)
  between operations  14.2 us (6%)
    all_to_all x2, starting transfers between devices, on_device(): lax.all_to_all(answered, 'seq', split_axis=0, concat_axis=0, tiled=True)  40.6 us
    pallas_call x2, Pallas kernels, attend(): pl.pallas_call(functools.partial(attend_kernel, scale, group, head_dim),...  38.4 us
    all_to_all x1, waiting for transfers between devices, on_device(): lax.all_to_all(outgoing, 'seq', split_axis=0, concat_axis=0, tiled=True)  34.4 us
    all_to_all x2, waiting for transfers between devices, on_device(): lax.all_to_all(answered, 'seq', split_axis=0, concat_axis=0, tiled=True)  23.1 us
    dot_general x2, matrix products, on_device(): jnp.dot(image_block, weight_part, preferred_element_type=jnp.float32)  21 us
    gather x1, local copies, waits for them, and re-layouts, on_device(): packed_rows = received.reshape(-1, width_cols)[packed_slot]  11.6 us
    gather x2, local copies, waits for them, and re-layouts, on_device(): answered = answered[slot_packed].reshape(seq_devices, capacity, -1)  10.7 us
    gather x2, local copies, waits for them, and re-layouts, on_device(): pieces.append(returned.reshape(rows, -1)[slot_index])  7.37 us
  transfers between devices with their start and end apart: 6, of which 3 were waited for; matrix products, arithmetic and copies ran while one was open for 25% of the time, Pallas kernels for 16%

profile of v8, /device:TPU:0, one launch (start us, length us, event | category | flops | bytes accessed | tf_op | source)
XLA Modules:
  0.0 245.6 jit_solution(5705965118716932613)
XLA Ops:
  6.5 0.0 reduce-scatter.5.cloned.1.call-start
  6.5 0.0 copy-start.3
  6.5 4.9 %fusion.44 = (bf16[2048,256]{1,0:T(8,128)(2,1)S(1)}, bf16[2048,256]{1,0:T(8,128)(2,1)S(1)}, bf16[2048,256]{1,0:T(8,128)(2,1)S(1)}, bf16[2048,256]{1,0:T(8,128)(2...) fusion(bf16[2048,2048]{1,0:T(8,128)(2,1)} %param.7), kind=kLoop, calls=%fused_computation.82 | loop fusion | bytes 16777216 | tf_op jit(solution)/shard_map/slice | solution.py:126
  11.5 0.9 copy-done.3
  12.4 9.0 %fusion.28 = bf16[1601,1024]{1,0:T(8,128)(2,1)} fusion(bf16[1,1601,2048]{2,1,0:T(8,128)(2,1)S(1)} %copy-done.3, bf16[2048,256]{1,0:T(8,128)(2,1)S(1)} %get-tuple-element.13, bf16[2048,256]{1,0:T(8,128)(2,1)S(1)} %get-tuple-element.14, bf16[2048,256]{1,0:T(8,128)(2,1)S(1)} %get-tuple-element.8, bf16[2048,256]{1,0:T(8,128)(2,1)S(1)} %get-tuple-element.9), kind=kOutput, calls=%fused_computation.26 | convolution fusion | flops 6733497344 | bytes 14030848 | tf_op jit(solution)/shard_map/dot_general | solution.py:132
  21.4 0.0 reduce-scatter.5.cloned.1.call-update
  21.4 0.0 reduce-scatter.3.cloned.1.call-start
  21.5 0.0 copy-start.2
  21.5 12.0 %fusion.33 = bf16[1601,1024]{1,0:T(8,128)(2,1)} fusion(bf16[1,1601,2048]{2,1,0:T(8,128)(2,1)} %param.6, bf16[2048,256]{1,0:T(8,128)(2,1)S(1)} %get-tuple-element.10, bf16[2048,256]{1,0:T(8,128)(2,1)S(1)} %get-tuple-element.11, bf16[2048,256]{1,0:T(8,128)(2,1)} %get-tuple-element.12, bf16[2048,256]{1,0:T(8,128)(2,1)S(1)} %get-tuple-element.7), kind=kOutput, calls=%fused_computation.27 | convolution fusion | flops 6733497344 | bytes 14030848 | tf_op jit(solution)/shard_map/dot_general | solution.py:132
  33.5 0.0 reduce-scatter.3.cloned.1.call-update
  33.5 0.0 copy-done.2
  33.5 1.1 reduce-window.11
  34.7 0.2 slice_reduce_fusion
  34.9 0.1 fusion.40
  35.1 0.7 copy.7
  35.8 5.2 %all-to-all-start = ((s32[8,1,1]{2,1,0:T(1,128)}), s32[8,1,1]{2,1,0:T(1,128)S(1)}, u32[]{:S(2)}, u32[]{:S(2)}) async-start(s32[8,1,1]{2,1,0:T(1,128)} %copy.7), calls=%async_computation | async-start | bytes 8192 | tf_op jit(solution)/shard_map/all_to_all | solution.py:99
  41.0 7.3 %scatter_custom_fusion = bf16[1024,2048]{1,0:T(8,128)(2,1)} fusion(s32[512]{0:T(512)S(1)} %bitcast.82, bf16[512,2048]{1,0:T(8,128)(2,1)} %param.4, bf16[]{:T(256)} %constant.63.clone.1), kind=kCustom, calls=%fused_computation.29 | custom fusion | bytes 4194816 | tf_op jit(solution)/shard_map/scatter | solution.py:95
  48.3 0.0 all-to-all-done
  48.3 4.5 %all-to-all-start.1 = ((bf16[8,128,2048]{2,1,0:T(8,128)(2,1)}), bf16[8,128,2048]{2,1,0:T(8,128)(2,1)}, u32[]{:S(2)}, u32[]{:S(2)}) async-start(bf16[8,128,2048]{2,1,0:T(8,128)(2,1)} %bitcast.66), calls=%async_computation.1 | async-start | bytes 8388608 | tf_op jit(solution)/shard_map/all_to_all | solution.py:120
  52.8 0.2 reduce
  53.1 0.2 reduce-window.10
  53.3 0.6 slice.46
  54.5 0.6 fusion.45
  55.1 4.4 %compare_select_fusion.13 = s32[1024,1]{0,1:T(1,128)S(1)} fusion(s32[]{:T(128)} %bitcast.27, s32[]{:T(128)} %bitcast.28, s32[]{:T(128)} %bitcast.29, s32[]{:T(128)} %bitcast.30, s32[]{:T(128)} %bitcast.31, s32[]{:T(128)} %bitcast.33, s32[]{:T(128)} %bitcast.32), kind=kLoop, calls=%fused_computation.57 | loop fusion | flops 23552 | bytes 4124 | tf_op jit(solution)/shard_map/gather | solution.py:112
  59.6 0.7 fusion.46
  60.2 0.1 convert_reduce_fusion
  60.4 4.4 %compare_select_fusion.4 = (s32[1024,1]{0,1:T(1,128)S(1)}, s32[1024,1]{0,1:T(1,128)S(1)}) fusion(s32[]{:T(128)} %bitcast.14, s32[]{:T(128)} %bitcast.15, s32[]{:T(128)} %bitcast.16, s32[]{:T(128)} %bitcast.17, s32[]{:T(128)} %bitcast.18, s32[]{:T(128)} %bitcast.20, s32[]{:T(128)} %bitcast.19, s32[1024,1]{0,1:T(1,128)S(1)} %bitcast.70), kind=kLoop, calls=%fused_computation.46 | loop fusion | flops 38912 | bytes 12316 | tf_op jit(solution)/shard_map/gather | solution.py:108
  64.8 0.7 broadcast_select_fusion.2
  65.5 0.7 compare_select_fusion.2
  66.2 1.3 broadcast_select_fusion.1
  67.5 34.4 %all-to-all-done.1 = bf16[8,128,2048]{2,1,0:T(8,128)(2,1)} async-done(((bf16[8,128,2048]{2,1,0:T(8,128)(2,1)}), bf16[8,128,2048]{2,1,0:T(8,128)(2,1)}, u32[]{:S(2)}, u32[]{:S(2)}) %all-to-all-start.1) | async-done | bytes 4194336 | tf_op jit(solution)/shard_map/all_to_all | solution.py:120
  101.9 11.6 %gather_fusion = bf16[1024,2048]{1,0:T(8,128)(2,1)} fusion(bf16[1024,2048]{1,0:T(8,128)(2,1)} %bitcast.10, s32[1024]{0:T(1024)S(1)} %broadcast_clamp_fusion.1), kind=kCustom, calls=%fused_computation | custom fusion | bytes 8392704 | tf_op jit(solution)/shard_map/gather | solution.py:121
  113.5 0.0 reduce-scatter.5.cloned.1.call-done.k_ref.v_ref
  113.5 0.0 copy-start
  113.5 1.1 copy-done
  114.6 19.2 %shard_map.47 = bf16[1024,1024]{1,0:T(8,128)(2,1)S(1)} custom-call(s32[1]{0:T(128)} %bitcast.3.tiles_ref, bf16[1024,2048]{1,0:T(8,128)(2,1)} %gather_fusion, bf16[1601,256]{1,0:T(8,128)(2,1)S(1)} %copy-done, bf16[1601,256]{1,0:T(8,128)(2,1)S(1)} %copy-done), custom_call_target="tpu_custom_call" | custom-call | flops 3357540352 | bytes 2916864 | tf_op jit(solution)/shard_map/pallas_call | solution.py:55
  133.8 5.3 %gather_fusion.3 = bf16[1024,1024]{1,0:T(8,128)(2,1)} fusion(bf16[1024,1024]{1,0:T(8,128)(2,1)S(1)} %shard_map.47, s32[1024]{0:T(1024)S(1)} %broadcast_clamp_fusion), kind=kCustom, calls=%fused_computation.3 | custom fusion | bytes 4198400 | tf_op jit(solution)/shard_map/gather | solution.py:140
  139.2 19.4 %all-to-all-start.3 = ((bf16[8,128,1024]{2,1,0:T(8,128)(2,1)}), bf16[8,128,1024]{2,1,0:T(8,128)(2,1)}, u32[]{:S(2)}, u32[]{:S(2)}) async-start(bf16[8,128,1024]{2,1,0:T(8,128)(2,1)} %bitcast.67), calls=%async_computation.5 | async-start | bytes 4194304 | tf_op jit(solution)/shard_map/all_to_all | solution.py:141
  158.6 0.0 reduce-scatter.3.cloned.1.call-done.k_ref.v_ref
  158.6 0.0 copy-start.1
  158.6 1.1 copy-done.1
  159.8 19.2 %shard_map.46 = bf16[1024,1024]{1,0:T(8,128)(2,1)S(1)} custom-call(s32[1]{0:T(128)} %bitcast.3.tiles_ref, bf16[1024,2048]{1,0:T(8,128)(2,1)} %gather_fusion, bf16[1601,256]{1,0:T(8,128)(2,1)S(1)} %copy-done.1, bf16[1601,256]{1,0:T(8,128)(2,1)S(1)} %copy-done.1), custom_call_target="tpu_custom_call" | custom-call | flops 3357540352 | bytes 2916864 | tf_op jit(solution)/shard_map/pallas_call | solution.py:55
  179.0 5.4 %gather_fusion.1 = bf16[1024,1024]{1,0:T(8,128)(2,1)} fusion(bf16[1024,1024]{1,0:T(8,128)(2,1)S(1)} %shard_map.46, s32[1024]{0:T(1024)S(1)} %broadcast_clamp_fusion), kind=kCustom, calls=%fused_computation.1 | custom fusion | bytes 4198400 | tf_op jit(solution)/shard_map/gather | solution.py:140
  184.4 1.1 all-to-all-done.3
  185.5 21.2 %all-to-all-start.2 = ((bf16[8,128,1024]{2,1,0:T(8,128)(2,1)}), bf16[8,128,1024]{2,1,0:T(8,128)(2,1)S(1)}, u32[]{:S(2)}, u32[]{:S(2)}) async-start(bf16[8,128,1024]{2,1,0:T(8,128)(2,1)} %bitcast.68), calls=%async_computation.3 | async-start | bytes 4194304 | tf_op jit(solution)/shard_map/all_to_all | solution.py:141
  206.7 4.6 %gather_fusion.4 = bf16[512,1024]{1,0:T(8,128)(2,1)S(1)} fusion(bf16[1024,1024]{1,0:T(8,128)(2,1)} %bitcast.43, s32[1024]{0:T(1024)S(1)} %pad_clamp_fusion), kind=kCustom, calls=%fused_computation.4 | custom fusion | bytes 2099200 | tf_op jit(solution)/shard_map/gather | solution.py:142
  211.3 22.0 %all-to-all-done.2 = bf16[8,128,1024]{2,1,0:T(8,128)(2,1)S(1)} async-done(((bf16[8,128,1024]{2,1,0:T(8,128)(2,1)}), bf16[8,128,1024]{2,1,0:T(8,128)(2,1)S(1)}, u32[]{:S(2)}, u32[]{:S(2)}) %all-to-all-start.2) | async-done | bytes 2097184 | tf_op jit(solution)/shard_map/all_to_all | solution.py:141
  233.3 2.8 %gather_fusion.2 = bf16[512,1024]{1,0:T(8,128)(2,1)} fusion(bf16[1024,1024]{1,0:T(8,128)(2,1)S(1)} %bitcast.65, s32[1024]{0:T(1024)S(1)} %pad_clamp_fusion), kind=kCustom, calls=%fused_computation.2 | custom fusion | bytes 2099200 | tf_op jit(solution)/shard_map/gather | solution.py:142
  236.0 2.7 %pad_maximum_fusion = bf16[512,2048]{1,0:T(8,128)(2,1)} fusion(bf16[512,1024]{1,0:T(8,128)(2,1)S(1)} %gather_fusion.4, bf16[512,1024]{1,0:T(8,128)(2,1)} %gather_fusion.2), kind=kLoop, calls=%fused_computation.28 | loop fusion | flops 4194304 | bytes 4194304 | tf_op jit(solution)/shard_map/concatenate | solution.py:143
  (12 shorter events, 0.1 us)
Async XLA Ops:
  6.5 107.0 %reduce-scatter.5.cloned.1.call-start = ((), (), s32[]{:S(2)}) async-start(), calls=%async_computation.7 | async-start | bytes 4116480 | tf_op jit(solution)/shard_map/reduce_scatter | solution.py:131
  6.5 5.9 %copy-start.3 = (bf16[1,1601,2048]{2,1,0:T(8,128)(2,1)S(1)}, bf16[1,1601,2048]{2,1,0:T(8,128)(2,1)}, u32[]{:S(2)}) copy-start(bf16[1,1601,2048]{2,1,0:T(8,128)(2,1)} %param.6) | copy-start | bytes 19673092
  21.4 137.2 %reduce-scatter.3.cloned.1.call-start = ((), (), s32[]{:S(2)}) async-start(), calls=%async_computation.6 | async-start | bytes 4116480 | tf_op jit(solution)/shard_map/reduce_scatter | solution.py:131
  21.5 12.0 %copy-start.2 = (s32[512,1]{0,1:T(1,128)S(1)}, s32[512,1]{0,1:T(1,128)}, u32[]{:S(2)}) copy-start(s32[512,1]{0,1:T(1,128)} %param.5) | copy-start | bytes 6148
  35.8 12.5 %all-to-all-start = ((s32[8,1,1]{2,1,0:T(1,128)}), s32[8,1,1]{2,1,0:T(1,128)S(1)}, u32[]{:S(2)}, u32[]{:S(2)}) async-start(s32[8,1,1]{2,1,0:T(1,128)} %copy.7), calls=%async_computation | async-start | bytes 8192 | tf_op jit(solution)/shard_map/all_to_all | solution.py:99
  48.3 53.6 %all-to-all-start.1 = ((bf16[8,128,2048]{2,1,0:T(8,128)(2,1)}), bf16[8,128,2048]{2,1,0:T(8,128)(2,1)}, u32[]{:S(2)}, u32[]{:S(2)}) async-start(bf16[8,128,2048]{2,1,0:T(8,128)(2,1)} %bitcast.66), calls=%async_computation.1 | async-start | bytes 8388608 | tf_op jit(solution)/shard_map/all_to_all | solution.py:120
  113.5 1.1 copy-start
  139.2 46.3 %all-to-all-start.3 = ((bf16[8,128,1024]{2,1,0:T(8,128)(2,1)}), bf16[8,128,1024]{2,1,0:T(8,128)(2,1)}, u32[]{:S(2)}, u32[]{:S(2)}) async-start(bf16[8,128,1024]{2,1,0:T(8,128)(2,1)} %bitcast.67), calls=%async_computation.5 | async-start | bytes 4194304 | tf_op jit(solution)/shard_map/all_to_all | solution.py:141
  158.6 1.1 copy-start.1
  185.5 47.8 %all-to-all-start.2 = ((bf16[8,128,1024]{2,1,0:T(8,128)(2,1)}), bf16[8,128,1024]{2,1,0:T(8,128)(2,1)S(1)}, u32[]{:S(2)}, u32[]{:S(2)}) async-start(bf16[8,128,1024]{2,1,0:T(8,128)(2,1)} %bitcast.68), calls=%async_computation.3 | async-start | bytes 4194304 | tf_op jit(solution)/shard_map/all_to_all | solution.py:141
Sparse Core Ops, SparseCore 0:
  21.6 65.5 reduce-scatter.4
  89.5 62.8 reduce-scatter.2

commit v9 on v5

--- a/solution.py
+++ b/solution.py
@@ -13,21 +13,15 @@
 ROW_TILE = 256
 
 
-def attend_kernel(scale, group, head_dim, tiles_ref, q_ref, k_ref, v_ref, o_ref):
+def attend_kernel(group, head_dim, tiles_ref, q_ref, k_ref, v_ref, o_ref):
     @pl.when(pl.program_id(0) < tiles_ref[0])
     def _():
         keys = k_ref[...]
         values = v_ref[...]
         for head in range(group):
             columns = slice(head * head_dim, (head + 1) * head_dim)
-            scores = (
-                lax.dot_general(
-                    q_ref[:, columns],
-                    keys,
-                    (((1,), (1,)), ((), ())),
-                    preferred_element_type=jnp.float32,
-                )
-                * scale
+            scores = lax.dot_general(
+                q_ref[:, columns], keys, (((1,), (1,)), ((), ())), preferred_element_type=jnp.float32
             )
             row_max = jnp.max(scores, axis=1, keepdims=True)
             weights_exp = jnp.exp(scores - row_max)
@@ -42,14 +36,13 @@
     width = group * head_dim
     image_len = key_values.shape[0]
     assert rows % tile == 0 and first_head % group == 0
-    scale = head_dim ** (-0.5)
     flops = 4 * rows * group * image_len * head_dim
 
     def row_block(i, tiles):
         return jnp.minimum(i, tiles[0] - 1)
 
     return pl.pallas_call(
-        functools.partial(attend_kernel, scale, group, head_dim),
+        functools.partial(attend_kernel, group, head_dim),
         out_shape=jax.ShapeDtypeStruct((rows, width), jnp.bfloat16),
         grid_spec=pltpu.PrefetchScalarGridSpec(
             num_scalar_prefetch=1,
@@ -117,7 +110,10 @@
     )
     kv_width = 2 * HEAD_DIM
     received = lax.all_to_all(outgoing, "seq", split_axis=0, concat_axis=0, tiled=True)
-    packed_rows = received.reshape(-1, width_cols)[packed_slot]
+    score_scale = HEAD_DIM ** (-0.5)
+    packed_rows = (
+        received.reshape(-1, width_cols)[packed_slot].astype(jnp.float32) * score_scale
+    ).astype(jnp.bfloat16)
     pieces = []
     for head in range(local_kv):
         key_values = lax.psum_scatter(

time: 234 us -> 233 us (level)
  other arithmetic: 21.1 us -> 26.7 us
  waiting for transfers between devices: 70.3 us -> 66.6 us
  Pallas kernels: 27.7 us -> 25.3 us
    convert_element_type x0 -> x1, other arithmetic: none -> 5.54 us  [on_device(): packed_rows = (received.reshape(-1, width_cols)[packed_slot].astype(jnp.f...]
    reduce_scatter x2, waiting for transfers between devices: 13.8 us -> 10.2 us  [on_device(): lax.psum_scatter(jnp.concatenate([projected[:, (dest * local_kv + head) *...]
    pallas_call x2, Pallas kernels: 27.7 us -> 25.3 us  [attend(): pl.pallas_call(functools.partial(attend_kernel, group, head_dim), out_sha...]
  transfers between devices with their start and end apart: 6 -> 6, of which waited for: 3 -> 3; matrix products, arithmetic and copies ran while one was open for 23% -> 25% of each run, Pallas kernels for 12% -> 11%
where the time goes in v9:
time: 233 us; the launch traced here: 232 us
  waiting for transfers between devices  66.6 us (29%)
  local copies, waits for them, and re-layouts  42.4 us (18%)
  starting transfers between devices  38.5 us (17%)
  other arithmetic  26.7 us (11%)
  Pallas kernels  25.3 us (11%)
  matrix products  18 us (8%)
  between operations  14.2 us (6%)
    all_to_all x1, waiting for transfers between devices, on_device(): lax.all_to_all(outgoing, 'seq', split_axis=0, concat_axis=0, tiled=True)  34.4 us
    all_to_all x2, starting transfers between devices, on_device(): lax.all_to_all(answered, 'seq', split_axis=0, concat_axis=0, tiled=True)  28.5 us
    pallas_call x2, Pallas kernels, attend(): pl.pallas_call(functools.partial(attend_kernel, group, head_dim), out_sha...  25.3 us
    all_to_all x2, waiting for transfers between devices, on_device(): lax.all_to_all(answered, 'seq', split_axis=0, concat_axis=0, tiled=True)  22 us
    dot_general x1, matrix products, on_device(): jnp.dot(image_block, kv_weight, preferred_element_type=jnp.float32)  18 us
    gather x1, local copies, waits for them, and re-layouts, on_device(): received.reshape(-1, width_cols)[packed_slot].astype(jnp.float32)  11.6 us
    gather x2, local copies, waits for them, and re-layouts, on_device(): answered = answered[slot_packed].reshape(seq_devices, capacity, -1)  10.7 us
    reduce_scatter x2, waiting for transfers between devices, on_device(): lax.psum_scatter(jnp.concatenate([projected[:, (dest * local_kv + head) *...  10.2 us
  transfers between devices with their start and end apart: 6, of which 3 were waited for; matrix products, arithmetic and copies ran while one was open for 25% of the time, Pallas kernels for 11%

profile of v9, /device:TPU:0, one launch (start us, length us, event | category | flops | bytes accessed | tf_op | source)
XLA Modules:
  0.0 231.6 jit_solution(11446188302342316953)
XLA Ops:
  6.5 0.0 reduce-scatter.3.cloned.1.call-start
  6.5 18.0 %convolution_convert_fusion = bf16[1601,2048]{1,0:T(8,128)(2,1)S(1)} fusion(bf16[2048,2048]{1,0:T(8,128)(2,1)} %param.7, bf16[1,1601,2048]{2,1,0:T(8,128)(2,1)} %param.6), kind=kOutput, calls=%fused_computation.7 | convolution fusion | flops 13433440256 | bytes 21504000 | tf_op jit(solution)/shard_map/dot_general | solution.py:108
  24.5 0.4 fusion.5
  24.9 2.5 %pad_maximum_fusion = bf16[1601,1024]{1,0:T(8,128)(2,1)} fusion(bf16[1601,256]{1,0:T(8,128)(2,1)S(1)} %get-tuple-element.12, bf16[1601,256]{1,0:T(8,128)(2,1)S(1)} %get-tuple-element.13, bf16[1601,256]{1,0:T(8,128)(2,1)S(1)} %get-tuple-element.14, bf16[1601,256]{1,0:T(8,128)(2,1)S(1)} %get-tuple-element.7), kind=kLoop, calls=%fused_computation.9 | loop fusion | flops 13115392 | bytes 6557696 | tf_op jit(solution)/shard_map/concatenate | solution.py:120
  27.4 0.0 reduce-scatter.3.cloned.1.call-update
  27.4 0.0 reduce-scatter.5.cloned.1.call-start
  27.5 0.0 copy-start.2
  27.5 2.5 %pad_maximum_fusion.1 = bf16[1601,1024]{1,0:T(8,128)(2,1)} fusion(bf16[1601,256]{1,0:T(8,128)(2,1)S(1)} %get-tuple-element.8, bf16[1601,256]{1,0:T(8,128)(2,1)S(1)} %get-tuple-element.9, bf16[1601,256]{1,0:T(8,128)(2,1)S(1)} %get-tuple-element.10, bf16[1601,256]{1,0:T(8,128)(2,1)S(1)} %get-tuple-element.11), kind=kLoop, calls=%fused_computation.10 | loop fusion | flops 13115392 | bytes 6557696 | tf_op jit(solution)/shard_map/concatenate | solution.py:120
  30.0 0.0 reduce-scatter.5.cloned.1.call-update
  30.0 0.0 copy-done.2
  30.0 1.1 reduce-window.11
  31.2 0.2 slice_reduce_fusion
  31.4 0.1 fusion.3
  31.6 0.7 copy.7
  32.3 5.2 %all-to-all-start = ((s32[8,1,1]{2,1,0:T(1,128)}), s32[8,1,1]{2,1,0:T(1,128)S(1)}, u32[]{:S(2)}, u32[]{:S(2)}) async-start(s32[8,1,1]{2,1,0:T(1,128)} %copy.7), calls=%async_computation | async-start | bytes 8192 | tf_op jit(solution)/shard_map/all_to_all | solution.py:88
  37.5 7.3 %scatter_custom_fusion = bf16[1024,2048]{1,0:T(8,128)(2,1)} fusion(s32[512]{0:T(512)S(1)} %bitcast.69, bf16[512,2048]{1,0:T(8,128)(2,1)} %param.4, bf16[]{:T(256)} %constant.64.clone.1), kind=kCustom, calls=%fused_computation.12 | custom fusion | bytes 4194816 | tf_op jit(solution)/shard_map/scatter | solution.py:84
  44.7 0.0 all-to-all-done
  44.7 4.7 %all-to-all-start.1 = ((bf16[8,128,2048]{2,1,0:T(8,128)(2,1)}), bf16[8,128,2048]{2,1,0:T(8,128)(2,1)}, u32[]{:S(2)}, u32[]{:S(2)}) async-start(bf16[8,128,2048]{2,1,0:T(8,128)(2,1)} %bitcast.53), calls=%async_computation.1 | async-start | bytes 8388608 | tf_op jit(solution)/shard_map/all_to_all | solution.py:112
  49.5 0.2 reduce
  49.7 0.2 reduce-window.10
  49.9 0.6 slice.46
  51.2 0.6 fusion.6
  51.8 4.4 %compare_select_fusion.13 = s32[1024,1]{0,1:T(1,128)S(1)} fusion(s32[]{:T(128)} %bitcast.26, s32[]{:T(128)} %bitcast.27, s32[]{:T(128)} %bitcast.28, s32[]{:T(128)} %bitcast.29, s32[]{:T(128)} %bitcast.30, s32[]{:T(128)} %bitcast.32, s32[]{:T(128)} %bitcast.31), kind=kLoop, calls=%fused_computation.40 | loop fusion | flops 23552 | bytes 4124 | tf_op jit(solution)/shard_map/gather | solution.py:101
  56.2 0.7 fusion.7
  56.9 0.1 convert_reduce_fusion
  57.0 4.4 %compare_select_fusion.4 = (s32[1024,1]{0,1:T(1,128)S(1)}, s32[1024,1]{0,1:T(1,128)S(1)}) fusion(s32[]{:T(128)} %bitcast.14, s32[]{:T(128)} %bitcast.15, s32[]{:T(128)} %bitcast.16, s32[]{:T(128)} %bitcast.17, s32[]{:T(128)} %bitcast.18, s32[]{:T(128)} %bitcast.20, s32[]{:T(128)} %bitcast.19, s32[1024,1]{0,1:T(1,128)S(1)} %bitcast.57), kind=kLoop, calls=%fused_computation.29 | loop fusion | flops 38912 | bytes 12316 | tf_op jit(solution)/shard_map/gather | solution.py:97
  61.4 0.7 broadcast_select_fusion.2
  62.1 0.7 compare_select_fusion.2
  62.8 1.3 broadcast_select_fusion.1
  64.2 34.4 %all-to-all-done.1 = bf16[8,128,2048]{2,1,0:T(8,128)(2,1)} async-done(((bf16[8,128,2048]{2,1,0:T(8,128)(2,1)}), bf16[8,128,2048]{2,1,0:T(8,128)(2,1)}, u32[]{:S(2)}, u32[]{:S(2)}) %all-to-all-start.1) | async-done | bytes 4194336 | tf_op jit(solution)/shard_map/all_to_all | solution.py:112
  98.6 11.6 %gather_fusion = bf16[1024,2048]{1,0:T(8,128)(2,1)} fusion(bf16[1024,2048]{1,0:T(8,128)(2,1)} %bitcast.10, s32[1024]{0:T(1024)S(1)} %broadcast_clamp_fusion.1), kind=kCustom, calls=%fused_computation | custom fusion | bytes 8392704 | tf_op jit(solution)/shard_map/gather | solution.py:115
  110.1 5.5 %multiply_convert_fusion.q_ref = bf16[1024,2048]{1,0:T(8,128)(2,1)} fusion(bf16[1024,2048]{1,0:T(8,128)(2,1)} %gather_fusion), kind=kLoop, calls=%fused_computation.6 | loop fusion | flops 6291456 | bytes 8388608 | tf_op jit(solution)/shard_map/convert_element_type | solution.py:116
  115.7 0.0 reduce-scatter.3.cloned.1.call-done.k_ref.v_ref
  115.7 0.0 copy-start
  115.7 1.1 copy-done
  116.8 12.6 %shard_map.46 = bf16[1024,1024]{1,0:T(8,128)(2,1)S(1)} custom-call(s32[1]{0:T(128)} %bitcast.3.tiles_ref, bf16[1024,2048]{1,0:T(8,128)(2,1)} %multiply_convert_fusion.q_ref, bf16[1601,256]{1,0:T(8,128)(2,1)S(1)} %copy-done, bf16[1601,256]{1,0:T(8,128)(2,1)S(1)} %copy-done), custom_call_target="tpu_custom_call" | custom-call | flops 3357540352 | bytes 2916864 | tf_op jit(solution)/shard_map/pallas_call | solution.py:44
  129.5 5.4 %gather_fusion.1 = bf16[1024,1024]{1,0:T(8,128)(2,1)} fusion(bf16[1024,1024]{1,0:T(8,128)(2,1)S(1)} %shard_map.46, s32[1024]{0:T(1024)S(1)} %broadcast_clamp_fusion), kind=kCustom, calls=%fused_computation.1 | custom fusion | bytes 4198400 | tf_op jit(solution)/shard_map/gather | solution.py:132
  134.9 13.4 %all-to-all-start.2 = ((bf16[8,128,1024]{2,1,0:T(8,128)(2,1)}), bf16[8,128,1024]{2,1,0:T(8,128)(2,1)}, u32[]{:S(2)}, u32[]{:S(2)}) async-start(bf16[8,128,1024]{2,1,0:T(8,128)(2,1)} %bitcast.54), calls=%async_computation.3 | async-start | bytes 4194304 | tf_op jit(solution)/shard_map/all_to_all | solution.py:133
  148.3 10.2 %reduce-scatter.5.cloned.1.call-done.k_ref.v_ref = bf16[1601,256]{1,0:T(8,128)(2,1)} async-done(((bf16[1601,1024]{1,0:T(8,128)(2,1)}), bf16[1601,256]{1,0:T(8,128)(2,1)}) %reduce-scatter.5.cloned.1.call-update) | async-done | bytes 819728 | tf_op jit(solution)/shard_map/reduce_scatter | solution.py:119
  158.4 0.0 copy-start.1
  158.4 1.1 copy-done.1
  159.6 12.6 %shard_map.47 = bf16[1024,1024]{1,0:T(8,128)(2,1)S(1)} custom-call(s32[1]{0:T(128)} %bitcast.3.tiles_ref, bf16[1024,2048]{1,0:T(8,128)(2,1)} %multiply_convert_fusion.q_ref, bf16[1601,256]{1,0:T(8,128)(2,1)S(1)} %copy-done.1, bf16[1601,256]{1,0:T(8,128)(2,1)S(1)} %copy-done.1), custom_call_target="tpu_custom_call" | custom-call | flops 3357540352 | bytes 2916864 | tf_op jit(solution)/shard_map/pallas_call | solution.py:44
  172.2 5.3 %gather_fusion.3 = bf16[1024,1024]{1,0:T(8,128)(2,1)} fusion(bf16[1024,1024]{1,0:T(8,128)(2,1)S(1)} %shard_map.47, s32[1024]{0:T(1024)S(1)} %broadcast_clamp_fusion), kind=kCustom, calls=%fused_computation.3 | custom fusion | bytes 4198400 | tf_op jit(solution)/shard_map/gather | solution.py:132
  177.5 0.0 all-to-all-done.2
  177.5 15.1 %all-to-all-start.3 = ((bf16[8,128,1024]{2,1,0:T(8,128)(2,1)}), bf16[8,128,1024]{2,1,0:T(8,128)(2,1)S(1)}, u32[]{:S(2)}, u32[]{:S(2)}) async-start(bf16[8,128,1024]{2,1,0:T(8,128)(2,1)} %bitcast.55), calls=%async_computation.5 | async-start | bytes 4194304 | tf_op jit(solution)/shard_map/all_to_all | solution.py:133
  192.7 4.6 %gather_fusion.2 = bf16[512,1024]{1,0:T(8,128)(2,1)S(1)} fusion(bf16[1024,1024]{1,0:T(8,128)(2,1)} %bitcast.39, s32[1024]{0:T(1024)S(1)} %pad_clamp_fusion), kind=kCustom, calls=%fused_computation.2 | custom fusion | bytes 2099200 | tf_op jit(solution)/shard_map/gather | solution.py:134
  197.3 22.0 %all-to-all-done.3 = bf16[8,128,1024]{2,1,0:T(8,128)(2,1)S(1)} async-done(((bf16[8,128,1024]{2,1,0:T(8,128)(2,1)}), bf16[8,128,1024]{2,1,0:T(8,128)(2,1)S(1)}, u32[]{:S(2)}, u32[]{:S(2)}) %all-to-all-start.3) | async-done | bytes 2097184 | tf_op jit(solution)/shard_map/all_to_all | solution.py:133
  219.3 2.8 %gather_fusion.4 = bf16[512,1024]{1,0:T(8,128)(2,1)} fusion(bf16[1024,1024]{1,0:T(8,128)(2,1)S(1)} %bitcast.52, s32[1024]{0:T(1024)S(1)} %pad_clamp_fusion), kind=kCustom, calls=%fused_computation.4 | custom fusion | bytes 2099200 | tf_op jit(solution)/shard_map/gather | solution.py:134
  222.0 2.8 %pad_maximum_fusion.2 = bf16[512,2048]{1,0:T(8,128)(2,1)} fusion(bf16[512,1024]{1,0:T(8,128)(2,1)} %gather_fusion.4, bf16[512,1024]{1,0:T(8,128)(2,1)S(1)} %gather_fusion.2), kind=kLoop, calls=%fused_computation.11 | loop fusion | flops 4194304 | bytes 4194304 | tf_op jit(solution)/shard_map/concatenate | solution.py:135
  (12 shorter events, 0.1 us)
Async XLA Ops:
  6.5 109.1 %reduce-scatter.3.cloned.1.call-start = ((), (), s32[]{:S(2)}) async-start(), calls=%async_computation.6 | async-start | bytes 4116480 | tf_op jit(solution)/shard_map/reduce_scatter | solution.py:119
  27.4 131.0 %reduce-scatter.5.cloned.1.call-start = ((), (), s32[]{:S(2)}) async-start(), calls=%async_computation.7 | async-start | bytes 4116480 | tf_op jit(solution)/shard_map/reduce_scatter | solution.py:119
  27.5 2.5 %copy-start.2 = (s32[512,1]{0,1:T(1,128)S(1)}, s32[512,1]{0,1:T(1,128)}, u32[]{:S(2)}) copy-start(s32[512,1]{0,1:T(1,128)} %param.5) | copy-start | bytes 6148
  32.3 12.5 %all-to-all-start = ((s32[8,1,1]{2,1,0:T(1,128)}), s32[8,1,1]{2,1,0:T(1,128)S(1)}, u32[]{:S(2)}, u32[]{:S(2)}) async-start(s32[8,1,1]{2,1,0:T(1,128)} %copy.7), calls=%async_computation | async-start | bytes 8192 | tf_op jit(solution)/shard_map/all_to_all | solution.py:88
  44.7 53.9 %all-to-all-start.1 = ((bf16[8,128,2048]{2,1,0:T(8,128)(2,1)}), bf16[8,128,2048]{2,1,0:T(8,128)(2,1)}, u32[]{:S(2)}, u32[]{:S(2)}) async-start(bf16[8,128,2048]{2,1,0:T(8,128)(2,1)} %bitcast.53), calls=%async_computation.1 | async-start | bytes 8388608 | tf_op jit(solution)/shard_map/all_to_all | solution.py:112
  115.7 1.1 copy-start
  134.9 42.7 %all-to-all-start.2 = ((bf16[8,128,1024]{2,1,0:T(8,128)(2,1)}), bf16[8,128,1024]{2,1,0:T(8,128)(2,1)}, u32[]{:S(2)}, u32[]{:S(2)}) async-start(bf16[8,128,1024]{2,1,0:T(8,128)(2,1)} %bitcast.54), calls=%async_computation.3 | async-start | bytes 4194304 | tf_op jit(solution)/shard_map/all_to_all | solution.py:133
  158.4 1.1 copy-start.1
  177.5 41.7 %all-to-all-start.3 = ((bf16[8,128,1024]{2,1,0:T(8,128)(2,1)}), bf16[8,128,1024]{2,1,0:T(8,128)(2,1)S(1)}, u32[]{:S(2)}, u32[]{:S(2)}) async-start(bf16[8,128,1024]{2,1,0:T(8,128)(2,1)} %bitcast.55), calls=%async_computation.5 | async-start | bytes 4194304 | tf_op jit(solution)/shard_map/all_to_all | solution.py:133
Sparse Core Ops, SparseCore 0:
  27.6 65.5 reduce-scatter.2
  95.5 62.8 reduce-scatter.4

commit v10 on v9

v10 whole, which is shorter than its diff:
```python
import functools

import jax
import jax.numpy as jnp
from jax import lax
from jax.experimental import pallas as pl
from jax.experimental.pallas import tpu as pltpu
from jax.sharding import PartitionSpec as P

HEADS = 64
KV_HEADS = 8
HEAD_DIM = 128
ROW_TILE = 256


def attend_kernel(group, head_dim, q_ref, k_ref, v_ref, o_ref):
    if True:
        keys = k_ref[...]
        values = v_ref[...]
        for head in range(group):
            columns = slice(head * head_dim, (head + 1) * head_dim)
            scores = lax.dot_general(
                q_ref[:, columns], keys, (((1,), (1,)), ((), ())), preferred_element_type=jnp.float32
            )
            row_max = jnp.max(scores, axis=1, keepdims=True)
            weights_exp = jnp.exp(scores - row_max)
            totals = jnp.sum(weights_exp, axis=1, keepdims=True)
            probs = weights_exp.astype(jnp.bfloat16)
            weighted = jnp.dot(probs, values, preferred_element_type=jnp.float32)
            o_ref[:, columns] = (weighted / totals).astype(o_ref.dtype)


def attend(query_rows, key_values, group, head_dim, first_head, tile):
    rows = query_rows.shape[0]
    width = group * head_dim
    image_len = key_values.shape[0]
    assert rows % tile == 0 and first_head % group == 0
    flops = 4 * rows * group * image_len * head_dim
    return pl.pallas_call(
        functools.partial(attend_kernel, group, head_dim),
        out_shape=jax.ShapeDtypeStruct((rows, width), jnp.bfloat16),
        grid=(rows // tile,),
        in_specs=[
            pl.BlockSpec((tile, width), lambda i: (i, first_head // group)),
            pl.BlockSpec((image_len, head_dim), lambda i: (0, 0)),
            pl.BlockSpec((image_len, head_dim), lambda i: (0, 1)),
        ],
        out_specs=pl.BlockSpec((tile, width), lambda i: (i, 0)),
        compiler_params=pltpu.CompilerParams(
            dimension_semantics=("arbitrary",),
            vmem_limit_bytes=48 * 1024 * 1024,
        ),
        cost_estimate=pl.CostEstimate(
            flops=flops,
            transcendentals=rows * group * image_len,
            bytes_accessed=2 * (2 * rows * width + key_values.size),
        ),
    )(query_rows, key_values, key_values)


def on_device(queries, image_refs, features, kv_weight):
    seq_devices = lax.axis_size("seq")
    token_count = queries.shape[0]
    width_cols = queries.shape[1]
    capacity = 2 * token_count // seq_devices
    rows = seq_devices * capacity
    tile = min(ROW_TILE, rows)
    owners = image_refs[:, 0]
    onehot = (owners[:, None] == jnp.arange(seq_devices, dtype=jnp.int32)[None, :]).astype(
        jnp.int32
    )
    running = jnp.cumsum(onehot, axis=0)
    position = jnp.sum(onehot * (running - 1), axis=1)
    slot_index = owners * capacity + position
    outgoing = (
        jnp.zeros((rows, width_cols), jnp.bfloat16).at[slot_index].set(queries)
    )
    outgoing = outgoing.reshape(seq_devices, capacity, width_cols)
    group = HEADS // KV_HEADS
    image_block = features[0]
    tensor_devices = lax.axis_size("tensor")
    local_kv = KV_HEADS // tensor_devices
    projected = jnp.dot(image_block, kv_weight, preferred_element_type=jnp.float32).astype(
        jnp.bfloat16
    )
    kv_width = 2 * HEAD_DIM
    received = lax.all_to_all(outgoing, "seq", split_axis=0, concat_axis=0, tiled=True)
    score_scale = HEAD_DIM ** (-0.5)
    scaled_rows = (received.reshape(-1, width_cols).astype(jnp.float32) * score_scale).astype(
        jnp.bfloat16
    )
    result = None
    for head in range(local_kv):
        key_values = lax.psum_scatter(
            jnp.concatenate(
                [
                    projected[:, (dest * local_kv + head) * kv_width :][:, :kv_width]
                    for dest in range(tensor_devices)
                ],
                axis=1,
            ),
            "tensor",
            scatter_dimension=1,
            tiled=True,
        )
        answered = attend(scaled_rows, key_values, group, HEAD_DIM, head * group, tile)
        answered = answered.reshape(seq_devices, capacity, -1)
        returned = lax.all_to_all(answered, "seq", split_axis=0, concat_axis=0, tiled=True)
        piece = returned.reshape(rows, -1)[slot_index]
        if result is None:
            result = jnp.zeros((token_count, width_cols), jnp.bfloat16)
        result = lax.dynamic_update_slice(result, piece, (0, head * piece.shape[1]))
    return result


def solution(mesh):
    placed = (P("seq", "tensor"), P("seq", None), P("seq", None, "tensor"), P("tensor", None))
    return jax.shard_map(
        on_device, mesh=mesh, in_specs=placed, out_specs=P("seq", "tensor"), check_vma=False
    )
```

time: 233 us -> 229 us (0.983)
  blocking collectives: 0 us -> 54.2 us
  starting transfers between devices: 38.5 us -> 8.22 us
  local copies, waits for them, and re-layouts: 42.4 us -> 16.8 us
  Pallas kernels: 25.3 us -> 49.8 us
  other arithmetic: 26.7 us -> 10.9 us
  waiting for transfers between devices: 66.6 us -> 57 us
    all_to_all x0 -> x1, blocking collectives: none -> 54.2 us  [on_device(): lax.all_to_all(outgoing, 'seq', split_axis=0, concat_axis=0, tiled=True)]
    all_to_all x2 -> x0, waiting for transfers between devices: 34.4 us -> none  [the longest x1 34.4 us: on_device(): lax.all_to_all(outgoing, 'seq', split_axis=0, concat_axis=0, tiled=True)]
    pallas_call x2, Pallas kernels: 25.3 us -> 49.8 us  [attend(): pl.pallas_call(functools.partial(attend_kernel, group, head_dim), out_sha...]
    gather x7 -> x2, local copies, waits for them, and re-layouts: 31 us -> 6.65 us  [on_device(): piece = returned.reshape(rows, -1)[slot_index]]
    reduce_scatter x2, waiting for transfers between devices: 10.2 us -> 32.4 us  [on_device(): lax.psum_scatter(jnp.concatenate([projected[:, (dest * local_kv + head) *...]
    all_to_all x2, starting transfers between devices: 28.5 us -> 8.17 us  [on_device(): lax.all_to_all(answered, 'seq', split_axis=0, concat_axis=0, tiled=True)]
    gather x9 -> x1, other arithmetic: 10.9 us -> 0.01 us  [on_device(): piece = returned.reshape(rows, -1)[slot_index]]
    all_to_all x2 -> x0, starting transfers between devices: 9.92 us -> none  [the longest x1 5.19 us: on_device(): lax.all_to_all(sent_counts, 'seq', split_axis=0, concat_axis=0, tiled=True)]
  transfers between devices with their start and end apart: 6 -> 4, of which waited for: 3 -> 2; matrix products, arithmetic and copies ran while one was open for 25% -> 7% of each run, Pallas kernels for 11% -> 22%
where the time goes in v10:
time: 229 us; the launch traced here: 228 us
  waiting for transfers between devices  57 us (25%)
  blocking collectives  54.2 us (24%)
  Pallas kernels  49.8 us (22%)
  matrix products  18 us (8%)
  local copies, waits for them, and re-layouts  16.8 us (7%)
  between operations  13.5 us (6%)
  other arithmetic  10.9 us (5%)
  starting transfers between devices  8.22 us (4%)
    all_to_all x1, blocking collectives, on_device(): lax.all_to_all(outgoing, 'seq', split_axis=0, concat_axis=0, tiled=True)  54.2 us
    pallas_call x2, Pallas kernels, attend(): pl.pallas_call(functools.partial(attend_kernel, group, head_dim), out_sha...  49.8 us
    reduce_scatter x2, waiting for transfers between devices, on_device(): lax.psum_scatter(jnp.concatenate([projected[:, (dest * local_kv + head) *...  32.4 us
    all_to_all x2, waiting for transfers between devices, on_device(): lax.all_to_all(answered, 'seq', split_axis=0, concat_axis=0, tiled=True)  24.5 us
    dot_general x1, matrix products, on_device(): jnp.dot(image_block, kv_weight, preferred_element_type=jnp.float32)  18 us
    all_to_all x2, starting transfers between devices, on_device(): lax.all_to_all(answered, 'seq', split_axis=0, concat_axis=0, tiled=True)  8.17 us
    scatter x1, local copies, waits for them, and re-layouts, on_device(): jnp.zeros((rows, width_cols), jnp.bfloat16).at[slot_index].set(queries)  7.21 us
    gather x2, local copies, waits for them, and re-layouts, on_device(): piece = returned.reshape(rows, -1)[slot_index]  6.65 us
  transfers between devices with their start and end apart: 4, of which 2 were waited for; matrix products, arithmetic and copies ran while one was open for 7% of the time, Pallas kernels for 22%

profile of v10, /device:TPU:0, one launch (start us, length us, event | category | flops | bytes accessed | tf_op | source)
XLA Modules:
  0.0 228.3 jit_solution(6306585270372706468)
XLA Ops:
  6.5 0.0 reduce-scatter.3.cloned.1.call-start
  6.5 18.0 %convolution_convert_fusion = bf16[1601,2048]{1,0:T(8,128)(2,1)S(1)} fusion(bf16[2048,2048]{1,0:T(8,128)(2,1)} %param.7, bf16[1,1601,2048]{2,1,0:T(8,128)(2,1)} %param.6), kind=kOutput, calls=%fused_computation.4 | convolution fusion | flops 13433440256 | bytes 21504000 | tf_op jit(solution)/shard_map/dot_general | solution.py:83
  24.5 0.4 fusion.5
  24.9 2.5 %pad_maximum_fusion = bf16[1601,1024]{1,0:T(8,128)(2,1)} fusion(bf16[1601,256]{1,0:T(8,128)(2,1)S(1)} %get-tuple-element.10, bf16[1601,256]{1,0:T(8,128)(2,1)S(1)} %get-tuple-element.11, bf16[1601,256]{1,0:T(8,128)(2,1)S(1)} %get-tuple-element.12, bf16[1601,256]{1,0:T(8,128)(2,1)S(1)} %get-tuple-element.5), kind=kLoop, calls=%fused_computation.6 | loop fusion | flops 13115392 | bytes 6557696 | tf_op jit(solution)/shard_map/concatenate | solution.py:95
  27.4 0.0 reduce-scatter.3.cloned.1.call-update
  27.5 0.0 reduce-scatter.5.cloned.1.call-start
  27.5 0.0 copy-start.2
  27.5 2.5 %pad_maximum_fusion.1 = bf16[1601,1024]{1,0:T(8,128)(2,1)} fusion(bf16[1601,256]{1,0:T(8,128)(2,1)S(1)} %get-tuple-element.6, bf16[1601,256]{1,0:T(8,128)(2,1)S(1)} %get-tuple-element.7, bf16[1601,256]{1,0:T(8,128)(2,1)S(1)} %get-tuple-element.8, bf16[1601,256]{1,0:T(8,128)(2,1)S(1)} %get-tuple-element.9), kind=kLoop, calls=%fused_computation.7 | loop fusion | flops 13115392 | bytes 6557696 | tf_op jit(solution)/shard_map/concatenate | solution.py:95
  30.0 0.0 reduce-scatter.5.cloned.1.call-update
  30.1 0.0 copy-done.2
  30.1 1.1 reduce-window.6
  31.2 0.2 slice_reduce_fusion
  31.5 0.1 fusion.3
  31.6 7.2 %scatter_custom_fusion = bf16[1024,2048]{1,0:T(8,128)(2,1)} fusion(s32[512]{0:T(512)S(1)} %bitcast.26, bf16[512,2048]{1,0:T(8,128)(2,1)} %param.4, bf16[]{:T(256)} %constant.6.clone.1), kind=kCustom, calls=%fused_computation.9 | custom fusion | bytes 4194816 | tf_op jit(solution)/shard_map/scatter | solution.py:76
  38.8 54.2 %all_to_all.15 = bf16[8,128,2048]{2,1,0:T(8,128)(2,1)S(1)} all-to-all(bf16[8,128,2048]{2,1,0:T(8,128)(2,1)} %bitcast.21), channel_id=1, replica_groups=mesh['seq'=8,'tensor'=4] {'seq'}, dimensions={0} | all-to-all | bytes 8388608 | tf_op jit(solution)/shard_map/all_to_all | solution.py:87
  93.0 3.1 %multiply_convert_fusion = bf16[8,128,2048]{2,1,0:T(8,128)(2,1)} fusion(bf16[8,128,2048]{2,1,0:T(8,128)(2,1)S(1)} %all_to_all.15), kind=kLoop, calls=%fused_computation.3 | loop fusion | flops 6291456 | bytes 8388608 | tf_op jit(solution)/shard_map/convert_element_type | solution.py:89
  96.1 0.0 reduce-scatter.3.cloned.1.call-done.k_ref.v_ref
  96.1 0.0 copy-start
  96.1 1.1 copy-done
  97.3 24.9 %shard_map.46 = bf16[1024,1024]{1,0:T(8,128)(2,1)} custom-call(bf16[1024,2048]{1,0:T(8,128)(2,1)} %bitcast.22, bf16[1601,256]{1,0:T(8,128)(2,1)S(1)} %copy-done, bf16[1601,256]{1,0:T(8,128)(2,1)S(1)} %copy-done), custom_call_target="tpu_custom_call" | custom-call | flops 6715080704 | bytes 5014016 | tf_op jit(solution)/shard_map/pallas_call | solution.py:39
  122.2 3.8 %all-to-all-start.1 = ((bf16[8,128,1024]{2,1,0:T(8,128)(2,1)}), bf16[8,128,1024]{2,1,0:T(8,128)(2,1)S(1)}, u32[]{:S(2)}, u32[]{:S(2)}) async-start(bf16[8,128,1024]{2,1,0:T(8,128)(2,1)} %bitcast.9), calls=%async_computation.2 | async-start | bytes 4194304 | tf_op jit(solution)/shard_map/all_to_all | solution.py:108
  126.0 32.4 %reduce-scatter.5.cloned.1.call-done.k_ref.v_ref = bf16[1601,256]{1,0:T(8,128)(2,1)} async-done(((bf16[1601,1024]{1,0:T(8,128)(2,1)}), bf16[1601,256]{1,0:T(8,128)(2,1)}) %reduce-scatter.5.cloned.1.call-update) | async-done | bytes 819728 | tf_op jit(solution)/shard_map/reduce_scatter | solution.py:94
  158.4 0.0 copy-start.1
  158.4 1.1 copy-done.1
  159.6 24.9 %shard_map.47 = bf16[1024,1024]{1,0:T(8,128)(2,1)} custom-call(bf16[1024,2048]{1,0:T(8,128)(2,1)} %bitcast.23, bf16[1601,256]{1,0:T(8,128)(2,1)S(1)} %copy-done.1, bf16[1601,256]{1,0:T(8,128)(2,1)S(1)} %copy-done.1), custom_call_target="tpu_custom_call" | custom-call | flops 6715080704 | bytes 5014016 | tf_op jit(solution)/shard_map/pallas_call | solution.py:39
  184.4 0.0 all-to-all-done.1
  184.4 4.3 %all-to-all-start.2 = ((bf16[8,128,1024]{2,1,0:T(8,128)(2,1)}), bf16[8,128,1024]{2,1,0:T(8,128)(2,1)}, u32[]{:S(2)}, u32[]{:S(2)}) async-start(bf16[8,128,1024]{2,1,0:T(8,128)(2,1)} %bitcast.11), calls=%async_computation.4 | async-start | bytes 4194304 | tf_op jit(solution)/shard_map/all_to_all | solution.py:108
  188.8 2.1 gather_fusion
  190.8 24.5 %all-to-all-done.2 = bf16[8,128,1024]{2,1,0:T(8,128)(2,1)} async-done(((bf16[8,128,1024]{2,1,0:T(8,128)(2,1)}), bf16[8,128,1024]{2,1,0:T(8,128)(2,1)}, u32[]{:S(2)}, u32[]{:S(2)}) %all-to-all-start.2) | async-done | bytes 2097184 | tf_op jit(solution)/shard_map/all_to_all | solution.py:108
  215.4 4.6 %gather_fusion.1 = bf16[512,1024]{1,0:T(8,128)(2,1)S(1)} fusion(bf16[1024,1024]{1,0:T(8,128)(2,1)} %bitcast.12, s32[1024]{0:T(1024)S(1)} %pad_clamp_fusion), kind=kCustom, calls=%fused_computation.1 | custom fusion | bytes 2099200 | tf_op jit(solution)/shard_map/gather | solution.py:109
  220.0 1.5 pad_maximum_fusion.2
  (5 shorter events, 0.1 us)
Async XLA Ops:
  6.5 89.6 %reduce-scatter.3.cloned.1.call-start = ((), (), s32[]{:S(2)}) async-start(), calls=%async_computation.5 | async-start | bytes 4116480 | tf_op jit(solution)/shard_map/reduce_scatter | solution.py:94
  27.5 131.0 %reduce-scatter.5.cloned.1.call-start = ((), (), s32[]{:S(2)}) async-start(), calls=%async_computation.6 | async-start | bytes 4116480 | tf_op jit(solution)/shard_map/reduce_scatter | solution.py:94
  27.5 2.6 %copy-start.2 = (s32[512,1]{0,1:T(1,128)S(1)}, s32[512,1]{0,1:T(1,128)}, u32[]{:S(2)}) copy-start(s32[512,1]{0,1:T(1,128)} %param.5) | copy-start | bytes 6148
  96.1 1.1 copy-start
  122.2 62.2 %all-to-all-start.1 = ((bf16[8,128,1024]{2,1,0:T(8,128)(2,1)}), bf16[8,128,1024]{2,1,0:T(8,128)(2,1)S(1)}, u32[]{:S(2)}, u32[]{:S(2)}) async-start(bf16[8,128,1024]{2,1,0:T(8,128)(2,1)} %bitcast.9), calls=%async_computation.2 | async-start | bytes 4194304 | tf_op jit(solution)/shard_map/all_to_all | solution.py:108
  158.4 1.1 copy-start.1
  184.4 31.0 %all-to-all-start.2 = ((bf16[8,128,1024]{2,1,0:T(8,128)(2,1)}), bf16[8,128,1024]{2,1,0:T(8,128)(2,1)}, u32[]{:S(2)}, u32[]{:S(2)}) async-start(bf16[8,128,1024]{2,1,0:T(8,128)(2,1)} %bitcast.11), calls=%async_computation.4 | async-start | bytes 4194304 | tf_op jit(solution)/shard_map/all_to_all | solution.py:108
Sparse Core Ops, SparseCore 0:
  27.6 65.5 reduce-scatter.2
  95.5 62.8 reduce-scatter.4

commit v11 on v10

--- a/solution.py
+++ b/solution.py
@@ -80,9 +80,6 @@
     image_block = features[0]
     tensor_devices = lax.axis_size("tensor")
     local_kv = KV_HEADS // tensor_devices
-    projected = jnp.dot(image_block, kv_weight, preferred_element_type=jnp.float32).astype(
-        jnp.bfloat16
-    )
     kv_width = 2 * HEAD_DIM
     received = lax.all_to_all(outgoing, "seq", split_axis=0, concat_axis=0, tiled=True)
     score_scale = HEAD_DIM ** (-0.5)
@@ -91,13 +88,16 @@
     )
     result = None
     for head in range(local_kv):
+        weight_part = jnp.concatenate(
+            [
+                kv_weight[:, (dest * local_kv + head) * kv_width :][:, :kv_width]
+                for dest in range(tensor_devices)
+            ],
+            axis=1,
+        )
         key_values = lax.psum_scatter(
-            jnp.concatenate(
-                [
-                    projected[:, (dest * local_kv + head) * kv_width :][:, :kv_width]
-                    for dest in range(tensor_devices)
-                ],
-                axis=1,
+            jnp.dot(image_block, weight_part, preferred_element_type=jnp.float32).astype(
+                jnp.bfloat16
             ),
             "tensor",
             scatter_dimension=1,

time: 229 us -> 223 us (0.974)
  waiting for transfers between devices: 57 us -> 47.4 us
  local copies, waits for them, and re-layouts: 16.8 us -> 22.2 us
  other arithmetic: 10.9 us -> 5.89 us
  matrix products: 18 us -> 20.8 us
    reduce_scatter x2, waiting for transfers between devices: 32.4 us -> 22.9 us  [on_device(): lax.psum_scatter(jnp.dot(image_block, weight_part, preferred_element_type...]
    concatenate x2 -> x0, other arithmetic: 5 us -> none  [on_device(): jnp.concatenate([projected[:, (dest * local_kv + head) * kv_width:][:, :k...]
    slice x2, local copies, waits for them, and re-layouts: 0.64 us -> 5.15 us  [the longest x1 4.94 us: on_device(): kv_weight[:, (dest * local_kv + head) * kv_width:][:, :kv_width]]
    dot_general x1 -> x2, matrix products: 18 us -> 20.8 us  [on_device(): jnp.dot(image_block, weight_part, preferred_element_type=jnp.float32)]
  transfers between devices with their start and end apart: 4 -> 4, of which waited for: 2 -> 2; matrix products, arithmetic and copies ran while one was open for 7% -> 12% of each run, Pallas kernels for 22% -> 22%
where the time goes in v11:
time: 223 us; the launch traced here: 222 us
  blocking collectives  54.3 us (24%)
  Pallas kernels  49.7 us (22%)
  waiting for transfers between devices  47.4 us (21%)
  local copies, waits for them, and re-layouts  22.2 us (10%)
  matrix products  20.8 us (9%)
  between operations  13.5 us (6%)
  starting transfers between devices  8.43 us (4%)
  other arithmetic  5.89 us (3%)
    all_to_all x1, blocking collectives, on_device(): lax.all_to_all(outgoing, 'seq', split_axis=0, concat_axis=0, tiled=True)  54.3 us
    pallas_call x2, Pallas kernels, attend(): pl.pallas_call(functools.partial(attend_kernel, group, head_dim), out_sha...  49.7 us
    all_to_all x2, waiting for transfers between devices, on_device(): lax.all_to_all(answered, 'seq', split_axis=0, concat_axis=0, tiled=True)  24.5 us
    reduce_scatter x2, waiting for transfers between devices, on_device(): lax.psum_scatter(jnp.dot(image_block, weight_part, preferred_element_type...  22.9 us
    dot_general x2, matrix products, on_device(): jnp.dot(image_block, weight_part, preferred_element_type=jnp.float32)  20.8 us
    all_to_all x2, starting transfers between devices, on_device(): lax.all_to_all(answered, 'seq', split_axis=0, concat_axis=0, tiled=True)  8.21 us
    scatter x1, local copies, waits for them, and re-layouts, on_device(): jnp.zeros((rows, width_cols), jnp.bfloat16).at[slot_index].set(queries)  7.21 us
    gather x2, local copies, waits for them, and re-layouts, on_device(): piece = returned.reshape(rows, -1)[slot_index]  6.65 us
  transfers between devices with their start and end apart: 4, of which 2 were waited for; matrix products, arithmetic and copies ran while one was open for 12% of the time, Pallas kernels for 22%

profile of v11, /device:TPU:0, one launch (start us, length us, event | category | flops | bytes accessed | tf_op | source)
XLA Modules:
  0.0 222.3 jit_solution(10314837598517686847)
XLA Ops:
  6.5 0.0 reduce-scatter.3.cloned.1.call-start
  6.5 0.0 copy-start.3
  6.5 4.9 %fusion.44 = (bf16[2048,256]{1,0:T(8,128)(2,1)S(1)}, bf16[2048,256]{1,0:T(8,128)(2,1)S(1)}, bf16[2048,256]{1,0:T(8,128)(2,1)S(1)}, bf16[2048,256]{1,0:T(8,128)(2...) fusion(bf16[2048,2048]{1,0:T(8,128)(2,1)} %param.7), kind=kLoop, calls=%fused_computation.39 | loop fusion | bytes 16777216 | tf_op jit(solution)/shard_map/slice | solution.py:93
  11.5 0.9 copy-done.3
  12.4 9.0 %fusion.33 = bf16[1601,1024]{1,0:T(8,128)(2,1)} fusion(bf16[1,1601,2048]{2,1,0:T(8,128)(2,1)S(1)} %copy-done.3, bf16[2048,256]{1,0:T(8,128)(2,1)S(1)} %get-tuple-element.8, bf16[2048,256]{1,0:T(8,128)(2,1)S(1)} %get-tuple-element.9, bf16[2048,256]{1,0:T(8,128)(2,1)S(1)} %get-tuple-element.10, bf16[2048,256]{1,0:T(8,128)(2,1)S(1)} %get-tuple-element.5), kind=kOutput, calls=%fused_computation.25 | convolution fusion | flops 6733497344 | bytes 14030848 | tf_op jit(solution)/shard_map/dot_general | solution.py:99
  21.4 0.0 reduce-scatter.3.cloned.1.call-update
  21.4 0.2 reduce-scatter.5.cloned.1.call-start
  21.7 0.0 copy-start.2
  21.7 11.8 %fusion.28 = bf16[1601,1024]{1,0:T(8,128)(2,1)} fusion(bf16[1,1601,2048]{2,1,0:T(8,128)(2,1)} %param.6, bf16[2048,256]{1,0:T(8,128)(2,1)S(1)} %get-tuple-element.11, bf16[2048,256]{1,0:T(8,128)(2,1)} %get-tuple-element.12, bf16[2048,256]{1,0:T(8,128)(2,1)S(1)} %get-tuple-element.6, bf16[2048,256]{1,0:T(8,128)(2,1)S(1)} %get-tuple-element.7), kind=kOutput, calls=%fused_computation.24 | convolution fusion | flops 6733497344 | bytes 14030848 | tf_op jit(solution)/shard_map/dot_general | solution.py:99
  33.5 0.0 reduce-scatter.5.cloned.1.call-update
  33.5 0.0 copy-done.2
  33.5 1.1 reduce-window.6
  34.7 0.2 slice_reduce_fusion
  34.9 0.1 fusion.40
  35.0 7.2 %scatter_custom_fusion = bf16[1024,2048]{1,0:T(8,128)(2,1)} fusion(s32[512]{0:T(512)S(1)} %bitcast.39, bf16[512,2048]{1,0:T(8,128)(2,1)} %param.4, bf16[]{:T(256)} %constant.6.clone.1), kind=kCustom, calls=%fused_computation.27 | custom fusion | bytes 4194816 | tf_op jit(solution)/shard_map/scatter | solution.py:76
  42.2 54.3 %all_to_all.15 = bf16[8,128,2048]{2,1,0:T(8,128)(2,1)S(1)} all-to-all(bf16[8,128,2048]{2,1,0:T(8,128)(2,1)} %bitcast.34), channel_id=1, replica_groups=mesh['seq'=8,'tensor'=4] {'seq'}, dimensions={0} | all-to-all | bytes 8388608 | tf_op jit(solution)/shard_map/all_to_all | solution.py:84
  96.5 3.1 %multiply_convert_fusion = bf16[8,128,2048]{2,1,0:T(8,128)(2,1)} fusion(bf16[8,128,2048]{2,1,0:T(8,128)(2,1)S(1)} %all_to_all.15), kind=kLoop, calls=%fused_computation.3 | loop fusion | flops 6291456 | bytes 8388608 | tf_op jit(solution)/shard_map/convert_element_type | solution.py:86
  99.6 0.0 reduce-scatter.3.cloned.1.call-done.k_ref.v_ref
  99.6 0.0 copy-start
  99.6 1.1 copy-done
  100.8 24.9 %shard_map.46 = bf16[1024,1024]{1,0:T(8,128)(2,1)} custom-call(bf16[1024,2048]{1,0:T(8,128)(2,1)} %bitcast.35, bf16[1601,256]{1,0:T(8,128)(2,1)S(1)} %copy-done, bf16[1601,256]{1,0:T(8,128)(2,1)S(1)} %copy-done), custom_call_target="tpu_custom_call" | custom-call | flops 6715080704 | bytes 5014016 | tf_op jit(solution)/shard_map/pallas_call | solution.py:39
  125.7 3.9 %all-to-all-start.1 = ((bf16[8,128,1024]{2,1,0:T(8,128)(2,1)}), bf16[8,128,1024]{2,1,0:T(8,128)(2,1)S(1)}, u32[]{:S(2)}, u32[]{:S(2)}) async-start(bf16[8,128,1024]{2,1,0:T(8,128)(2,1)} %bitcast.10), calls=%async_computation.2 | async-start | bytes 4194304 | tf_op jit(solution)/shard_map/all_to_all | solution.py:108
  129.5 22.9 %reduce-scatter.5.cloned.1.call-done.k_ref.v_ref = bf16[1601,256]{1,0:T(8,128)(2,1)} async-done(((bf16[1601,1024]{1,0:T(8,128)(2,1)}), bf16[1601,256]{1,0:T(8,128)(2,1)}) %reduce-scatter.5.cloned.1.call-update) | async-done | bytes 819728 | tf_op jit(solution)/shard_map/reduce_scatter | solution.py:98
  152.4 0.0 copy-start.1
  152.4 1.1 copy-done.1
  153.5 24.8 %shard_map.47 = bf16[1024,1024]{1,0:T(8,128)(2,1)} custom-call(bf16[1024,2048]{1,0:T(8,128)(2,1)} %bitcast.36, bf16[1601,256]{1,0:T(8,128)(2,1)S(1)} %copy-done.1, bf16[1601,256]{1,0:T(8,128)(2,1)S(1)} %copy-done.1), custom_call_target="tpu_custom_call" | custom-call | flops 6715080704 | bytes 5014016 | tf_op jit(solution)/shard_map/pallas_call | solution.py:39
  178.4 0.0 all-to-all-done.1
  178.4 4.3 %all-to-all-start.2 = ((bf16[8,128,1024]{2,1,0:T(8,128)(2,1)}), bf16[8,128,1024]{2,1,0:T(8,128)(2,1)}, u32[]{:S(2)}, u32[]{:S(2)}) async-start(bf16[8,128,1024]{2,1,0:T(8,128)(2,1)} %bitcast.13), calls=%async_computation.4 | async-start | bytes 4194304 | tf_op jit(solution)/shard_map/all_to_all | solution.py:108
  182.8 2.1 gather_fusion
  184.8 24.5 %all-to-all-done.2 = bf16[8,128,1024]{2,1,0:T(8,128)(2,1)} async-done(((bf16[8,128,1024]{2,1,0:T(8,128)(2,1)}), bf16[8,128,1024]{2,1,0:T(8,128)(2,1)}, u32[]{:S(2)}, u32[]{:S(2)}) %all-to-all-start.2) | async-done | bytes 2097184 | tf_op jit(solution)/shard_map/all_to_all | solution.py:108
  209.4 4.6 %gather_fusion.1 = bf16[512,1024]{1,0:T(8,128)(2,1)S(1)} fusion(bf16[1024,1024]{1,0:T(8,128)(2,1)} %bitcast.14, s32[1024]{0:T(1024)S(1)} %pad_clamp_fusion), kind=kCustom, calls=%fused_computation.1 | custom fusion | bytes 2099200 | tf_op jit(solution)/shard_map/gather | solution.py:109
  214.0 1.5 pad_maximum_fusion
  (5 shorter events, 0.1 us)
Async XLA Ops:
  6.5 93.1 %reduce-scatter.3.cloned.1.call-start = ((), (), s32[]{:S(2)}) async-start(), calls=%async_computation.5 | async-start | bytes 4116480 | tf_op jit(solution)/shard_map/reduce_scatter | solution.py:98
  6.5 5.9 %copy-start.3 = (bf16[1,1601,2048]{2,1,0:T(8,128)(2,1)S(1)}, bf16[1,1601,2048]{2,1,0:T(8,128)(2,1)}, u32[]{:S(2)}) copy-start(bf16[1,1601,2048]{2,1,0:T(8,128)(2,1)} %param.6) | copy-start | bytes 19673092
  21.4 131.0 %reduce-scatter.5.cloned.1.call-start = ((), (), s32[]{:S(2)}) async-start(), calls=%async_computation.6 | async-start | bytes 4116480 | tf_op jit(solution)/shard_map/reduce_scatter | solution.py:98
  21.7 11.8 %copy-start.2 = (s32[512,1]{0,1:T(1,128)S(1)}, s32[512,1]{0,1:T(1,128)}, u32[]{:S(2)}) copy-start(s32[512,1]{0,1:T(1,128)} %param.5) | copy-start | bytes 6148
  99.6 1.1 copy-start
  125.7 52.7 %all-to-all-start.1 = ((bf16[8,128,1024]{2,1,0:T(8,128)(2,1)}), bf16[8,128,1024]{2,1,0:T(8,128)(2,1)S(1)}, u32[]{:S(2)}, u32[]{:S(2)}) async-start(bf16[8,128,1024]{2,1,0:T(8,128)(2,1)} %bitcast.10), calls=%async_computation.2 | async-start | bytes 4194304 | tf_op jit(solution)/shard_map/all_to_all | solution.py:108
  152.4 1.1 copy-start.1
  178.4 31.0 %all-to-all-start.2 = ((bf16[8,128,1024]{2,1,0:T(8,128)(2,1)}), bf16[8,128,1024]{2,1,0:T(8,128)(2,1)}, u32[]{:S(2)}, u32[]{:S(2)}) async-start(bf16[8,128,1024]{2,1,0:T(8,128)(2,1)} %bitcast.13), calls=%async_computation.4 | async-start | bytes 4194304 | tf_op jit(solution)/shard_map/all_to_all | solution.py:108
Sparse Core Ops, SparseCore 0:
  21.6 65.5 reduce-scatter.2
  89.5 62.8 reduce-scatter.4

commit v12 on v11

--- a/solution.py
+++ b/solution.py
@@ -103,13 +103,17 @@
             scatter_dimension=1,
             tiled=True,
         )
-        answered = attend(scaled_rows, key_values, group, HEAD_DIM, head * group, tile)
-        answered = answered.reshape(seq_devices, capacity, -1)
-        returned = lax.all_to_all(answered, "seq", split_axis=0, concat_axis=0, tiled=True)
-        piece = returned.reshape(rows, -1)[slot_index]
-        if result is None:
-            result = jnp.zeros((token_count, width_cols), jnp.bfloat16)
-        result = lax.dynamic_update_slice(result, piece, (0, head * piece.shape[1]))
+        calls = 2
+        call_heads = group // calls
+        for part in range(calls):
+            first = head * group + part * call_heads
+            answered = attend(scaled_rows, key_values, call_heads, HEAD_DIM, first, tile)
+            answered = answered.reshape(seq_devices, capacity, -1)
+            returned = lax.all_to_all(answered, "seq", split_axis=0, concat_axis=0, tiled=True)
+            piece = returned.reshape(rows, -1)[slot_index]
+            if result is None:
+                result = jnp.zeros((token_count, width_cols), jnp.bfloat16)
+            result = lax.dynamic_update_slice(result, piece, (0, first * HEAD_DIM))
     return result
 
 

time: 223 us -> 222 us (level)
  waiting for transfers between devices: 47.4 us -> 19.4 us
  local copies, waits for them, and re-layouts: 22.2 us -> 39 us
  starting transfers between devices: 8.43 us -> 16.6 us
  Pallas kernels: 49.7 us -> 53.2 us
    all_to_all x2 -> x4, waiting for transfers between devices: 24.5 us -> 6.49 us  [on_device(): lax.all_to_all(answered, 'seq', split_axis=0, concat_axis=0, tiled=True)]
    reduce_scatter x2, waiting for transfers between devices: 22.9 us -> 12.9 us  [on_device(): lax.psum_scatter(jnp.dot(image_block, weight_part, preferred_element_type...]
    unnamed x8 -> x20, local copies, waits for them, and re-layouts: 3.21 us -> 12 us
    all_to_all x2 -> x4, starting transfers between devices: 8.21 us -> 16.4 us  [on_device(): lax.all_to_all(answered, 'seq', split_axis=0, concat_axis=0, tiled=True)]
    dynamic_update_slice x0 -> x4, local copies, waits for them, and re-layouts: none -> 4.06 us  [on_device(): result = lax.dynamic_update_slice(result, piece, (0, first * HEAD_DIM))]
    gather x2 -> x4, local copies, waits for them, and re-layouts: 6.65 us -> 10.6 us  [on_device(): piece = returned.reshape(rows, -1)[slot_index]]
    pallas_call x2 -> x4, Pallas kernels: 49.7 us -> 53.2 us  [attend(): pl.pallas_call(functools.partial(attend_kernel, group, head_dim), out_sha...]
  transfers between devices with their start and end apart: 4 -> 6, of which waited for: 2 -> 2; matrix products, arithmetic and copies ran while one was open for 12% -> 15% of each run, Pallas kernels for 22% -> 24%
where the time goes in v12:
time: 222 us; the launch traced here: 221 us
  blocking collectives  54.3 us (24%)
  Pallas kernels  53.2 us (24%)
  local copies, waits for them, and re-layouts  39 us (18%)
  matrix products  20.9 us (9%)
  waiting for transfers between devices  19.4 us (9%)
  starting transfers between devices  16.6 us (7%)
  between operations  13.5 us (6%)
  other arithmetic  4.42 us (2%)
    all_to_all x1, blocking collectives, on_device(): lax.all_to_all(outgoing, 'seq', split_axis=0, concat_axis=0, tiled=True)  54.3 us
    pallas_call x4, Pallas kernels, attend(): pl.pallas_call(functools.partial(attend_kernel, group, head_dim), out_sha...  53.2 us
    dot_general x2, matrix products, on_device(): jnp.dot(image_block, weight_part, preferred_element_type=jnp.float32)  20.9 us
    all_to_all x4, starting transfers between devices, on_device(): lax.all_to_all(answered, 'seq', split_axis=0, concat_axis=0, tiled=True)  16.4 us
    reduce_scatter x2, waiting for transfers between devices, on_device(): lax.psum_scatter(jnp.dot(image_block, weight_part, preferred_element_type...  12.9 us
    unnamed x20, local copies, waits for them, and re-layouts  12 us
    gather x4, local copies, waits for them, and re-layouts, on_device(): piece = returned.reshape(rows, -1)[slot_index]  10.6 us
    scatter x1, local copies, waits for them, and re-layouts, on_device(): jnp.zeros((rows, width_cols), jnp.bfloat16).at[slot_index].set(queries)  7.21 us
  transfers between devices with their start and end apart: 6, of which 2 were waited for; matrix products, arithmetic and copies ran while one was open for 15% of the time, Pallas kernels for 24%

profile of v12, /device:TPU:0, one launch (start us, length us, event | category | flops | bytes accessed | tf_op | source)
XLA Modules:
  0.0 221.4 jit_solution(13708115909387388229)
XLA Ops:
  6.5 0.0 reduce-scatter.3.cloned.1.call-start
  6.5 0.0 copy-start.9
  6.5 4.9 %fusion.44 = (bf16[2048,256]{1,0:T(8,128)(2,1)S(1)}, bf16[2048,256]{1,0:T(8,128)(2,1)S(1)}, bf16[2048,256]{1,0:T(8,128)(2,1)S(1)}, bf16[2048,256]{1,0:T(8,128)(2...) fusion(bf16[2048,2048]{1,0:T(8,128)(2,1)} %param.7), kind=kLoop, calls=%fused_computation.43 | loop fusion | bytes 16777216 | tf_op jit(solution)/shard_map/slice | solution.py:93
  11.5 0.9 copy-done.9
  12.4 9.0 %fusion.33 = bf16[1601,1024]{1,0:T(8,128)(2,1)} fusion(bf16[1,1601,2048]{2,1,0:T(8,128)(2,1)S(1)} %copy-done.9, bf16[2048,256]{1,0:T(8,128)(2,1)S(1)} %get-tuple-element.7, bf16[2048,256]{1,0:T(8,128)(2,1)S(1)} %get-tuple-element.8, bf16[2048,256]{1,0:T(8,128)(2,1)S(1)} %get-tuple-element.9, bf16[2048,256]{1,0:T(8,128)(2,1)S(1)} %get-tuple-element.10), kind=kOutput, calls=%fused_computation.27 | convolution fusion | flops 6733497344 | bytes 14030848 | tf_op jit(solution)/shard_map/dot_general | solution.py:99
  21.4 0.0 reduce-scatter.3.cloned.1.call-update
  21.5 0.2 reduce-scatter.5.cloned.1.call-start
  21.7 0.0 copy-start.8
  21.7 11.8 %fusion.28 = bf16[1601,1024]{1,0:T(8,128)(2,1)} fusion(bf16[1,1601,2048]{2,1,0:T(8,128)(2,1)} %param.6, bf16[2048,256]{1,0:T(8,128)(2,1)S(1)} %get-tuple-element.11, bf16[2048,256]{1,0:T(8,128)(2,1)} %get-tuple-element.12, bf16[2048,256]{1,0:T(8,128)(2,1)S(1)} %get-tuple-element.6, bf16[2048,256]{1,0:T(8,128)(2,1)S(1)} %get-tuple-element.5), kind=kOutput, calls=%fused_computation.26 | convolution fusion | flops 6733497344 | bytes 14030848 | tf_op jit(solution)/shard_map/dot_general | solution.py:99
  33.5 0.0 reduce-scatter.5.cloned.1.call-update
  33.6 0.0 copy-done.8
  33.6 1.1 reduce-window.6
  34.7 0.2 slice_reduce_fusion
  35.0 0.1 fusion.40
  35.1 7.2 %scatter_custom_fusion = bf16[1024,2048]{1,0:T(8,128)(2,1)} fusion(s32[512]{0:T(512)S(1)} %bitcast.46, bf16[512,2048]{1,0:T(8,128)(2,1)} %param.4, bf16[]{:T(256)} %constant.8.clone.1), kind=kCustom, calls=%fused_computation.28 | custom fusion | bytes 4194816 | tf_op jit(solution)/shard_map/scatter | solution.py:76
  42.3 54.3 %all_to_all.25 = bf16[8,128,2048]{2,1,0:T(8,128)(2,1)S(1)} all-to-all(bf16[8,128,2048]{2,1,0:T(8,128)(2,1)} %bitcast.43), channel_id=1, replica_groups=mesh['seq'=8,'tensor'=4] {'seq'}, dimensions={0} | all-to-all | bytes 8388608 | tf_op jit(solution)/shard_map/all_to_all | solution.py:84
  96.6 3.1 %multiply_convert_fusion = bf16[8,128,2048]{2,1,0:T(8,128)(2,1)} fusion(bf16[8,128,2048]{2,1,0:T(8,128)(2,1)S(1)} %all_to_all.25), kind=kLoop, calls=%fused_computation.5 | loop fusion | flops 6291456 | bytes 8388608 | tf_op jit(solution)/shard_map/convert_element_type | solution.py:86
  99.7 0.0 reduce-scatter.3.cloned.1.call-done.k_ref.v_ref
  99.7 0.0 copy-start
  99.7 2.2 copy-done
  101.9 0.0 copy-start.6
  101.9 1.1 copy-done.6
  103.0 0.0 copy-start.7
  103.0 13.3 %shard_map.47 = bf16[1024,512]{1,0:T(8,128)(2,1)} custom-call(bf16[1024,2048]{1,0:T(8,128)(2,1)S(1)} %bitcast.37, bf16[1601,256]{1,0:T(8,128)(2,1)S(1)} %copy-done.6, bf16[1601,256]{1,0:T(8,128)(2,1)S(1)} %copy-done.6), custom_call_target="tpu_custom_call" | custom-call | flops 3357540352 | bytes 2916864 | tf_op jit(solution)/shard_map/pallas_call | solution.py:39
  116.4 3.6 %all-to-all-start.2 = ((bf16[8,128,512]{2,1,0:T(8,128)(2,1)}), bf16[8,128,512]{2,1,0:T(8,128)(2,1)S(1)}, u32[]{:S(2)}, u32[]{:S(2)}) async-start(bf16[8,128,512]{2,1,0:T(8,128)(2,1)} %bitcast.12), calls=%async_computation.3 | async-start | bytes 2097152 | tf_op jit(solution)/shard_map/all_to_all | solution.py:112
  119.9 0.0 copy-done.7
  119.9 0.0 copy-start.1
  119.9 2.2 copy-done.1
  122.1 13.3 %shard_map.46 = bf16[1024,512]{1,0:T(8,128)(2,1)} custom-call(bf16[1024,2048]{1,0:T(8,128)(2,1)S(1)} %bitcast.38, bf16[1601,256]{1,0:T(8,128)(2,1)S(1)} %copy-done.7, bf16[1601,256]{1,0:T(8,128)(2,1)S(1)} %copy-done.7), custom_call_target="tpu_custom_call" | custom-call | flops 3357540352 | bytes 2916864 | tf_op jit(solution)/shard_map/pallas_call | solution.py:39
  135.4 0.0 all-to-all-done.2
  135.4 4.1 %all-to-all-start.1 = ((bf16[8,128,512]{2,1,0:T(8,128)(2,1)}), bf16[8,128,512]{2,1,0:T(8,128)(2,1)S(1)}, u32[]{:S(2)}, u32[]{:S(2)}) async-start(bf16[8,128,512]{2,1,0:T(8,128)(2,1)} %bitcast.10), calls=%async_computation.2 | async-start | bytes 2097152 | tf_op jit(solution)/shard_map/all_to_all | solution.py:112
  139.6 12.9 %reduce-scatter.5.cloned.1.call-done.k_ref.v_ref = bf16[1601,256]{1,0:T(8,128)(2,1)} async-done(((bf16[1601,1024]{1,0:T(8,128)(2,1)}), bf16[1601,256]{1,0:T(8,128)(2,1)}) %reduce-scatter.5.cloned.1.call-update) | async-done | bytes 819728 | tf_op jit(solution)/shard_map/reduce_scatter | solution.py:98
  152.4 0.0 copy-start.2
  152.4 2.2 copy-done.2
  154.6 0.0 copy-start.4
  154.6 1.1 copy-done.4
  155.8 0.0 copy-start.5
  155.8 13.3 %shard_map.48 = bf16[1024,512]{1,0:T(8,128)(2,1)} custom-call(bf16[1024,2048]{1,0:T(8,128)(2,1)S(1)} %bitcast.39, bf16[1601,256]{1,0:T(8,128)(2,1)S(1)} %copy-done.4, bf16[1601,256]{1,0:T(8,128)(2,1)S(1)} %copy-done.4), custom_call_target="tpu_custom_call" | custom-call | flops 3357540352 | bytes 2916864 | tf_op jit(solution)/shard_map/pallas_call | solution.py:39
  169.0 0.0 all-to-all-done.1
  169.0 4.5 %all-to-all-start.3 = ((bf16[8,128,512]{2,1,0:T(8,128)(2,1)}), bf16[8,128,512]{2,1,0:T(8,128)(2,1)}, u32[]{:S(2)}, u32[]{:S(2)}) async-start(bf16[8,128,512]{2,1,0:T(8,128)(2,1)} %bitcast.15), calls=%async_computation.5 | async-start | bytes 2097152 | tf_op jit(solution)/shard_map/all_to_all | solution.py:112
  173.5 0.0 copy-done.5
  173.6 0.0 copy-start.3
  173.6 2.2 copy-done.3
  175.7 13.3 %shard_map.49 = bf16[1024,512]{1,0:T(8,128)(2,1)} custom-call(bf16[1024,2048]{1,0:T(8,128)(2,1)S(1)} %bitcast.40, bf16[1601,256]{1,0:T(8,128)(2,1)S(1)} %copy-done.5, bf16[1601,256]{1,0:T(8,128)(2,1)S(1)} %copy-done.5), custom_call_target="tpu_custom_call" | custom-call | flops 3357540352 | bytes 2916864 | tf_op jit(solution)/shard_map/pallas_call | solution.py:39
  189.0 0.0 all-to-all-done.3
  189.0 4.2 %all-to-all-start.4 = ((bf16[8,128,512]{2,1,0:T(8,128)(2,1)}), bf16[8,128,512]{2,1,0:T(8,128)(2,1)}, u32[]{:S(2)}, u32[]{:S(2)}) async-start(bf16[8,128,512]{2,1,0:T(8,128)(2,1)} %bitcast.17), calls=%async_computation.6 | async-start | bytes 2097152 | tf_op jit(solution)/shard_map/all_to_all | solution.py:112
  193.3 2.0 gather_fusion.1
  195.3 2.0 gather_fusion
  197.3 1.6 dynamic_update_slice.12
  198.8 3.3 %gather_fusion.2 = bf16[512,512]{1,0:T(8,128)(2,1)S(1)} fusion(bf16[1024,512]{1,0:T(8,128)(2,1)} %bitcast.16, s32[1024]{0:T(1024)S(1)} %pad_clamp_fusion), kind=kCustom, calls=%fused_computation.2 | custom fusion | bytes 1050624 | tf_op jit(solution)/shard_map/gather | solution.py:113
  202.2 6.5 %all-to-all-done.4 = bf16[8,128,512]{2,1,0:T(8,128)(2,1)} async-done(((bf16[8,128,512]{2,1,0:T(8,128)(2,1)}), bf16[8,128,512]{2,1,0:T(8,128)(2,1)}, u32[]{:S(2)}, u32[]{:S(2)}) %all-to-all-start.4) | async-done | bytes 1048608 | tf_op jit(solution)/shard_map/all_to_all | solution.py:112
  208.7 3.3 %gather_fusion.3 = bf16[512,512]{1,0:T(8,128)(2,1)S(1)} fusion(bf16[1024,512]{1,0:T(8,128)(2,1)} %bitcast.18, s32[1024]{0:T(1024)S(1)} %pad_clamp_fusion), kind=kCustom, calls=%fused_computation.3 | custom fusion | bytes 1050624 | tf_op jit(solution)/shard_map/gather | solution.py:113
  212.0 0.8 constant_dynamic-update-slice_fusion.2
  212.9 0.8 constant_dynamic-update-slice_fusion.1
  213.7 0.8 constant_dynamic-update-slice_fusion
  (5 shorter events, 0.1 us)
Async XLA Ops:
  6.5 93.2 %reduce-scatter.3.cloned.1.call-start = ((), (), s32[]{:S(2)}) async-start(), calls=%async_computation.7 | async-start | bytes 4116480 | tf_op jit(solution)/shard_map/reduce_scatter | solution.py:98
  6.5 5.9 %copy-start.9 = (bf16[1,1601,2048]{2,1,0:T(8,128)(2,1)S(1)}, bf16[1,1601,2048]{2,1,0:T(8,128)(2,1)}, u32[]{:S(2)}) copy-start(bf16[1,1601,2048]{2,1,0:T(8,128)(2,1)} %param.6) | copy-start | bytes 19673092
  21.5 131.0 %reduce-scatter.5.cloned.1.call-start = ((), (), s32[]{:S(2)}) async-start(), calls=%async_computation.8 | async-start | bytes 4116480 | tf_op jit(solution)/shard_map/reduce_scatter | solution.py:98
  21.7 11.9 %copy-start.8 = (s32[512,1]{0,1:T(1,128)S(1)}, s32[512,1]{0,1:T(1,128)}, u32[]{:S(2)}) copy-start(s32[512,1]{0,1:T(1,128)} %param.5) | copy-start | bytes 6148
  99.7 2.2 copy-start
  101.9 1.1 copy-start.6
  103.0 16.9 %copy-start.7 = (bf16[1601,256]{1,0:T(8,128)(2,1)S(1)}, bf16[1601,256]{1,0:T(8,128)(2,1)}, u32[]{:S(2)}) copy-start(bf16[1601,256]{1,0:T(8,128)(2,1)} %reduce-scatter.3.cloned.1.call-done.k_ref.v_ref) | copy-start | bytes 2459140
  116.4 19.1 %all-to-all-start.2 = ((bf16[8,128,512]{2,1,0:T(8,128)(2,1)}), bf16[8,128,512]{2,1,0:T(8,128)(2,1)S(1)}, u32[]{:S(2)}, u32[]{:S(2)}) async-start(bf16[8,128,512]{2,1,0:T(8,128)(2,1)} %bitcast.12), calls=%async_computation.3 | async-start | bytes 2097152 | tf_op jit(solution)/shard_map/all_to_all | solution.py:112
  119.9 2.2 copy-start.1
  135.4 33.6 %all-to-all-start.1 = ((bf16[8,128,512]{2,1,0:T(8,128)(2,1)}), bf16[8,128,512]{2,1,0:T(8,128)(2,1)S(1)}, u32[]{:S(2)}, u32[]{:S(2)}) async-start(bf16[8,128,512]{2,1,0:T(8,128)(2,1)} %bitcast.10), calls=%async_computation.2 | async-start | bytes 2097152 | tf_op jit(solution)/shard_map/all_to_all | solution.py:112
  152.4 2.2 copy-start.2
  154.6 1.1 copy-start.4
  155.8 17.8 %copy-start.5 = (bf16[1601,256]{1,0:T(8,128)(2,1)S(1)}, bf16[1601,256]{1,0:T(8,128)(2,1)}, u32[]{:S(2)}) copy-start(bf16[1601,256]{1,0:T(8,128)(2,1)} %reduce-scatter.5.cloned.1.call-done.k_ref.v_ref) | copy-start | bytes 2459140
  169.0 20.0 %all-to-all-start.3 = ((bf16[8,128,512]{2,1,0:T(8,128)(2,1)}), bf16[8,128,512]{2,1,0:T(8,128)(2,1)}, u32[]{:S(2)}, u32[]{:S(2)}) async-start(bf16[8,128,512]{2,1,0:T(8,128)(2,1)} %bitcast.15), calls=%async_computation.5 | async-start | bytes 2097152 | tf_op jit(solution)/shard_map/all_to_all | solution.py:112
  173.6 2.2 copy-start.3
  189.0 19.6 %all-to-all-start.4 = ((bf16[8,128,512]{2,1,0:T(8,128)(2,1)}), bf16[8,128,512]{2,1,0:T(8,128)(2,1)}, u32[]{:S(2)}, u32[]{:S(2)}) async-start(bf16[8,128,512]{2,1,0:T(8,128)(2,1)} %bitcast.17), calls=%async_computation.6 | async-start | bytes 2097152 | tf_op jit(solution)/shard_map/all_to_all | solution.py:112
Sparse Core Ops, SparseCore 0:
  21.6 65.5 reduce-scatter.2
  89.5 62.8 reduce-scatter.4

commit v13 on v12

--- a/solution.py
+++ b/solution.py
@@ -48,7 +48,7 @@
         out_specs=pl.BlockSpec((tile, width), lambda i: (i, 0)),
         compiler_params=pltpu.CompilerParams(
             dimension_semantics=("arbitrary",),
-            vmem_limit_bytes=48 * 1024 * 1024,
+            vmem_limit_bytes=67043328,
         ),
         cost_estimate=pl.CostEstimate(
             flops=flops,

time: 222 us -> 217 us (0.977)
  local copies, waits for them, and re-layouts: 39 us -> 29.3 us
  Pallas kernels: 53.2 us -> 57.1 us
    unnamed x20 -> x6, local copies, waits for them, and re-layouts: 12 us -> 0.92 us
    pallas_call x4, Pallas kernels: 53.2 us -> 57.1 us  [attend(): pl.pallas_call(functools.partial(attend_kernel, group, head_dim), out_sha...]
  transfers between devices with their start and end apart: 6 -> 6, of which waited for: 2 -> 4; matrix products, arithmetic and copies ran while one was open for 15% -> 17% of each run, Pallas kernels for 24% -> 26%
where the time goes in v13:
time: 217 us; the launch traced here: 216 us
  Pallas kernels  57.1 us (26%)
  blocking collectives  54.3 us (25%)
  local copies, waits for them, and re-layouts  29.3 us (14%)
  matrix products  20.8 us (10%)
  waiting for transfers between devices  19.7 us (9%)
  starting transfers between devices  16.8 us (8%)
  between operations  13.5 us (6%)
  other arithmetic  5.02 us (2%)
    pallas_call x4, Pallas kernels, attend(): pl.pallas_call(functools.partial(attend_kernel, group, head_dim), out_sha...  57.1 us
    all_to_all x1, blocking collectives, on_device(): lax.all_to_all(outgoing, 'seq', split_axis=0, concat_axis=0, tiled=True)  54.3 us
    dot_general x2, matrix products, on_device(): jnp.dot(image_block, weight_part, preferred_element_type=jnp.float32)  20.8 us
    all_to_all x4, starting transfers between devices, on_device(): lax.all_to_all(answered, 'seq', split_axis=0, concat_axis=0, tiled=True)  16.6 us
    reduce_scatter x2, waiting for transfers between devices, on_device(): lax.psum_scatter(jnp.dot(image_block, weight_part, preferred_element_type...  14.6 us
    gather x4, local copies, waits for them, and re-layouts, on_device(): piece = returned.reshape(rows, -1)[slot_index]  12 us
    scatter x1, local copies, waits for them, and re-layouts, on_device(): jnp.zeros((rows, width_cols), jnp.bfloat16).at[slot_index].set(queries)  7.21 us
    all_to_all x4, waiting for transfers between devices, on_device(): lax.all_to_all(answered, 'seq', split_axis=0, concat_axis=0, tiled=True)  4.99 us
  transfers between devices with their start and end apart: 6, of which 4 were waited for; matrix products, arithmetic and copies ran while one was open for 17% of the time, Pallas kernels for 26%

profile of v13, /device:TPU:0, one launch (start us, length us, event | category | flops | bytes accessed | tf_op | source)
XLA Modules:
  0.0 216.5 jit_solution(3722651703391526707)
XLA Ops:
  6.5 0.0 reduce-scatter.3.cloned.1.call-start
  6.5 0.0 copy-start.2
  6.5 4.9 %fusion.44 = (bf16[2048,256]{1,0:T(8,128)(2,1)S(1)}, bf16[2048,256]{1,0:T(8,128)(2,1)S(1)}, bf16[2048,256]{1,0:T(8,128)(2,1)S(1)}, bf16[2048,256]{1,0:T(8,128)(2...) fusion(bf16[2048,2048]{1,0:T(8,128)(2,1)} %param.7), kind=kLoop, calls=%fused_computation.43 | loop fusion | bytes 16777216 | tf_op jit(solution)/shard_map/slice | solution.py:93
  11.5 0.9 copy-done.2
  12.4 9.0 %fusion.33 = bf16[1601,1024]{1,0:T(8,128)(2,1)} fusion(bf16[1,1601,2048]{2,1,0:T(8,128)(2,1)S(1)} %copy-done.2, bf16[2048,256]{1,0:T(8,128)(2,1)S(1)} %get-tuple-element.7, bf16[2048,256]{1,0:T(8,128)(2,1)S(1)} %get-tuple-element.8, bf16[2048,256]{1,0:T(8,128)(2,1)S(1)} %get-tuple-element.9, bf16[2048,256]{1,0:T(8,128)(2,1)S(1)} %get-tuple-element.10), kind=kOutput, calls=%fused_computation.27 | convolution fusion | flops 6733497344 | bytes 14030848 | tf_op jit(solution)/shard_map/dot_general | solution.py:99
  21.4 0.0 reduce-scatter.3.cloned.1.call-update
  21.4 0.2 reduce-scatter.5.cloned.1.call-start
  21.7 0.0 copy-start
  21.7 11.8 %fusion.28 = bf16[1601,1024]{1,0:T(8,128)(2,1)} fusion(bf16[1,1601,2048]{2,1,0:T(8,128)(2,1)} %param.6, bf16[2048,256]{1,0:T(8,128)(2,1)S(1)} %get-tuple-element.11, bf16[2048,256]{1,0:T(8,128)(2,1)} %get-tuple-element.12, bf16[2048,256]{1,0:T(8,128)(2,1)S(1)} %get-tuple-element.6, bf16[2048,256]{1,0:T(8,128)(2,1)S(1)} %get-tuple-element.5), kind=kOutput, calls=%fused_computation.26 | convolution fusion | flops 6733497344 | bytes 14030848 | tf_op jit(solution)/shard_map/dot_general | solution.py:99
  33.5 0.0 reduce-scatter.5.cloned.1.call-update
  33.5 0.0 copy-done
  33.5 1.1 reduce-window.6
  34.7 0.2 slice_reduce_fusion
  34.9 0.1 fusion.40
  35.0 0.0 copy-start.1
  35.0 7.2 %scatter_custom_fusion = bf16[1024,2048]{1,0:T(8,128)(2,1)} fusion(s32[512]{0:T(512)S(1)} %bitcast.49, bf16[512,2048]{1,0:T(8,128)(2,1)} %param.4, bf16[]{:T(256)} %constant.8.clone.1), kind=kCustom, calls=%fused_computation.28 | custom fusion | bytes 4194816 | tf_op jit(solution)/shard_map/scatter | solution.py:76
  42.3 54.3 %all_to_all.25 = bf16[8,128,2048]{2,1,0:T(8,128)(2,1)S(1)} all-to-all(bf16[8,128,2048]{2,1,0:T(8,128)(2,1)} %bitcast.38), channel_id=1, replica_groups=mesh['seq'=8,'tensor'=4] {'seq'}, dimensions={0} | all-to-all | bytes 8388608 | tf_op jit(solution)/shard_map/all_to_all | solution.py:84
  96.5 0.0 copy-done.1
  96.5 3.1 %multiply_convert_fusion = bf16[8,128,2048]{2,1,0:T(8,128)(2,1)} fusion(bf16[8,128,2048]{2,1,0:T(8,128)(2,1)S(1)} %all_to_all.25), kind=kLoop, calls=%fused_computation.5 | loop fusion | flops 6291456 | bytes 8388608 | tf_op jit(solution)/shard_map/convert_element_type | solution.py:86
  99.6 0.0 reduce-scatter.3.cloned.1.call-done.k_ref.v_ref
  99.6 14.2 %shard_map.47 = bf16[1024,512]{1,0:T(8,128)(2,1)} custom-call(bf16[1024,2048]{1,0:T(8,128)(2,1)} %bitcast.39, bf16[1601,256]{1,0:T(8,128)(2,1)} %reduce-scatter.3.cloned.1.call-done.k_ref.v_ref, bf16[1601,256]{1,0:T(8,128)(2,1)} %reduce-scatter.3.cloned.1.call-done.k_ref.v_ref), custom_call_target="tpu_custom_call" | custom-call | flops 3357540352 | bytes 2916864 | tf_op jit(solution)/shard_map/pallas_call | solution.py:39
  113.9 4.2 %all-to-all-start.2 = ((bf16[8,128,512]{2,1,0:T(8,128)(2,1)}), bf16[8,128,512]{2,1,0:T(8,128)(2,1)}, u32[]{:S(2)}, u32[]{:S(2)}) async-start(bf16[8,128,512]{2,1,0:T(8,128)(2,1)} %bitcast.46), calls=%async_computation.3 | async-start | bytes 2097152 | tf_op jit(solution)/shard_map/all_to_all | solution.py:112
  118.1 14.3 %shard_map.46 = bf16[1024,512]{1,0:T(8,128)(2,1)} custom-call(bf16[1024,2048]{1,0:T(8,128)(2,1)} %bitcast.40, bf16[1601,256]{1,0:T(8,128)(2,1)} %reduce-scatter.3.cloned.1.call-done.k_ref.v_ref, bf16[1601,256]{1,0:T(8,128)(2,1)} %reduce-scatter.3.cloned.1.call-done.k_ref.v_ref), custom_call_target="tpu_custom_call" | custom-call | flops 3357540352 | bytes 2916864 | tf_op jit(solution)/shard_map/pallas_call | solution.py:39
  132.4 1.1 all-to-all-done.2
  133.5 4.3 %all-to-all-start.1 = ((bf16[8,128,512]{2,1,0:T(8,128)(2,1)}), bf16[8,128,512]{2,1,0:T(8,128)(2,1)}, u32[]{:S(2)}, u32[]{:S(2)}) async-start(bf16[8,128,512]{2,1,0:T(8,128)(2,1)} %bitcast.44), calls=%async_computation.2 | async-start | bytes 2097152 | tf_op jit(solution)/shard_map/all_to_all | solution.py:112
  137.8 14.6 %reduce-scatter.5.cloned.1.call-done.k_ref.v_ref = bf16[1601,256]{1,0:T(8,128)(2,1)} async-done(((bf16[1601,1024]{1,0:T(8,128)(2,1)}), bf16[1601,256]{1,0:T(8,128)(2,1)}) %reduce-scatter.5.cloned.1.call-update) | async-done | bytes 819728 | tf_op jit(solution)/shard_map/reduce_scatter | solution.py:98
  152.4 14.3 %shard_map.48 = bf16[1024,512]{1,0:T(8,128)(2,1)} custom-call(bf16[1024,2048]{1,0:T(8,128)(2,1)} %bitcast.41, bf16[1601,256]{1,0:T(8,128)(2,1)} %reduce-scatter.5.cloned.1.call-done.k_ref.v_ref, bf16[1601,256]{1,0:T(8,128)(2,1)} %reduce-scatter.5.cloned.1.call-done.k_ref.v_ref), custom_call_target="tpu_custom_call" | custom-call | flops 3357540352 | bytes 2916864 | tf_op jit(solution)/shard_map/pallas_call | solution.py:39
  166.7 0.0 all-to-all-done.1
  166.7 4.5 %all-to-all-start.3 = ((bf16[8,128,512]{2,1,0:T(8,128)(2,1)}), bf16[8,128,512]{2,1,0:T(8,128)(2,1)}, u32[]{:S(2)}, u32[]{:S(2)}) async-start(bf16[8,128,512]{2,1,0:T(8,128)(2,1)} %bitcast.45), calls=%async_computation.5 | async-start | bytes 2097152 | tf_op jit(solution)/shard_map/all_to_all | solution.py:112
  171.2 14.3 %shard_map.49 = bf16[1024,512]{1,0:T(8,128)(2,1)} custom-call(bf16[1024,2048]{1,0:T(8,128)(2,1)} %bitcast.42, bf16[1601,256]{1,0:T(8,128)(2,1)} %reduce-scatter.5.cloned.1.call-done.k_ref.v_ref, bf16[1601,256]{1,0:T(8,128)(2,1)} %reduce-scatter.5.cloned.1.call-done.k_ref.v_ref), custom_call_target="tpu_custom_call" | custom-call | flops 3357540352 | bytes 2916864 | tf_op jit(solution)/shard_map/pallas_call | solution.py:39
  185.4 0.9 all-to-all-done.3
  186.3 3.6 %all-to-all-start.4 = ((bf16[8,128,512]{2,1,0:T(8,128)(2,1)}), bf16[8,128,512]{2,1,0:T(8,128)(2,1)S(1)}, u32[]{:S(2)}, u32[]{:S(2)}) async-start(bf16[8,128,512]{2,1,0:T(8,128)(2,1)} %bitcast.43), calls=%async_computation.6 | async-start | bytes 2097152 | tf_op jit(solution)/shard_map/all_to_all | solution.py:112
  189.9 0.6 pad_clamp_fusion
  190.5 3.3 %gather_fusion.1 = bf16[512,512]{1,0:T(8,128)(2,1)S(1)} fusion(bf16[1024,512]{1,0:T(8,128)(2,1)} %bitcast.13, s32[1024]{0:T(1024)S(1)} %pad_clamp_fusion), kind=kCustom, calls=%fused_computation.1 | custom fusion | bytes 1050624 | tf_op jit(solution)/shard_map/gather | solution.py:113
  193.8 3.3 %gather_fusion = bf16[512,512]{1,0:T(8,128)(2,1)S(1)} fusion(bf16[1024,512]{1,0:T(8,128)(2,1)} %bitcast.11, s32[1024]{0:T(1024)S(1)} %pad_clamp_fusion), kind=kCustom, calls=%fused_computation | custom fusion | bytes 1050624 | tf_op jit(solution)/shard_map/gather | solution.py:113
  197.2 1.6 dynamic_update_slice.12
  198.8 3.3 %gather_fusion.2 = bf16[512,512]{1,0:T(8,128)(2,1)S(1)} fusion(bf16[1024,512]{1,0:T(8,128)(2,1)} %bitcast.16, s32[1024]{0:T(1024)S(1)} %pad_clamp_fusion), kind=kCustom, calls=%fused_computation.2 | custom fusion | bytes 1050624 | tf_op jit(solution)/shard_map/gather | solution.py:113
  202.1 3.1 %all-to-all-done.4 = bf16[8,128,512]{2,1,0:T(8,128)(2,1)S(1)} async-done(((bf16[8,128,512]{2,1,0:T(8,128)(2,1)}), bf16[8,128,512]{2,1,0:T(8,128)(2,1)S(1)}, u32[]{:S(2)}, u32[]{:S(2)}) %all-to-all-start.4) | async-done | bytes 1048608 | tf_op jit(solution)/shard_map/all_to_all | solution.py:112
  205.2 2.0 gather_fusion.3
  207.1 0.8 constant_dynamic-update-slice_fusion.2
  208.0 0.8 constant_dynamic-update-slice_fusion.1
  208.8 0.8 constant_dynamic-update-slice_fusion
  (4 shorter events, 0.1 us)
Async XLA Ops:
  6.5 93.1 %reduce-scatter.3.cloned.1.call-start = ((), (), s32[]{:S(2)}) async-start(), calls=%async_computation.7 | async-start | bytes 4116480 | tf_op jit(solution)/shard_map/reduce_scatter | solution.py:98
  6.5 5.9 %copy-start.2 = (bf16[1,1601,2048]{2,1,0:T(8,128)(2,1)S(1)}, bf16[1,1601,2048]{2,1,0:T(8,128)(2,1)}, u32[]{:S(2)}) copy-start(bf16[1,1601,2048]{2,1,0:T(8,128)(2,1)} %param.6) | copy-start | bytes 19673092
  21.4 131.0 %reduce-scatter.5.cloned.1.call-start = ((), (), s32[]{:S(2)}) async-start(), calls=%async_computation.8 | async-start | bytes 4116480 | tf_op jit(solution)/shard_map/reduce_scatter | solution.py:98
  21.7 11.8 %copy-start = (s32[512,1]{0,1:T(1,128)S(1)}, s32[512,1]{0,1:T(1,128)}, u32[]{:S(2)}) copy-start(s32[512,1]{0,1:T(1,128)} %param.5) | copy-start | bytes 6148
  35.0 61.5 %copy-start.1 = (s32[512,1]{0,1:T(1,128)}, s32[512,1]{0,1:T(1,128)S(1)}, u32[]{:S(2)}) copy-start(s32[512,1]{0,1:T(1,128)S(1)} %compare_select_fusion) | copy-start | bytes 6148
  113.9 19.6 %all-to-all-start.2 = ((bf16[8,128,512]{2,1,0:T(8,128)(2,1)}), bf16[8,128,512]{2,1,0:T(8,128)(2,1)}, u32[]{:S(2)}, u32[]{:S(2)}) async-start(bf16[8,128,512]{2,1,0:T(8,128)(2,1)} %bitcast.46), calls=%async_computation.3 | async-start | bytes 2097152 | tf_op jit(solution)/shard_map/all_to_all | solution.py:112
  133.5 33.2 %all-to-all-start.1 = ((bf16[8,128,512]{2,1,0:T(8,128)(2,1)}), bf16[8,128,512]{2,1,0:T(8,128)(2,1)}, u32[]{:S(2)}, u32[]{:S(2)}) async-start(bf16[8,128,512]{2,1,0:T(8,128)(2,1)} %bitcast.44), calls=%async_computation.2 | async-start | bytes 2097152 | tf_op jit(solution)/shard_map/all_to_all | solution.py:112
  166.7 19.6 %all-to-all-start.3 = ((bf16[8,128,512]{2,1,0:T(8,128)(2,1)}), bf16[8,128,512]{2,1,0:T(8,128)(2,1)}, u32[]{:S(2)}, u32[]{:S(2)}) async-start(bf16[8,128,512]{2,1,0:T(8,128)(2,1)} %bitcast.45), calls=%async_computation.5 | async-start | bytes 2097152 | tf_op jit(solution)/shard_map/all_to_all | solution.py:112
  186.3 18.9 %all-to-all-start.4 = ((bf16[8,128,512]{2,1,0:T(8,128)(2,1)}), bf16[8,128,512]{2,1,0:T(8,128)(2,1)S(1)}, u32[]{:S(2)}, u32[]{:S(2)}) async-start(bf16[8,128,512]{2,1,0:T(8,128)(2,1)} %bitcast.43), calls=%async_computation.6 | async-start | bytes 2097152 | tf_op jit(solution)/shard_map/all_to_all | solution.py:112
Sparse Core Ops, SparseCore 0:
  21.6 65.5 reduce-scatter.2
  89.5 62.8 reduce-scatter.4
